TPU v7x, 256 devices: a whole 4x4x8 slice. The times are simulated.
256 devices in a mesh: segment: 4 (over x), dp: 64 (over y, z, core).
Axes of the slice: x: 4, y: 4, z: 8, core: 2. Of those that a mesh axis runs over, the one named last changes fastest.
Arguments:
- tokens: bfloat16 [32768, 8192], P('dp', 'segment'), may hold values from -16 to 16
- block_values: bfloat16 [8192, 768], P('segment'), may hold values from -0.09375 to 0.09375
- column_blocks: int32 [128, 12], P('segment'), may hold values from 0 to 15, as said below
- counts: int32 [128], P('segment'), may hold values from 4 to 12, as said below
- cotangent: bfloat16 [32768, 1024], P(('dp', 'segment')), may hold values from -6 to 6
Outputs:
- activation: bfloat16 [32768, 1024], P(('dp', 'segment'))
- input_grad: bfloat16 [32768, 8192], P('dp', 'segment')
- weight_grad: float32 [8192, 768], P(('segment', 'dp'))
Inputs may be any that keep to these rules, and one draw needn't show every extreme that they name: `column_blocks`: the first counts[r] entries of row r are distinct column blocks; entries at later slots are column blocks too and are ignored. `counts`: some row block uses all 12 slots.
All inputs are finite; a program needn't handle non-finite values.
Results may differ from a plain program's by a relative error of at most 0.001.
Values may be sent and summed in bfloat16 or wider, within the bound.
No kernel may reach another device: no remote copies, remote signals or barrier semaphores. Data moves between devices by JAX's collectives and lax.ppermute only.
A program may use at most 128 MiB of HBM per device.

v0:
```python
import jax
import jax.numpy as jnp
from jax import lax
from jax.sharding import PartitionSpec as P


def block_onehot(column_blocks, counts, col_blocks):
    slots = column_blocks.shape[1]
    named = column_blocks[:, :, None] == jnp.arange(col_blocks, dtype=jnp.int32)[None, None, :]
    alive = jnp.arange(slots, dtype=jnp.int32)[None, :, None] < counts[:, None, None]
    return named & alive


def select_slots(dense_rows, first_row, column_blocks, counts, block, col_blocks):
    row_count = dense_rows.shape[0]
    slots = column_blocks.shape[1]
    row_block = (first_row + jnp.arange(row_count, dtype=jnp.int32)) // block
    block_ids = jnp.take(column_blocks, row_block, axis=0)
    live_count = jnp.take(counts, row_block, axis=0)
    onehot = block_onehot(block_ids, live_count, col_blocks).astype(jnp.float32)
    picked = jnp.einsum(
        "rkc,rcj->rkj",
        onehot,
        dense_rows.reshape(row_count, col_blocks, block),
        precision=lax.Precision.HIGHEST,
    )
    return picked.reshape(row_count, slots * block)


def per_device(tokens, block_values, column_blocks, counts, cotangent):
    local_rows, features = tokens.shape
    width = cotangent.shape[1]
    row_blocks, slots = column_blocks.shape
    block = features // row_blocks
    col_blocks = width // block
    sections = lax.axis_size("segment")
    replicas = lax.axis_size("dp")
    onehot = block_onehot(column_blocks, counts, col_blocks).astype(jnp.bfloat16)
    blocks_view = block_values.reshape(row_blocks, block, slots, block)
    weight = (
        jnp.einsum("bkc,bikj->bicj", onehot, blocks_view, preferred_element_type=jnp.float32)
        .astype(jnp.bfloat16)
        .reshape(features, width)
    )
    share_rows = local_rows // sections
    own_start = lax.axis_index("segment") * share_rows
    partial_value = jnp.dot(tokens, weight, preferred_element_type=jnp.float32)
    preact_all = lax.psum(partial_value, "segment")
    cotangent_all = lax.all_gather(cotangent, "segment", axis=0, tiled=True)
    activation = lax.dynamic_slice_in_dim(preact_all, own_start, share_rows, 0).astype(jnp.bfloat16)
    owned_rows = features // replicas
    product = lax.dot_general(
        tokens, cotangent_all, (((0,), (0,)), ((), ())), preferred_element_type=jnp.float32
    )
    summed = lax.psum_scatter(product / replicas, "dp", scatter_dimension=0, tiled=True)
    weight_grad = select_slots(
        summed, lax.axis_index("dp") * owned_rows, column_blocks, counts, block, col_blocks
    )
    input_grad = lax.dot_general(
        cotangent_all, weight, (((1,), (1,)), ((), ())), preferred_element_type=jnp.float32
    ).astype(jnp.bfloat16)
    return (activation, input_grad, weight_grad)


def solution(mesh):
    in_specs = (
        P("dp", "segment"),
        P("segment", None),
        P("segment", None),
        P("segment"),
        P(("dp", "segment"), None),
    )
    out_specs = (P(("dp", "segment"), None), P("dp", "segment"), P(("segment", "dp"), None))
    return jax.shard_map(
        per_device, mesh=mesh, in_specs=in_specs, out_specs=out_specs, check_vma=False
    )
```

profile of v0, /device:TPU:2, one launch (start us, length us, event | category | flops | bytes accessed | tf_op | source)
XLA Modules:
  0.0 208.3 jit_solution(9606807791745923992)
XLA Ops:
  7.2 0.0 all-gather.2.cloned.1.call-start
  7.2 0.7 all-gather.2.cloned.1.call-update
  7.9 0.0 reduce-scatter.2.cloned.1.call-start
  8.0 30.3 %all-gather.2.cloned.1.call-done = bf16[512,1024]{1,0:T(8,128)(2,1)} async-done(((bf16[128,1024]{1,0:T(8,128)(2,1)}), bf16[512,1024]{1,0:T(8,128)(2,1)}) %all-gather.2.cloned.1.call-update) | async-done | bytes 1048592 | tf_op jit(solution)/shard_map/all_gather | solution.py:49
  38.3 6.8 %convolution_multiply_fusion = f32[2048,1024]{1,0:T(8,128)} fusion(bf16[512,2048]{1,0:T(8,128)(2,1)S(1)} %copy-done, bf16[512,1024]{1,0:T(8,128)(2,1)} %all-gather.2.cloned.1.call-done), kind=kOutput, calls=%fused_computation.3 | convolution fusion | flops 2149580800 | bytes 11534336 | tf_op jit(solution)/shard_map/dot_general | solution.py:52
  45.1 0.0 reduce-scatter.2.cloned.1.call-update
  45.1 10.6 %reshape.199 = bf16[32,64,12,64]{3,2,1,0:T(8,128)(2,1)} reshape(bf16[2048,768]{1,0:T(8,128)(2,1)} %param.6) | data formatting | bytes 6291456 | tf_op jit(solution)/shard_map/reshape | solution.py:39
  55.7 0.1 copy.12
  55.9 0.6 gather_fusion
  56.4 0.7 gather_fusion.1
  57.1 0.1 iota_compare_fusion.3
  57.2 9.1 %convert_bitcast_fusion = bf16[32,64,16,64]{3,2,1,0:T(8,128)(2,1)} fusion(bf16[32,64,12,64]{3,2,1,0:T(8,128)(2,1)} %reshape.199, s32[32,12]{1,0:T(8,128)S(1)} %copy.12, pred[32,12]{1,0:T(8,128)(4,1)S(1)} %iota_compare_fusion.3), kind=kOutput, calls=%fused_computation.2 | convolution fusion | flops 52441088 | bytes 7341952 | tf_op jit(solution)/shard_map/bkc,bikj->bicj/dot_general | solution.py:41
  66.3 12.0 %reshape.179 = bf16[2048,1024]{1,0:T(8,128)(2,1)} reshape(bf16[32,64,16,64]{3,2,1,0:T(8,128)(2,1)} %convert_bitcast_fusion) | data formatting | bytes 8388608 | tf_op jit(solution)/shard_map/reshape | solution.py:43
  78.3 6.0 %convolution_bitcast_fusion = f32[512,1024]{0,1:T(8,128)} fusion(bf16[2048,1024]{1,0:T(8,128)(2,1)} %reshape.179, bf16[512,2048]{1,0:T(8,128)(2,1)S(1)} %copy-done), kind=kOutput, calls=%fused_computation.6 | convolution fusion | flops 2147483648 | bytes 8388608 | tf_op jit(solution)/shard_map/dot_general | solution.py:47
  84.3 41.4 %all-reduce.1 = bf16[512,1024]{0,1:T(8,128)(2,1)S(1)} all-reduce(f32[512,1024]{0,1:T(8,128)} %convolution_bitcast_fusion), channel_id=1, replica_groups=mesh['segment'=4,'dp'=64] {'segment'}, use_global_device_ids=true, to_apply=%region_0.0 | all-reduce | flops 524288 | bytes 3145728 | tf_op jit(solution)/shard_map/psum | solution.py:48
  125.8 0.9 copy.16
  126.7 0.1 iota_compare_fusion.2
  126.8 0.1 broadcast_select_fusion
  126.9 6.2 %fusion = bf16[512,2048]{0,1:T(8,128)(2,1)} fusion(bf16[2048,1024]{1,0:T(8,128)(2,1)} %reshape.179, bf16[512,1024]{1,0:T(8,128)(2,1)} %all-gather.2.cloned.1.call-done), kind=kOutput, calls=%fused_computation.5 | convolution fusion | flops 2148532224 | bytes 7340032 | tf_op jit(solution)/shard_map/dot_general | solution.py:59
  133.1 3.9 %copy.17 = bf16[512,2048]{1,0:T(8,128)(2,1)} copy(bf16[512,2048]{0,1:T(8,128)(2,1)} %fusion) | data formatting | bytes 4194304
  137.0 62.2 %reduce-scatter.2.cloned.1.call-done = f32[32,1024]{1,0:T(8,128)} async-done(((f32[2048,1024]{1,0:T(8,128)}), f32[32,1024]{1,0:T(8,128)}) %reduce-scatter.2.cloned.1.call-update) | async-done | bytes 131088 | tf_op jit(solution)/shard_map/reduce_scatter | solution.py:55
  199.3 1.0 reshape.180
  200.3 0.4 fusion.5
  200.7 0.7 reshape.181
  (11 shorter events, 0.1 us)
Async XLA Ops:
  7.2 31.1 %copy-start = (bf16[512,2048]{1,0:T(8,128)(2,1)S(1)}, bf16[512,2048]{1,0:T(8,128)(2,1)}, u32[]{:S(2)}) copy-start(bf16[512,2048]{1,0:T(8,128)(2,1)} %param.5) | copy-start | bytes 6291460
  7.2 31.1 %all-gather.2.cloned.1.call-start = ((), (), s32[]{:S(2)}) async-start(), calls=%async_computation.1 | async-start | bytes 1310720 | tf_op jit(solution)/shard_map/all_gather | solution.py:49
  7.9 191.3 %reduce-scatter.2.cloned.1.call-start = ((), (), s32[]{:S(2)}) async-start(), calls=%async_computation.2 | async-start | bytes 8519680 | tf_op jit(solution)/shard_map/reduce_scatter | solution.py:55
  45.1 10.6 %copy-start.2 = (s32[32,12]{0,1:T(8,128)S(1)}, s32[32,12]{0,1:T(8,128)}, u32[]{:S(2)}) copy-start(s32[32,12]{0,1:T(8,128)} %param.7) | copy-start | bytes 4612
  45.1 11.3 %copy-start.1 = (s32[32]{0:T(128)S(1)}, s32[32]{0:T(128)}, u32[]{:S(2)}) copy-start(s32[32]{0:T(128)} %param.8) | copy-start | bytes 388
Sparse Core Ops, SparseCore 0:
  9.8 28.4 all-gather.1
  45.2 153.9 reduce-scatter.1
where the time goes:
time: 209 us; the launch traced here: 208 us
  waiting for transfers between devices  93.2 us (45%)
  blocking collectives  41.4 us (20%)
  local copies, waits for them, and re-layouts  30.6 us (15%)
  matrix products  28.6 us (14%)
  between operations  14.1 us (7%)
    reduce_scatter x1, waiting for transfers between devices, per_device(): lax.psum_scatter(product / replicas, 'dp', scatter_dimension=0, tiled=True)  62.2 us
    psum x1, blocking collectives, per_device(): preact_all = lax.psum(partial_value, 'segment')  41.4 us
    all_gather x1, waiting for transfers between devices, per_device(): cotangent_all = lax.all_gather(cotangent, 'segment', axis=0, tiled=True)  30.3 us
    reshape x1, local copies, waits for them, and re-layouts, per_device(): weight = jnp.einsum('bkc,bikj->bicj', onehot, blocks_view, preferred_elem...  12 us
    reshape x1, local copies, waits for them, and re-layouts, per_device(): blocks_view = block_values.reshape(row_blocks, block, slots, block)  10.6 us
    dot_general x1, matrix products, per_device(): jnp.einsum('bkc,bikj->bicj', onehot, blocks_view, preferred_element_type=...  9.11 us
    dot_general x1, matrix products, per_device(): lax.dot_general(tokens, cotangent_all, (((0,), (0,)), ((), ())), preferre...  6.82 us
    dot_general x1, matrix products, per_device(): lax.dot_general(cotangent_all, weight, (((1,), (1,)), ((), ())), preferre...  6.23 us
  transfers between devices with their start and end apart: 2, of which 2 were waited for; matrix products, arithmetic and copies ran while one was open for 24% of the time, Pallas kernels for 0%

commit v1 on v0

v1 whole, which is shorter than its diff:
```python
import jax
import jax.numpy as jnp
from jax import lax
from jax.sharding import Mesh
from jax.sharding import PartitionSpec as P

DP_AXES = ("y", "z", "core")


def block_onehot(column_blocks, counts, col_blocks):
    slots = column_blocks.shape[1]
    named = column_blocks[:, :, None] == jnp.arange(col_blocks, dtype=jnp.int32)[None, None, :]
    alive = jnp.arange(slots, dtype=jnp.int32)[None, :, None] < counts[:, None, None]
    return named & alive


def slot_grad(tokens, cotangent_all, column_blocks, counts, block, replicas):
    local_rows, features = tokens.shape
    width = cotangent_all.shape[1]
    row_blocks, slots = column_blocks.shape
    col_blocks = width // block
    cot_rows = cotangent_all.T.reshape(col_blocks, block, local_rows)
    picked = jnp.take(cot_rows, column_blocks, axis=0, mode="clip")
    picked = picked.reshape(row_blocks, slots * block, local_rows)
    tok_rows = tokens.reshape(local_rows, row_blocks, block).transpose(1, 2, 0)
    grad = lax.dot_general(
        tok_rows, picked, (((2,), (2,)), ((0,), (0,))), preferred_element_type=jnp.float32
    )
    live = jnp.arange(slots, dtype=jnp.int32)[None, :] < counts[:, None]
    live = jnp.repeat(live, block, axis=1)[:, None, :]
    return jnp.where(live, grad / replicas, 0.0)


def per_device(tokens, block_values, column_blocks, counts, cotangent):
    local_rows, features = tokens.shape
    width = cotangent.shape[1]
    row_blocks, slots = column_blocks.shape
    block = features // row_blocks
    col_blocks = width // block
    sections = lax.axis_size("x")
    replicas = lax.axis_size(DP_AXES)
    n_y, n_z, n_core = (lax.axis_size(a) for a in DP_AXES)
    onehot = block_onehot(column_blocks, counts, col_blocks).astype(jnp.bfloat16)
    blocks_view = block_values.reshape(row_blocks, block, slots, block)
    weight = (
        jnp.einsum("bkc,bikj->bicj", onehot, blocks_view, preferred_element_type=jnp.float32)
        .astype(jnp.bfloat16)
        .reshape(features, width)
    )
    share_rows = local_rows // sections
    own_start = lax.axis_index("x") * share_rows
    partial_value = jnp.dot(tokens, weight, preferred_element_type=jnp.float32)
    preact_all = lax.psum(partial_value, "x")
    cotangent_all = lax.all_gather(cotangent, "x", axis=0, tiled=True)
    activation = lax.dynamic_slice_in_dim(preact_all, own_start, share_rows, 0).astype(jnp.bfloat16)
    picked = slot_grad(tokens, cotangent_all, column_blocks, counts, block, replicas)
    owned = features // replicas
    staged = (
        picked.reshape(n_y, n_z, n_core, owned, slots * block)
        .transpose(2, 1, 0, 3, 4)
        .reshape(features, slots * block)
    )
    staged = lax.psum_scatter(staged, "core", scatter_dimension=0, tiled=True)
    staged = lax.psum_scatter(staged, "z", scatter_dimension=0, tiled=True)
    weight_grad = lax.psum_scatter(staged, "y", scatter_dimension=0, tiled=True)
    input_grad = lax.dot_general(
        cotangent_all, weight, (((1,), (1,)), ((), ())), preferred_element_type=jnp.float32
    ).astype(jnp.bfloat16)
    return (activation, input_grad, weight_grad)


def solution(mesh):
    sections, replicas = mesh.devices.shape
    n_core = 2
    n_y = 4
    n_z = replicas // (n_y * n_core)
    fine = Mesh(mesh.devices.reshape(sections, n_y, n_z, n_core), ("x",) + DP_AXES)
    in_specs = (
        P(DP_AXES, "x"),
        P("x", None),
        P("x", None),
        P("x"),
        P(DP_AXES + ("x",), None),
    )
    out_specs = (P(DP_AXES + ("x",), None), P(DP_AXES, "x"), P(("x",) + DP_AXES, None))
    return jax.shard_map(
        per_device, mesh=fine, in_specs=in_specs, out_specs=out_specs, check_vma=False
    )
```

time: 209 us -> 205 us (0.981)
  waiting for transfers between devices: 93.2 us -> 66.4 us
  local copies, waits for them, and re-layouts: 30.6 us -> 49.3 us
  matrix products: 28.6 us -> 32.8 us
    reduce_scatter x1 -> x3, waiting for transfers between devices: 62.2 us -> 39.5 us  [the longest x1 21.9 us: per_device(): staged = lax.psum_scatter(staged, 'core', scatter_dimension=0, tiled=True)]
    gather x2 -> x1, local copies, waits for them, and re-layouts: 1.27 us -> 14.1 us  [slot_grad(): picked = jnp.take(cot_rows, column_blocks, axis=0, mode='clip')]
    dot_general x2 -> x1, matrix products: 7.23 us -> 14.1 us  [slot_grad(): lax.dot_general(tok_rows, picked, (((2,), (2,)), ((0,), (0,))), preferred...]
    transpose x0 -> x1, local copies, waits for them, and re-layouts: none -> 6.17 us  [per_device(): staged = picked.reshape(n_y, n_z, n_core, owned, slots * block).transpose...]
    unnamed x9, local copies, waits for them, and re-layouts: 4.89 us -> 8.68 us
    all_gather x1, waiting for transfers between devices: 30.3 us -> 26.8 us  [per_device(): cotangent_all = lax.all_gather(cotangent, 'x', axis=0, tiled=True)]
    reshape x1, local copies, waits for them, and re-layouts: 10.6 us -> 7.14 us  [per_device(): blocks_view = block_values.reshape(row_blocks, block, slots, block)]
  transfers between devices with their start and end apart: 2 -> 4, of which waited for: 2 -> 3; matrix products, arithmetic and copies ran while one was open for 24% -> 23% of each run, Pallas kernels for 0% -> 0%
where the time goes in v1:
time: 205 us; the launch traced here: 204 us
  waiting for transfers between devices  66.4 us (32%)
  local copies, waits for them, and re-layouts  49.3 us (24%)
  blocking collectives  40.4 us (20%)
  matrix products  32.8 us (16%)
  between operations  13.8 us (7%)
    psum x1, blocking collectives, per_device(): preact_all = lax.psum(partial_value, 'x')  40.4 us
    all_gather x1, waiting for transfers between devices, per_device(): cotangent_all = lax.all_gather(cotangent, 'x', axis=0, tiled=True)  26.8 us
    reduce_scatter x1, waiting for transfers between devices, per_device(): staged = lax.psum_scatter(staged, 'core', scatter_dimension=0, tiled=True)  21.9 us
    reduce_scatter x1, waiting for transfers between devices, per_device(): staged = lax.psum_scatter(staged, 'z', scatter_dimension=0, tiled=True)  17.6 us
    dot_general x1, matrix products, slot_grad(): lax.dot_general(tok_rows, picked, (((2,), (2,)), ((0,), (0,))), preferred...  14.1 us
    gather x1, local copies, waits for them, and re-layouts, slot_grad(): picked = jnp.take(cot_rows, column_blocks, axis=0, mode='clip')  14.1 us
    reshape x1, local copies, waits for them, and re-layouts, per_device(): weight = jnp.einsum('bkc,bikj->bicj', onehot, blocks_view, preferred_elem...  11.9 us
    dot_general x1, matrix products, per_device(): jnp.einsum('bkc,bikj->bicj', onehot, blocks_view, preferred_element_type=...  8.92 us
  transfers between devices with their start and end apart: 4, of which 3 were waited for; matrix products, arithmetic and copies ran while one was open for 23% of the time, Pallas kernels for 0%

profile of v1, /device:TPU:2, one launch (start us, length us, event | category | flops | bytes accessed | tf_op | source)
XLA Modules:
  0.0 203.6 jit_solution(3340737239426838955)
XLA Ops:
  7.2 1.8 copy.17
  9.0 0.0 reduce-scatter.4.cloned.1.call-start
  9.1 0.8 copy.14
  9.9 0.1 reshape.64
  10.0 0.7 iota_compare_fusion.1
  10.7 0.1 broadcast_in_dim.27
  10.8 0.1 broadcast_in_dim.28
  11.0 2.9 %copy.19 = bf16[512,2048]{0,1:T(8,128)(2,1)S(1)} copy(bf16[512,2048]{1,0:T(8,128)(2,1)} %param.5) | data formatting | bytes 4194304 | tf_op args[0]
  13.9 26.8 %all-gather.2.cloned.1.call-done = bf16[512,1024]{0,1:T(8,128)(2,1)} async-done(((bf16[128,1024]{0,1:T(8,128)(2,1)}), bf16[512,1024]{0,1:T(8,128)(2,1)}) %all-gather.2.cloned.1.call-update) | async-done | bytes 1048592 | tf_op jit(solution)/shard_map/all_gather | solution.py:54
  40.6 14.1 %gather_fusion = bf16[384,64,512]{2,1,0:T(8,128)(2,1)} fusion(bf16[16,64,512]{2,1,0:T(8,128)(2,1)} %bitcast.33, s32[1024]{0:T(1024)S(1)} %pad_clamp_fusion), kind=kCustom, calls=%fused_computation | custom fusion | bytes 50333184 | tf_op jit(solution)/shard_map/jit(_take)/gather | solution.py:23
  54.7 14.1 %multiply_select_fusion = f32[32,768,64]{1,2,0:T(8,128)} fusion(pred[32,768]{1,0:T(8,128)(4,1)S(1)} %broadcast_in_dim.28, bf16[32,768,512]{2,1,0:T(8,128)(2,1)} %bitcast.34, bf16[32,64,512]{2,1,0:T(8,128)(2,1)S(1)} %bitcast.37), kind=kOutput, calls=%fused_computation.2 | convolution fusion | flops 1613758464 | bytes 33579008 | tf_op jit(solution)/shard_map/dot_general | solution.py:26
  68.8 6.2 %copy.20 = f32[2,8,4,32,768]{4,3,2,1,0:T(8,128)} copy(f32[2,8,4,32,768]{4,3,0,1,2:T(8,128)} %bitcast.36) | data formatting | bytes 12582912 | tf_op jit(solution)/shard_map/transpose | solution.py:60
  75.0 0.0 reduce-scatter.6.cloned.1.call-start
  75.0 21.9 %reduce-scatter.4.cloned.1.call-done = f32[1024,768]{1,0:T(8,128)} async-done(((f32[2048,768]{1,0:T(8,128)}), f32[1024,768]{1,0:T(8,128)}) %reduce-scatter.4.cloned.1.call-update) | async-done | bytes 3145744 | tf_op jit(solution)/shard_map/reduce_scatter | solution.py:63
  97.1 7.1 %reshape.74 = bf16[32,64,12,64]{3,2,1,0:T(8,128)(2,1)} reshape(bf16[2048,768]{1,0:T(8,128)(2,1)S(1)} %copy-done.1) | data formatting | bytes 6291456 | tf_op jit(solution)/shard_map/reshape | solution.py:44
  104.2 8.9 %convert_bitcast_fusion = bf16[32,64,16,64]{3,2,1,0:T(8,128)(2,1)} fusion(bf16[32,64,12,64]{3,2,1,0:T(8,128)(2,1)} %reshape.74, s32[32,12]{1,0:T(8,128)S(1)} %copy.14, pred[32,12]{1,0:T(8,128)(4,1)S(1)} %iota_compare_fusion.1), kind=kOutput, calls=%fused_computation.1 | convolution fusion | flops 52441088 | bytes 7341952 | tf_op jit(solution)/shard_map/bkc,bikj->bicj/dot_general | solution.py:46
  113.1 11.9 %reshape.56 = bf16[2048,1024]{1,0:T(8,128)(2,1)} reshape(bf16[32,64,16,64]{3,2,1,0:T(8,128)(2,1)} %convert_bitcast_fusion) | data formatting | bytes 8388608 | tf_op jit(solution)/shard_map/reshape | solution.py:48
  125.1 5.3 %convolution_bitcast_fusion = f32[512,1024]{0,1:T(8,128)S(1)} fusion(bf16[2048,1024]{1,0:T(8,128)(2,1)} %reshape.56, bf16[512,2048]{1,0:T(8,128)(2,1)} %param.5), kind=kOutput, calls=%fused_computation.5 | convolution fusion | flops 2147483648 | bytes 8388608 | tf_op jit(solution)/shard_map/dot_general | solution.py:52
  130.4 17.6 %reduce-scatter.6.cloned.1.call-done = f32[128,768]{1,0:T(8,128)} async-done(((f32[1024,768]{1,0:T(8,128)}), f32[128,768]{1,0:T(8,128)}) %reduce-scatter.6.cloned.1.call-update) | async-done | bytes 393232 | tf_op jit(solution)/shard_map/reduce_scatter | solution.py:64
  148.0 40.4 %all-reduce.1 = bf16[512,1024]{0,1:T(8,128)(2,1)} all-reduce(f32[512,1024]{0,1:T(8,128)S(1)} %convolution_bitcast_fusion), channel_id=1, replica_groups=mesh['x'=4,'y'=4,'z'=8,'core'=2] {'x'}, use_global_device_ids=true, to_apply=%region_0.0 | all-reduce | flops 524288 | bytes 3145728 | tf_op jit(solution)/shard_map/psum | solution.py:53
  188.4 1.0 dynamic-slice_convert_fusion
  189.3 0.9 copy.21
  190.2 4.5 %fusion = bf16[512,2048]{0,1:T(8,128)(2,1)S(1)} fusion(bf16[2048,1024]{1,0:T(8,128)(2,1)} %reshape.56, bf16[512,1024]{0,1:T(8,128)(2,1)S(1)} %copy-done), kind=kOutput, calls=%fused_computation.4 | convolution fusion | flops 2148532224 | bytes 7340032 | tf_op jit(solution)/shard_map/dot_general | solution.py:66
  194.7 2.4 %copy.22 = bf16[512,2048]{1,0:T(8,128)(2,1)} copy(bf16[512,2048]{0,1:T(8,128)(2,1)S(1)} %fusion) | data formatting | bytes 4194304
  (12 shorter events, 0.2 us)
Async XLA Ops:
  7.2 33.5 %all-gather.2.cloned.1.call-start = ((), (), s32[]{:S(2)}) async-start(), calls=%async_computation.3 | async-start | bytes 1310720 | tf_op jit(solution)/shard_map/all_gather | solution.py:54
  9.0 88.0 %reduce-scatter.4.cloned.1.call-start = ((), (), s32[]{:S(2)}) async-start(), calls=%async_computation.4 | async-start | bytes 9437184 | tf_op jit(solution)/shard_map/reduce_scatter | solution.py:63
  75.0 22.1 %copy-start.1 = (bf16[2048,768]{1,0:T(8,128)(2,1)S(1)}, bf16[2048,768]{1,0:T(8,128)(2,1)}, u32[]{:S(2)}) copy-start(bf16[2048,768]{1,0:T(8,128)(2,1)} %param.6) | copy-start | bytes 9437188
  75.0 73.0 %reduce-scatter.6.cloned.1.call-start = ((), (), s32[]{:S(2)}) async-start(), calls=%async_computation.5 | async-start | bytes 3538944 | tf_op jit(solution)/shard_map/reduce_scatter | solution.py:64
  97.0 100.1 %reduce-scatter.8.cloned.1.call-start = ((), (), s32[]{:S(2)}) async-start(), calls=%async_computation.6 | async-start | bytes 491520 | tf_op jit(solution)/shard_map/reduce_scatter | solution.py:65
  130.4 59.8 %copy-start = (bf16[512,1024]{0,1:T(8,128)(2,1)S(1)}, bf16[512,1024]{0,1:T(8,128)(2,1)}, u32[]{:S(2)}) copy-start(bf16[512,1024]{0,1:T(8,128)(2,1)} %all-gather.2.cloned.1.call-done) | copy-start | bytes 3145732
Sparse Core Ops, SparseCore 0:
  10.3 30.2 all-gather.1
  75.1 21.8 reduce-scatter.3
  99.5 48.3 reduce-scatter.5
  150.9 23.1 reduce-scatter.7

commit v2 on v1

--- a/solution.py
+++ b/solution.py
@@ -31,6 +31,30 @@
     return jnp.where(live, grad / replicas, 0.0)
 
 
+def ring_scatter(value, axis):
+    n = lax.axis_size(axis)
+    if n == 1:
+        return value
+    idx = lax.axis_index(axis)
+    rows = value.shape[0] // n
+    chunks = value.reshape(n, rows, value.shape[1])
+
+    def take(j):
+        return lax.dynamic_index_in_dim(chunks, j % n, 0, keepdims=False)
+
+    if n == 2:
+        return take(idx) + lax.ppermute(take(idx + 1), axis, [(0, 1), (1, 0)])
+    half = value.shape[1] // 2
+    fwd = [(i, (i + 1) % n) for i in range(n)]
+    bwd = [(i, (i - 1) % n) for i in range(n)]
+    a = take(idx - 1)[:, :half]
+    b = take(idx + 1)[:, half:]
+    for s in range(n - 1):
+        a = lax.ppermute(a, axis, fwd) + take(idx - s - 2)[:, :half]
+        b = lax.ppermute(b, axis, bwd) + take(idx + s + 2)[:, half:]
+    return jnp.concatenate([a, b], axis=1)
+
+
 def per_device(tokens, block_values, column_blocks, counts, cotangent):
     local_rows, features = tokens.shape
     width = cotangent.shape[1]
@@ -47,12 +71,10 @@
         .astype(jnp.bfloat16)
         .reshape(features, width)
     )
-    share_rows = local_rows // sections
-    own_start = lax.axis_index("x") * share_rows
     partial_value = jnp.dot(tokens, weight, preferred_element_type=jnp.float32)
-    preact_all = lax.psum(partial_value, "x")
+    preact_own = lax.psum_scatter(partial_value, "x", scatter_dimension=0, tiled=True)
     cotangent_all = lax.all_gather(cotangent, "x", axis=0, tiled=True)
-    activation = lax.dynamic_slice_in_dim(preact_all, own_start, share_rows, 0).astype(jnp.bfloat16)
+    activation = preact_own.astype(jnp.bfloat16)
     picked = slot_grad(tokens, cotangent_all, column_blocks, counts, block, replicas)
     owned = features // replicas
     staged = (
@@ -60,9 +82,9 @@
         .transpose(2, 1, 0, 3, 4)
         .reshape(features, slots * block)
     )
-    staged = lax.psum_scatter(staged, "core", scatter_dimension=0, tiled=True)
-    staged = lax.psum_scatter(staged, "z", scatter_dimension=0, tiled=True)
-    weight_grad = lax.psum_scatter(staged, "y", scatter_dimension=0, tiled=True)
+    staged = ring_scatter(staged, "core")
+    staged = ring_scatter(staged, "z")
+    weight_grad = ring_scatter(staged, "y")
     input_grad = lax.dot_general(
         cotangent_all, weight, (((1,), (1,)), ((), ())), preferred_element_type=jnp.float32
     ).astype(jnp.bfloat16)

time: 205 us -> 208 us (1.015)
  blocking collectives: 40.4 us -> 0 us
  starting transfers between devices: 0.16 us -> 38.8 us
  other arithmetic: 0.74 us -> 11.9 us
  waiting for transfers between devices: 66.4 us -> 55.6 us
  local copies, waits for them, and re-layouts: 49.3 us -> 54.7 us
  matrix products: 32.8 us -> 29.1 us
    psum x1 -> x0, blocking collectives: 40.4 us -> none  [per_device(): preact_all = lax.psum(partial_value, 'x')]
    reduce_scatter x3 -> x1, waiting for transfers between devices: 39.5 us -> 0.01 us  [per_device(): lax.psum_scatter(partial_value, 'x', scatter_dimension=0, tiled=True)]
    ppermute x0 -> x21, starting transfers between devices: none -> 38.7 us  [the longest x10 34.6 us: ring_scatter(): b = lax.ppermute(b, axis, bwd) + take(idx + s + 2)[:, half:]]
    ppermute x0 -> x21, waiting for transfers between devices: none -> 28.8 us  [the longest x10 27.8 us: ring_scatter(): b = lax.ppermute(b, axis, bwd) + take(idx + s + 2)[:, half:]]
    add x0 -> x21, other arithmetic: none -> 9.39 us  [the longest x1 3.23 us: ring_scatter(): return take(idx) + lax.ppermute(take(idx + 1), axis, [(0, 1), (1, 0)])]
    transpose x1 -> x0, local copies, waits for them, and re-layouts: 6.17 us -> none  [per_device(): staged = picked.reshape(n_y, n_z, n_core, owned, slots * block).transpose...]
    reshape x0 -> x1, local copies, waits for them, and re-layouts: none -> 3.51 us  [per_device(): picked.reshape(n_y, n_z, n_core, owned, slots * block)]
    reshape x1, local copies, waits for them, and re-layouts: 7.14 us -> 10.6 us  [per_device(): blocks_view = block_values.reshape(row_blocks, block, slots, block)]
  transfers between devices with their start and end apart: 4 -> 23, of which waited for: 3 -> 14; matrix products, arithmetic and copies ran while one was open for 23% -> 26% of each run, Pallas kernels for 0% -> 0%
where the time goes in v2:
time: 208 us; the launch traced here: 205 us
  waiting for transfers between devices  55.6 us (27%)
  local copies, waits for them, and re-layouts  54.7 us (26%)
  starting transfers between devices  38.8 us (19%)
  matrix products  29.1 us (14%)
  between operations  14.7 us (7%)
  other arithmetic  11.9 us (6%)
    ppermute x10, starting transfers between devices, ring_scatter(): b = lax.ppermute(b, axis, bwd) + take(idx + s + 2)[:, half:]  34.6 us
    ppermute x10, waiting for transfers between devices, ring_scatter(): b = lax.ppermute(b, axis, bwd) + take(idx + s + 2)[:, half:]  27.8 us
    all_gather x1, waiting for transfers between devices, per_device(): cotangent_all = lax.all_gather(cotangent, 'x', axis=0, tiled=True)  26.7 us
    gather x1, local copies, waits for them, and re-layouts, slot_grad(): picked = jnp.take(cot_rows, column_blocks, axis=0, mode='clip')  14.2 us
    dot_general x1, matrix products, slot_grad(): lax.dot_general(tok_rows, picked, (((2,), (2,)), ((0,), (0,))), preferred...  14 us
    reshape x1, local copies, waits for them, and re-layouts, per_device(): weight = jnp.einsum('bkc,bikj->bicj', onehot, blocks_view, preferred_elem...  11.9 us
    unnamed x15, local copies, waits for them, and re-layouts  11.3 us
    reshape x1, local copies, waits for them, and re-layouts, per_device(): blocks_view = block_values.reshape(row_blocks, block, slots, block)  10.6 us
  transfers between devices with their start and end apart: 23, of which 14 were waited for; matrix products, arithmetic and copies ran while one was open for 26% of the time, Pallas kernels for 0%

profile of v2, /device:TPU:2, one launch (start us, length us, event | category | flops | bytes accessed | tf_op | source)
XLA Modules:
  0.0 204.8 jit_solution(13065534780658456703)
XLA Ops:
  11.0 2.9 %copy.18 = bf16[512,2048]{0,1:T(8,128)(2,1)S(1)} copy(bf16[512,2048]{1,0:T(8,128)(2,1)} %param.5) | data formatting | bytes 4194304 | tf_op args[0]
  13.9 26.7 %all-gather.2.cloned.1.call-done = bf16[512,1024]{0,1:T(8,128)(2,1)} async-done(((bf16[128,1024]{0,1:T(8,128)(2,1)}), bf16[512,1024]{0,1:T(8,128)(2,1)}) %all-gather.2.cloned.1.call-update) | async-done | bytes 1048592 | tf_op jit(solution)/shard_map/all_gather | solution.py:76
  40.6 14.2 %gather_fusion = bf16[384,64,512]{2,1,0:T(8,128)(2,1)} fusion(bf16[16,64,512]{2,1,0:T(8,128)(2,1)} %bitcast.87, s32[1024]{0:T(1024)S(1)} %pad_clamp_fusion), kind=kCustom, calls=%fused_computation | custom fusion | bytes 50333184 | tf_op jit(solution)/shard_map/jit(_take)/gather | solution.py:23
  54.8 14.0 %multiply_select_fusion = f32[32,768,64]{1,2,0:T(8,128)} fusion(pred[32,768]{1,0:T(8,128)(4,1)S(1)} %broadcast_in_dim.28, bf16[32,768,512]{2,1,0:T(8,128)(2,1)} %bitcast.89, bf16[32,64,512]{2,1,0:T(8,128)(2,1)S(1)} %bitcast.94), kind=kOutput, calls=%fused_computation.2 | convolution fusion | flops 1613758464 | bytes 33579008 | tf_op jit(solution)/shard_map/dot_general | solution.py:26
  68.8 3.5 %copy.19 = f32[4,8,2,32,768]{4,3,0,1,2:T(8,128)S(1)} copy(f32[4,8,2,32,768]{4,3,2,1,0:T(8,128)} %bitcast.92) | data formatting | bytes 12582912 | tf_op jit(solution)/shard_map/reshape | solution.py:81
  75.6 10.6 %reshape.78 = bf16[32,64,12,64]{3,2,1,0:T(8,128)(2,1)} reshape(bf16[2048,768]{1,0:T(8,128)(2,1)} %param.6) | data formatting | bytes 6291456 | tf_op jit(solution)/shard_map/reshape | solution.py:68
  86.2 9.0 %convert_bitcast_fusion = bf16[32,64,16,64]{3,2,1,0:T(8,128)(2,1)} fusion(bf16[32,64,12,64]{3,2,1,0:T(8,128)(2,1)} %reshape.78, s32[32,12]{1,0:T(8,128)S(1)} %copy.13, pred[32,12]{1,0:T(8,128)(4,1)S(1)} %iota_compare_fusion.1), kind=kOutput, calls=%fused_computation.1 | convolution fusion | flops 52441088 | bytes 7341952 | tf_op jit(solution)/shard_map/bkc,bikj->bicj/dot_general | solution.py:70
  95.2 11.9 %reshape.59 = bf16[2048,1024]{1,0:T(8,128)(2,1)} reshape(bf16[32,64,16,64]{3,2,1,0:T(8,128)(2,1)} %convert_bitcast_fusion) | data formatting | bytes 8388608 | tf_op jit(solution)/shard_map/reshape | solution.py:72
  107.1 3.2 %bitcast_add_fusion = f32[1024,768]{1,0:T(8,128)S(1)} fusion(f32[1024,768]{1,0:T(8,128)} %collective-permute-done, f32[2,1024,768]{2,1,0:T(8,128)} %bitcast.91, s32[]{:T(128)S(6)} %select_n.198), kind=kLoop, calls=%fused_computation.3 | loop fusion | flops 786432 | bytes 9437188 | tf_op jit(solution)/shard_map/add | solution.py:46
  114.4 3.7 %convolution_bitcast_fusion = f32[512,1024]{0,1:T(8,128)} fusion(bf16[2048,1024]{1,0:T(8,128)(2,1)S(1)} %copy-done.2, bf16[512,2048]{1,0:T(8,128)(2,1)S(1)} %copy-done.4), kind=kOutput, calls=%fused_computation.7 | convolution fusion | flops 2147483648 | bytes 8388608 | tf_op jit(solution)/shard_map/dot_general | solution.py:74
  118.3 3.1 %collective-permute-start.8 = (f32[128,384]{1,0:T(8,128)S(1)}, f32[128,384]{1,0:T(8,128)S(1)}, u32[]{:S(2)}, u32[]{:S(2)}) collective-permute-start(f32[128,384]{1,0:T(8,128)S(1)} %slice.106), channel_id=1, source_target_pairs={{0,14},{2,0},{4,2},{6,4},{8,6},{10,8},{12,10},{14,12},{1,15},{3,1}... | collective-permute-start | bytes 589832 | tf_op jit(solution)/shard_map/ppermute | solution.py:54
  122.9 3.1 %collective-permute-done.8 = f32[128,384]{1,0:T(8,128)S(1)} collective-permute-done((f32[128,384]{1,0:T(8,128)S(1)}, f32[128,384]{1,0:T(8,128)S(1)}, u32[]{:S(2)}, u32[]{:S(2)}) %collective-permute-start.8) | collective-permute-done | bytes 196640 | tf_op jit(solution)/shard_map/ppermute | solution.py:54
  126.9 3.8 %collective-permute-start.9 = (f32[128,384]{1,0:T(8,128)S(1)}, f32[128,384]{1,0:T(8,128)S(1)}, u32[]{:S(2)}, u32[]{:S(2)}) collective-permute-start(f32[128,384]{1,0:T(8,128)S(1)} %slice_add_fusion.6), channel_id=1, source_target_pairs={{0,14},{2,0},{4,2},{6,4},{8,6},{10,8},{12,10},{14,12},{1,15},{3,1}... | collective-permute-start | bytes 589832 | tf_op jit(solution)/shard_map/ppermute | solution.py:54
  135.4 3.8 %collective-permute-start.10 = (f32[128,384]{1,0:T(8,128)S(1)}, f32[128,384]{1,0:T(8,128)S(1)}, u32[]{:S(2)}, u32[]{:S(2)}) collective-permute-start(f32[128,384]{1,0:T(8,128)S(1)} %slice_add_fusion.5), channel_id=1, source_target_pairs={{0,14},{2,0},{4,2},{6,4},{8,6},{10,8},{12,10},{14,12},{1,15},{3,1}... | collective-permute-start | bytes 589832 | tf_op jit(solution)/shard_map/ppermute | solution.py:54
  143.3 3.8 %collective-permute-start.11 = (f32[128,384]{1,0:T(8,128)S(1)}, f32[128,384]{1,0:T(8,128)S(1)}, u32[]{:S(2)}, u32[]{:S(2)}) collective-permute-start(f32[128,384]{1,0:T(8,128)S(1)} %slice_add_fusion.4), channel_id=1, source_target_pairs={{0,14},{2,0},{4,2},{6,4},{8,6},{10,8},{12,10},{14,12},{1,15},{3,1}... | collective-permute-start | bytes 589832 | tf_op jit(solution)/shard_map/ppermute | solution.py:54
  147.2 3.1 %collective-permute-done.11 = f32[128,384]{1,0:T(8,128)S(1)} collective-permute-done((f32[128,384]{1,0:T(8,128)S(1)}, f32[128,384]{1,0:T(8,128)S(1)}, u32[]{:S(2)}, u32[]{:S(2)}) %collective-permute-start.11) | collective-permute-done | bytes 196640 | tf_op jit(solution)/shard_map/ppermute | solution.py:54
  150.3 3.8 %collective-permute-start.12 = (f32[128,384]{1,0:T(8,128)S(1)}, f32[128,384]{1,0:T(8,128)S(1)}, u32[]{:S(2)}, u32[]{:S(2)}) collective-permute-start(f32[128,384]{1,0:T(8,128)S(1)} %slice_add_fusion.3), channel_id=1, source_target_pairs={{0,14},{2,0},{4,2},{6,4},{8,6},{10,8},{12,10},{14,12},{1,15},{3,1}... | collective-permute-start | bytes 589832 | tf_op jit(solution)/shard_map/ppermute | solution.py:54
  154.3 3.9 %collective-permute-done.12 = f32[128,384]{1,0:T(8,128)S(1)} collective-permute-done((f32[128,384]{1,0:T(8,128)S(1)}, f32[128,384]{1,0:T(8,128)S(1)}, u32[]{:S(2)}, u32[]{:S(2)}) %collective-permute-start.12) | collective-permute-done | bytes 196640 | tf_op jit(solution)/shard_map/ppermute | solution.py:54
  158.3 3.8 %collective-permute-start.13 = (f32[128,384]{1,0:T(8,128)S(1)}, f32[128,384]{1,0:T(8,128)S(1)}, u32[]{:S(2)}, u32[]{:S(2)}) collective-permute-start(f32[128,384]{1,0:T(8,128)S(1)} %slice_add_fusion.2), channel_id=1, source_target_pairs={{0,14},{2,0},{4,2},{6,4},{8,6},{10,8},{12,10},{14,12},{1,15},{3,1}... | collective-permute-start | bytes 589832 | tf_op jit(solution)/shard_map/ppermute | solution.py:54
  162.6 4.6 %collective-permute-done.13 = f32[128,384]{1,0:T(8,128)S(1)} collective-permute-done((f32[128,384]{1,0:T(8,128)S(1)}, f32[128,384]{1,0:T(8,128)S(1)}, u32[]{:S(2)}, u32[]{:S(2)}) %collective-permute-start.13) | collective-permute-done | bytes 196640 | tf_op jit(solution)/shard_map/ppermute | solution.py:54
  167.2 4.0 %collective-permute-start.14 = (f32[128,384]{1,0:T(8,128)S(1)}, f32[128,384]{1,0:T(8,128)S(1)}, u32[]{:S(2)}, u32[]{:S(2)}) collective-permute-start(f32[128,384]{1,0:T(8,128)S(1)} %slice_add_fusion.1), channel_id=1, source_target_pairs={{0,14},{2,0},{4,2},{6,4},{8,6},{10,8},{12,10},{14,12},{1,15},{3,1}... | collective-permute-start | bytes 589832 | tf_op jit(solution)/shard_map/ppermute | solution.py:54
  171.2 3.2 %collective-permute-done.14 = f32[128,384]{1,0:T(8,128)S(1)} collective-permute-done((f32[128,384]{1,0:T(8,128)S(1)}, f32[128,384]{1,0:T(8,128)S(1)}, u32[]{:S(2)}, u32[]{:S(2)}) %collective-permute-start.14) | collective-permute-done | bytes 196640 | tf_op jit(solution)/shard_map/ppermute | solution.py:54
  186.9 3.3 %collective-permute-start.19 = (f32[32,384]{1,0:T(8,128)S(1)}, f32[32,384]{1,0:T(8,128)S(1)}, u32[]{:S(2)}, u32[]{:S(2)}) collective-permute-start(f32[32,384]{1,0:T(8,128)S(1)} %slice_add_fusion.16), channel_id=1, source_target_pairs={{0,48},{16,0},{32,16},{48,32},{1,49},{17,1},{33,17},{49,33},{2,50}... | collective-permute-start | bytes 147464 | tf_op jit(solution)/shard_map/ppermute | solution.py:54
  191.9 3.6 %collective-permute-start.20 = (f32[32,384]{1,0:T(8,128)S(1)}, f32[32,384]{1,0:T(8,128)S(1)}, u32[]{:S(2)}, u32[]{:S(2)}) collective-permute-start(f32[32,384]{1,0:T(8,128)S(1)} %slice_add_fusion.15), channel_id=1, source_target_pairs={{0,48},{16,0},{32,16},{48,32},{1,49},{17,1},{33,17},{49,33},{2,50}... | collective-permute-start | bytes 147464 | tf_op jit(solution)/shard_map/ppermute | solution.py:54
  (83 shorter events, 39.7 us)
Async XLA Ops:
  7.2 33.5 %all-gather.2.cloned.1.call-start = ((), (), s32[]{:S(2)}) async-start(), calls=%async_computation.2 | async-start | bytes 1310720 | tf_op jit(solution)/shard_map/all_gather | solution.py:76
  9.0 171.8 %reduce-scatter.2.cloned.1.call-start = ((), (), s32[]{:S(2)}) async-start(), calls=%async_computation.1 | async-start | bytes 2621440 | tf_op jit(solution)/shard_map/reduce_scatter | solution.py:75
  75.2 31.9 %collective-permute-start = (f32[1024,768]{1,0:T(8,128)S(1)}, f32[1024,768]{1,0:T(8,128)}, u32[]{:S(2)}, u32[]{:S(2)}) collective-permute-start(f32[1024,768]{1,0:T(8,128)S(1)} %dynamic-slice_bitcast_fusion), channel_id=1, source_target_pairs={{0,1},{1,0},{2,3},{3,2},{4,5},{5,4},{6,7},{7,6},{8,9},{9,8},{10,11... | collective-permute-start | bytes 9437192 | tf_op jit(solution)/shard_map/ppermute | solution.py:46
  112.8 8.9 %collective-permute-start.1 = (f32[128,384]{1,0:T(8,128)}, f32[128,384]{1,0:T(8,128)}, u32[]{:S(2)}, u32[]{:S(2)}) collective-permute-start(f32[128,384]{1,0:T(8,128)} %slice.98), channel_id=1, source_target_pairs={{0,2},{2,4},{4,6},{6,8},{8,10},{10,12},{12,14},{14,0},{1,3},{3,5},... | collective-permute-start | bytes 589832 | tf_op jit(solution)/shard_map/ppermute | solution.py:53
  118.3 7.7 %collective-permute-start.8 = (f32[128,384]{1,0:T(8,128)S(1)}, f32[128,384]{1,0:T(8,128)S(1)}, u32[]{:S(2)}, u32[]{:S(2)}) collective-permute-start(f32[128,384]{1,0:T(8,128)S(1)} %slice.106), channel_id=1, source_target_pairs={{0,14},{2,0},{4,2},{6,4},{8,6},{10,8},{12,10},{14,12},{1,15},{3,1}... | collective-permute-start | bytes 589832 | tf_op jit(solution)/shard_map/ppermute | solution.py:54
  122.8 7.9 %collective-permute-start.2 = (f32[128,384]{1,0:T(8,128)S(1)}, f32[128,384]{1,0:T(8,128)S(1)}, u32[]{:S(2)}, u32[]{:S(2)}) collective-permute-start(f32[128,384]{1,0:T(8,128)S(1)} %slice_add_fusion.13), channel_id=1, source_target_pairs={{0,2},{2,4},{4,6},{6,8},{8,10},{10,12},{12,14},{14,0},{1,3},{3,5},... | collective-permute-start | bytes 589832 | tf_op jit(solution)/shard_map/ppermute | solution.py:53
  126.9 7.5 %collective-permute-start.9 = (f32[128,384]{1,0:T(8,128)S(1)}, f32[128,384]{1,0:T(8,128)S(1)}, u32[]{:S(2)}, u32[]{:S(2)}) collective-permute-start(f32[128,384]{1,0:T(8,128)S(1)} %slice_add_fusion.6), channel_id=1, source_target_pairs={{0,14},{2,0},{4,2},{6,4},{8,6},{10,8},{12,10},{14,12},{1,15},{3,1}... | collective-permute-start | bytes 589832 | tf_op jit(solution)/shard_map/ppermute | solution.py:54
  131.7 7.4 %collective-permute-start.3 = (f32[128,384]{1,0:T(8,128)S(1)}, f32[128,384]{1,0:T(8,128)S(1)}, u32[]{:S(2)}, u32[]{:S(2)}) collective-permute-start(f32[128,384]{1,0:T(8,128)S(1)} %slice_add_fusion.12), channel_id=1, source_target_pairs={{0,2},{2,4},{4,6},{6,8},{8,10},{10,12},{12,14},{14,0},{1,3},{3,5},... | collective-permute-start | bytes 589832 | tf_op jit(solution)/shard_map/ppermute | solution.py:53
  135.3 40.7 %copy-start = (bf16[512,1024]{0,1:T(8,128)(2,1)S(1)}, bf16[512,1024]{0,1:T(8,128)(2,1)}, u32[]{:S(2)}) copy-start(bf16[512,1024]{0,1:T(8,128)(2,1)} %all-gather.2.cloned.1.call-done) | copy-start | bytes 3145732
  135.4 7.0 %collective-permute-start.10 = (f32[128,384]{1,0:T(8,128)S(1)}, f32[128,384]{1,0:T(8,128)S(1)}, u32[]{:S(2)}, u32[]{:S(2)}) collective-permute-start(f32[128,384]{1,0:T(8,128)S(1)} %slice_add_fusion.5), channel_id=1, source_target_pairs={{0,14},{2,0},{4,2},{6,4},{8,6},{10,8},{12,10},{14,12},{1,15},{3,1}... | collective-permute-start | bytes 589832 | tf_op jit(solution)/shard_map/ppermute | solution.py:54
  140.1 7.0 %collective-permute-start.4 = (f32[128,384]{1,0:T(8,128)S(1)}, f32[128,384]{1,0:T(8,128)S(1)}, u32[]{:S(2)}, u32[]{:S(2)}) collective-permute-start(f32[128,384]{1,0:T(8,128)S(1)} %slice_add_fusion.11), channel_id=1, source_target_pairs={{0,2},{2,4},{4,6},{6,8},{8,10},{10,12},{12,14},{14,0},{1,3},{3,5},... | collective-permute-start | bytes 589832 | tf_op jit(solution)/shard_map/ppermute | solution.py:53
  143.3 7.0 %collective-permute-start.11 = (f32[128,384]{1,0:T(8,128)S(1)}, f32[128,384]{1,0:T(8,128)S(1)}, u32[]{:S(2)}, u32[]{:S(2)}) collective-permute-start(f32[128,384]{1,0:T(8,128)S(1)} %slice_add_fusion.4), channel_id=1, source_target_pairs={{0,14},{2,0},{4,2},{6,4},{8,6},{10,8},{12,10},{14,12},{1,15},{3,1}... | collective-permute-start | bytes 589832 | tf_op jit(solution)/shard_map/ppermute | solution.py:54
  147.1 7.1 %collective-permute-start.5 = (f32[128,384]{1,0:T(8,128)S(1)}, f32[128,384]{1,0:T(8,128)S(1)}, u32[]{:S(2)}, u32[]{:S(2)}) collective-permute-start(f32[128,384]{1,0:T(8,128)S(1)} %slice_add_fusion.10), channel_id=1, source_target_pairs={{0,2},{2,4},{4,6},{6,8},{8,10},{10,12},{12,14},{14,0},{1,3},{3,5},... | collective-permute-start | bytes 589832 | tf_op jit(solution)/shard_map/ppermute | solution.py:53
  150.3 8.0 %collective-permute-start.12 = (f32[128,384]{1,0:T(8,128)S(1)}, f32[128,384]{1,0:T(8,128)S(1)}, u32[]{:S(2)}, u32[]{:S(2)}) collective-permute-start(f32[128,384]{1,0:T(8,128)S(1)} %slice_add_fusion.3), channel_id=1, source_target_pairs={{0,14},{2,0},{4,2},{6,4},{8,6},{10,8},{12,10},{14,12},{1,15},{3,1}... | collective-permute-start | bytes 589832 | tf_op jit(solution)/shard_map/ppermute | solution.py:54
  154.2 8.3 %collective-permute-start.6 = (f32[128,384]{1,0:T(8,128)S(1)}, f32[128,384]{1,0:T(8,128)S(1)}, u32[]{:S(2)}, u32[]{:S(2)}) collective-permute-start(f32[128,384]{1,0:T(8,128)S(1)} %slice_add_fusion.9), channel_id=1, source_target_pairs={{0,2},{2,4},{4,6},{6,8},{8,10},{10,12},{12,14},{14,0},{1,3},{3,5},... | collective-permute-start | bytes 589832 | tf_op jit(solution)/shard_map/ppermute | solution.py:53
  158.3 8.9 %collective-permute-start.13 = (f32[128,384]{1,0:T(8,128)S(1)}, f32[128,384]{1,0:T(8,128)S(1)}, u32[]{:S(2)}, u32[]{:S(2)}) collective-permute-start(f32[128,384]{1,0:T(8,128)S(1)} %slice_add_fusion.2), channel_id=1, source_target_pairs={{0,14},{2,0},{4,2},{6,4},{8,6},{10,8},{12,10},{14,12},{1,15},{3,1}... | collective-permute-start | bytes 589832 | tf_op jit(solution)/shard_map/ppermute | solution.py:54
  162.5 8.7 %collective-permute-start.7 = (f32[128,384]{1,0:T(8,128)S(1)}, f32[128,384]{1,0:T(8,128)S(1)}, u32[]{:S(2)}, u32[]{:S(2)}) collective-permute-start(f32[128,384]{1,0:T(8,128)S(1)} %slice_add_fusion.8), channel_id=1, source_target_pairs={{0,2},{2,4},{4,6},{6,8},{8,10},{10,12},{12,14},{14,0},{1,3},{3,5},... | collective-permute-start | bytes 589832 | tf_op jit(solution)/shard_map/ppermute | solution.py:53
  167.2 7.2 %collective-permute-start.14 = (f32[128,384]{1,0:T(8,128)S(1)}, f32[128,384]{1,0:T(8,128)S(1)}, u32[]{:S(2)}, u32[]{:S(2)}) collective-permute-start(f32[128,384]{1,0:T(8,128)S(1)} %slice_add_fusion.1), channel_id=1, source_target_pairs={{0,14},{2,0},{4,2},{6,4},{8,6},{10,8},{12,10},{14,12},{1,15},{3,1}... | collective-permute-start | bytes 589832 | tf_op jit(solution)/shard_map/ppermute | solution.py:54
  174.5 10.0 %collective-permute-start.15 = (f32[32,384]{1,0:T(8,128)S(1)}, f32[32,384]{1,0:T(8,128)S(1)}, u32[]{:S(2)}, u32[]{:S(2)}) collective-permute-start(f32[32,384]{1,0:T(8,128)S(1)} %slice.114), channel_id=1, source_target_pairs={{0,16},{16,32},{32,48},{48,0},{1,17},{17,33},{33,49},{49,1},{2,18}... | collective-permute-start | bytes 147464 | tf_op jit(solution)/shard_map/ppermute | solution.py:53
  182.8 4.1 %collective-permute-start.18 = (f32[32,384]{1,0:T(8,128)S(1)}, f32[32,384]{1,0:T(8,128)S(1)}, u32[]{:S(2)}, u32[]{:S(2)}) collective-permute-start(f32[32,384]{1,0:T(8,128)S(1)} %slice.118), channel_id=1, source_target_pairs={{0,48},{16,0},{32,16},{48,32},{1,49},{17,1},{33,17},{49,33},{2,50}... | collective-permute-start | bytes 147464 | tf_op jit(solution)/shard_map/ppermute | solution.py:54
  184.5 5.6 %collective-permute-start.16 = (f32[32,384]{1,0:T(8,128)S(1)}, f32[32,384]{1,0:T(8,128)S(1)}, u32[]{:S(2)}, u32[]{:S(2)}) collective-permute-start(f32[32,384]{1,0:T(8,128)S(1)} %slice_add_fusion.19), channel_id=1, source_target_pairs={{0,16},{16,32},{32,48},{48,0},{1,17},{17,33},{33,49},{49,1},{2,18}... | collective-permute-start | bytes 147464 | tf_op jit(solution)/shard_map/ppermute | solution.py:53
  186.9 5.0 %collective-permute-start.19 = (f32[32,384]{1,0:T(8,128)S(1)}, f32[32,384]{1,0:T(8,128)S(1)}, u32[]{:S(2)}, u32[]{:S(2)}) collective-permute-start(f32[32,384]{1,0:T(8,128)S(1)} %slice_add_fusion.16), channel_id=1, source_target_pairs={{0,48},{16,0},{32,16},{48,32},{1,49},{17,1},{33,17},{49,33},{2,50}... | collective-permute-start | bytes 147464 | tf_op jit(solution)/shard_map/ppermute | solution.py:54
  190.2 5.4 %collective-permute-start.17 = (f32[32,384]{1,0:T(8,128)S(1)}, f32[32,384]{1,0:T(8,128)S(1)}, u32[]{:S(2)}, u32[]{:S(2)}) collective-permute-start(f32[32,384]{1,0:T(8,128)S(1)} %slice_add_fusion.18), channel_id=1, source_target_pairs={{0,16},{16,32},{32,48},{48,0},{1,17},{17,33},{33,49},{49,1},{2,18}... | collective-permute-start | bytes 147464 | tf_op jit(solution)/shard_map/ppermute | solution.py:53
  191.9 5.4 %collective-permute-start.20 = (f32[32,384]{1,0:T(8,128)S(1)}, f32[32,384]{1,0:T(8,128)S(1)}, u32[]{:S(2)}, u32[]{:S(2)}) collective-permute-start(f32[32,384]{1,0:T(8,128)S(1)} %slice_add_fusion.15), channel_id=1, source_target_pairs={{0,48},{16,0},{32,16},{48,32},{1,49},{17,1},{33,17},{49,33},{2,50}... | collective-permute-start | bytes 147464 | tf_op jit(solution)/shard_map/ppermute | solution.py:54
  (4 other events, 51.5 us)
Sparse Core Ops, SparseCore 0:
  10.3 30.2 all-gather.1
  118.2 32.3 reduce-scatter.1

commit v3 on v2

--- a/solution.py
+++ b/solution.py
@@ -61,7 +61,6 @@
     row_blocks, slots = column_blocks.shape
     block = features // row_blocks
     col_blocks = width // block
-    sections = lax.axis_size("x")
     replicas = lax.axis_size(DP_AXES)
     n_y, n_z, n_core = (lax.axis_size(a) for a in DP_AXES)
     onehot = block_onehot(column_blocks, counts, col_blocks).astype(jnp.bfloat16)
@@ -72,8 +71,9 @@
         .reshape(features, width)
     )
     partial_value = jnp.dot(tokens, weight, preferred_element_type=jnp.float32)
+    cotangent_all = lax.all_gather(cotangent, "x", axis=0, tiled=True)
+    partial_value, cotangent_all = lax.optimization_barrier((partial_value, cotangent_all))
     preact_own = lax.psum_scatter(partial_value, "x", scatter_dimension=0, tiled=True)
-    cotangent_all = lax.all_gather(cotangent, "x", axis=0, tiled=True)
     activation = preact_own.astype(jnp.bfloat16)
     picked = slot_grad(tokens, cotangent_all, column_blocks, counts, block, replicas)
     owned = features // replicas

time: 208 us -> 194 us (0.933); the launches traced: 205 us -> 194 us
  waiting for transfers between devices: 55.6 us -> 44.1 us
  matrix products: 29.1 us -> 32.6 us
  local copies, waits for them, and re-layouts: 54.7 us -> 51.5 us
    all_gather x1, waiting for transfers between devices: 26.7 us -> 0.01 us  [per_device(): cotangent_all = lax.all_gather(cotangent, 'x', axis=0, tiled=True)]
    ppermute x10, waiting for transfers between devices: 0.97 us -> 19.2 us  [ring_scatter(): a = lax.ppermute(a, axis, fwd) + take(idx - s - 2)[:, :half]]
    ppermute x10, waiting for transfers between devices: 27.8 us -> 19.3 us  [ring_scatter(): b = lax.ppermute(b, axis, bwd) + take(idx + s + 2)[:, half:]]
    ppermute x1, waiting for transfers between devices: 0.01 us -> 5.48 us  [ring_scatter(): return take(idx) + lax.ppermute(take(idx + 1), axis, [(0, 1), (1, 0)])]
    ppermute x10, starting transfers between devices: 34.6 us -> 38.3 us  [ring_scatter(): b = lax.ppermute(b, axis, bwd) + take(idx + s + 2)[:, half:]]
    unnamed x15 -> x18, local copies, waits for them, and re-layouts: 11.3 us -> 7.89 us
    ppermute x10, starting transfers between devices: 4.05 us -> 0.96 us  [ring_scatter(): a = lax.ppermute(a, axis, fwd) + take(idx - s - 2)[:, :half]]
    dot_general x1, matrix products: 3.73 us -> 5.91 us  [per_device(): partial_value = jnp.dot(tokens, weight, preferred_element_type=jnp.float32)]
  transfers between devices with their start and end apart: 23 -> 23, of which waited for: 14 -> 15; matrix products, arithmetic and copies ran while one was open for 26% -> 27% of each run, Pallas kernels for 0% -> 0%
where the time goes in v3:
time: 194 us
  local copies, waits for them, and re-layouts  51.5 us (27%)
  waiting for transfers between devices  44.1 us (23%)
  starting transfers between devices  39.6 us (20%)
  matrix products  32.6 us (17%)
  between operations  14.6 us (8%)
  other arithmetic  11.2 us (6%)
    ppermute x10, starting transfers between devices, ring_scatter(): b = lax.ppermute(b, axis, bwd) + take(idx + s + 2)[:, half:]  38.3 us
    ppermute x10, waiting for transfers between devices, ring_scatter(): b = lax.ppermute(b, axis, bwd) + take(idx + s + 2)[:, half:]  19.3 us
    ppermute x10, waiting for transfers between devices, ring_scatter(): a = lax.ppermute(a, axis, fwd) + take(idx - s - 2)[:, :half]  19.2 us
    gather x1, local copies, waits for them, and re-layouts, slot_grad(): picked = jnp.take(cot_rows, column_blocks, axis=0, mode='clip')  14.3 us
    dot_general x1, matrix products, slot_grad(): lax.dot_general(tok_rows, picked, (((2,), (2,)), ((0,), (0,))), preferred...  14 us
    reshape x1, local copies, waits for them, and re-layouts, per_device(): weight = jnp.einsum('bkc,bikj->bicj', onehot, blocks_view, preferred_elem...  12.1 us
    reshape x1, local copies, waits for them, and re-layouts, per_device(): blocks_view = block_values.reshape(row_blocks, block, slots, block)  10.6 us
    dot_general x1, matrix products, per_device(): jnp.einsum('bkc,bikj->bicj', onehot, blocks_view, preferred_element_type=...  8.97 us
  transfers between devices with their start and end apart: 23, of which 15 were waited for; matrix products, arithmetic and copies ran while one was open for 27% of the time, Pallas kernels for 0%

profile of v3, /device:TPU:2, one launch (start us, length us, event | category | flops | bytes accessed | tf_op | source)
XLA Modules:
  0.0 193.6 jit_solution(4972281606961725056)
XLA Ops:
  9.1 10.6 %reshape.78 = bf16[32,64,12,64]{3,2,1,0:T(8,128)(2,1)} reshape(bf16[2048,768]{1,0:T(8,128)(2,1)} %param.6) | data formatting | bytes 6291456 | tf_op jit(solution)/shard_map/reshape | solution.py:67
  20.0 9.0 %convert_bitcast_fusion = bf16[32,64,16,64]{3,2,1,0:T(8,128)(2,1)} fusion(bf16[32,64,12,64]{3,2,1,0:T(8,128)(2,1)} %reshape.78, s32[32,12]{1,0:T(8,128)S(1)} %copy.12, pred[32,12]{1,0:T(8,128)(4,1)S(1)} %iota_compare_fusion.1), kind=kOutput, calls=%fused_computation.1 | convolution fusion | flops 52441088 | bytes 7341952 | tf_op jit(solution)/shard_map/bkc,bikj->bicj/dot_general | solution.py:69
  29.0 12.1 %reshape.59 = bf16[2048,1024]{1,0:T(8,128)(2,1)} reshape(bf16[32,64,16,64]{3,2,1,0:T(8,128)(2,1)} %convert_bitcast_fusion) | data formatting | bytes 8388608 | tf_op jit(solution)/shard_map/reshape | solution.py:71
  43.8 5.9 %convolution_bitcast_fusion = f32[512,1024]{0,1:T(8,128)} fusion(bf16[2048,1024]{1,0:T(8,128)(2,1)} %reshape.59, bf16[512,2048]{1,0:T(8,128)(2,1)S(1)} %copy-done.3), kind=kOutput, calls=%fused_computation.6 | convolution fusion | flops 2147483648 | bytes 8388608 | tf_op jit(solution)/shard_map/dot_general | solution.py:73
  49.7 14.3 %gather_fusion = bf16[384,64,512]{2,1,0:T(8,128)(2,1)} fusion(bf16[16,64,512]{2,1,0:T(8,128)(2,1)} %bitcast.85, s32[1024]{0:T(1024)S(1)} %pad_clamp_fusion), kind=kCustom, calls=%fused_computation | custom fusion | bytes 50333184 | tf_op jit(solution)/shard_map/jit(_take)/gather | solution.py:23
  64.1 14.0 %multiply_select_fusion = f32[32,768,64]{1,2,0:T(8,128)} fusion(pred[32,768]{1,0:T(8,128)(4,1)S(1)} %broadcast_in_dim.28, bf16[32,768,512]{2,1,0:T(8,128)(2,1)} %bitcast.87, bf16[32,64,512]{2,1,0:T(8,128)(2,1)S(1)} %bitcast.92), kind=kOutput, calls=%fused_computation.2 | convolution fusion | flops 1613758464 | bytes 33579008 | tf_op jit(solution)/shard_map/dot_general | solution.py:26
  78.1 3.5 %copy.18 = f32[4,8,2,32,768]{4,3,0,1,2:T(8,128)S(1)} copy(f32[4,8,2,32,768]{4,3,2,1,0:T(8,128)} %bitcast.90) | data formatting | bytes 12582912 | tf_op jit(solution)/shard_map/reshape | solution.py:81
  85.0 5.5 %collective-permute-done = f32[1024,768]{1,0:T(8,128)} collective-permute-done((f32[1024,768]{1,0:T(8,128)S(1)}, f32[1024,768]{1,0:T(8,128)}, u32[]{:S(2)}, u32[]{:S(2)}) %collective-permute-start) | collective-permute-done | bytes 3145760 | tf_op jit(solution)/shard_map/ppermute | solution.py:46
  90.5 3.2 %bitcast_add_fusion = f32[1024,768]{1,0:T(8,128)S(1)} fusion(f32[1024,768]{1,0:T(8,128)} %collective-permute-done, f32[2,1024,768]{2,1,0:T(8,128)} %bitcast.89, s32[]{:T(128)S(6)} %select_n.198), kind=kLoop, calls=%fused_computation.3 | loop fusion | flops 786432 | bytes 9437188 | tf_op jit(solution)/shard_map/add | solution.py:46
  96.2 6.0 %collective-permute-start.8 = (f32[128,384]{1,0:T(8,128)}, f32[128,384]{1,0:T(8,128)}, u32[]{:S(2)}, u32[]{:S(2)}) collective-permute-start(f32[128,384]{1,0:T(8,128)} %slice.106), channel_id=1, source_target_pairs={{0,14},{2,0},{4,2},{6,4},{8,6},{10,8},{12,10},{14,12},{1,15},{3,1}... | collective-permute-start | bytes 589832 | tf_op jit(solution)/shard_map/ppermute | solution.py:54
  102.3 4.6 %collective-permute-done.8 = f32[128,384]{1,0:T(8,128)} collective-permute-done((f32[128,384]{1,0:T(8,128)}, f32[128,384]{1,0:T(8,128)}, u32[]{:S(2)}, u32[]{:S(2)}) %collective-permute-start.8) | collective-permute-done | bytes 196640 | tf_op jit(solution)/shard_map/ppermute | solution.py:54
  108.0 3.8 %collective-permute-start.9 = (f32[128,384]{1,0:T(8,128)S(1)}, f32[128,384]{1,0:T(8,128)S(1)}, u32[]{:S(2)}, u32[]{:S(2)}) collective-permute-start(f32[128,384]{1,0:T(8,128)S(1)} %slice_add_fusion.6), channel_id=1, source_target_pairs={{0,14},{2,0},{4,2},{6,4},{8,6},{10,8},{12,10},{14,12},{1,15},{3,1}... | collective-permute-start | bytes 589832 | tf_op jit(solution)/shard_map/ppermute | solution.py:54
  116.4 3.8 %collective-permute-start.10 = (f32[128,384]{1,0:T(8,128)S(1)}, f32[128,384]{1,0:T(8,128)S(1)}, u32[]{:S(2)}, u32[]{:S(2)}) collective-permute-start(f32[128,384]{1,0:T(8,128)S(1)} %slice_add_fusion.5), channel_id=1, source_target_pairs={{0,14},{2,0},{4,2},{6,4},{8,6},{10,8},{12,10},{14,12},{1,15},{3,1}... | collective-permute-start | bytes 589832 | tf_op jit(solution)/shard_map/ppermute | solution.py:54
  124.3 3.8 %collective-permute-start.11 = (f32[128,384]{1,0:T(8,128)S(1)}, f32[128,384]{1,0:T(8,128)S(1)}, u32[]{:S(2)}, u32[]{:S(2)}) collective-permute-start(f32[128,384]{1,0:T(8,128)S(1)} %slice_add_fusion.4), channel_id=1, source_target_pairs={{0,14},{2,0},{4,2},{6,4},{8,6},{10,8},{12,10},{14,12},{1,15},{3,1}... | collective-permute-start | bytes 589832 | tf_op jit(solution)/shard_map/ppermute | solution.py:54
  131.3 3.8 %collective-permute-start.12 = (f32[128,384]{1,0:T(8,128)S(1)}, f32[128,384]{1,0:T(8,128)S(1)}, u32[]{:S(2)}, u32[]{:S(2)}) collective-permute-start(f32[128,384]{1,0:T(8,128)S(1)} %slice_add_fusion.3), channel_id=1, source_target_pairs={{0,14},{2,0},{4,2},{6,4},{8,6},{10,8},{12,10},{14,12},{1,15},{3,1}... | collective-permute-start | bytes 589832 | tf_op jit(solution)/shard_map/ppermute | solution.py:54
  139.4 3.8 %collective-permute-start.13 = (f32[128,384]{1,0:T(8,128)S(1)}, f32[128,384]{1,0:T(8,128)S(1)}, u32[]{:S(2)}, u32[]{:S(2)}) collective-permute-start(f32[128,384]{1,0:T(8,128)S(1)} %slice_add_fusion.2), channel_id=1, source_target_pairs={{0,14},{2,0},{4,2},{6,4},{8,6},{10,8},{12,10},{14,12},{1,15},{3,1}... | collective-permute-start | bytes 589832 | tf_op jit(solution)/shard_map/ppermute | solution.py:54
  144.8 3.5 %collective-permute-done.13 = f32[128,384]{1,0:T(8,128)S(1)} collective-permute-done((f32[128,384]{1,0:T(8,128)S(1)}, f32[128,384]{1,0:T(8,128)S(1)}, u32[]{:S(2)}, u32[]{:S(2)}) %collective-permute-start.13) | collective-permute-done | bytes 196640 | tf_op jit(solution)/shard_map/ppermute | solution.py:54
  148.3 3.8 %collective-permute-start.14 = (f32[128,384]{1,0:T(8,128)S(1)}, f32[128,384]{1,0:T(8,128)S(1)}, u32[]{:S(2)}, u32[]{:S(2)}) collective-permute-start(f32[128,384]{1,0:T(8,128)S(1)} %slice_add_fusion.1), channel_id=1, source_target_pairs={{0,14},{2,0},{4,2},{6,4},{8,6},{10,8},{12,10},{14,12},{1,15},{3,1}... | collective-permute-start | bytes 589832 | tf_op jit(solution)/shard_map/ppermute | solution.py:54
  155.3 5.4 %collective-permute-done.7 = f32[128,384]{1,0:T(8,128)S(1)} collective-permute-done((f32[128,384]{1,0:T(8,128)S(1)}, f32[128,384]{1,0:T(8,128)S(1)}, u32[]{:S(2)}, u32[]{:S(2)}) %collective-permute-start.7) | collective-permute-done | bytes 196640 | tf_op jit(solution)/shard_map/ppermute | solution.py:53
  160.9 3.1 %collective-permute-start.18 = (f32[32,384]{1,0:T(8,128)S(1)}, f32[32,384]{1,0:T(8,128)S(1)}, u32[]{:S(2)}, u32[]{:S(2)}) collective-permute-start(f32[32,384]{1,0:T(8,128)S(1)} %slice.118), channel_id=1, source_target_pairs={{0,48},{16,0},{32,16},{48,32},{1,49},{17,1},{33,17},{49,33},{2,50}... | collective-permute-start | bytes 147464 | tf_op jit(solution)/shard_map/ppermute | solution.py:54
  164.0 3.7 %convolution_convert_fusion = bf16[512,2048]{1,0:T(8,128)(2,1)} fusion(bf16[512,1024]{0,1:T(8,128)(2,1)S(1)} %copy-done, bf16[2048,1024]{1,0:T(8,128)(2,1)S(1)} %copy-done.2), kind=kOutput, calls=%fused_computation.5 | convolution fusion | flops 2148532224 | bytes 7340032 | tf_op jit(solution)/shard_map/dot_general | solution.py:88
  169.6 3.3 %collective-permute-start.19 = (f32[32,384]{1,0:T(8,128)S(1)}, f32[32,384]{1,0:T(8,128)S(1)}, u32[]{:S(2)}, u32[]{:S(2)}) collective-permute-start(f32[32,384]{1,0:T(8,128)S(1)} %slice_add_fusion.16), channel_id=1, source_target_pairs={{0,48},{16,0},{32,16},{48,32},{1,49},{17,1},{33,17},{49,33},{2,50}... | collective-permute-start | bytes 147464 | tf_op jit(solution)/shard_map/ppermute | solution.py:54
  175.4 3.3 %collective-permute-start.20 = (f32[32,384]{1,0:T(8,128)S(1)}, f32[32,384]{1,0:T(8,128)S(1)}, u32[]{:S(2)}, u32[]{:S(2)}) collective-permute-start(f32[32,384]{1,0:T(8,128)S(1)} %slice_add_fusion.15), channel_id=1, source_target_pairs={{0,48},{16,0},{32,16},{48,32},{1,49},{17,1},{33,17},{49,33},{2,50}... | collective-permute-start | bytes 147464 | tf_op jit(solution)/shard_map/ppermute | solution.py:54
  180.8 5.3 %collective-permute-done.17 = f32[32,384]{1,0:T(8,128)S(1)} collective-permute-done((f32[32,384]{1,0:T(8,128)S(1)}, f32[32,384]{1,0:T(8,128)S(1)}, u32[]{:S(2)}, u32[]{:S(2)}) %collective-permute-start.17) | collective-permute-done | bytes 49184 | tf_op jit(solution)/shard_map/ppermute | solution.py:53
  (86 shorter events, 40.0 us)
Async XLA Ops:
  7.2 42.5 %all-gather.2.cloned.1.call-start = ((), (), s32[]{:S(2)}) async-start(), calls=%async_computation.1 | async-start | bytes 1310720 | tf_op jit(solution)/shard_map/all_gather | solution.py:74
  9.0 158.6 %reduce-scatter.2.cloned.1.call-start = ((), (), s32[]{:S(2)}) async-start(), calls=%async_computation.2 | async-start | bytes 2621440 | tf_op jit(solution)/shard_map/reduce_scatter | solution.py:76
  84.4 6.1 %collective-permute-start = (f32[1024,768]{1,0:T(8,128)S(1)}, f32[1024,768]{1,0:T(8,128)}, u32[]{:S(2)}, u32[]{:S(2)}) collective-permute-start(f32[1024,768]{1,0:T(8,128)S(1)} %dynamic-slice_bitcast_fusion), channel_id=1, source_target_pairs={{0,1},{1,0},{2,3},{3,2},{4,5},{5,4},{6,7},{7,6},{8,9},{9,8},{10,11... | collective-permute-start | bytes 9437192 | tf_op jit(solution)/shard_map/ppermute | solution.py:46
  96.2 10.8 %collective-permute-start.8 = (f32[128,384]{1,0:T(8,128)}, f32[128,384]{1,0:T(8,128)}, u32[]{:S(2)}, u32[]{:S(2)}) collective-permute-start(f32[128,384]{1,0:T(8,128)} %slice.106), channel_id=1, source_target_pairs={{0,14},{2,0},{4,2},{6,4},{8,6},{10,8},{12,10},{14,12},{1,15},{3,1}... | collective-permute-start | bytes 589832 | tf_op jit(solution)/shard_map/ppermute | solution.py:54
  102.3 9.5 %collective-permute-start.1 = (f32[128,384]{1,0:T(8,128)S(1)}, f32[128,384]{1,0:T(8,128)S(1)}, u32[]{:S(2)}, u32[]{:S(2)}) collective-permute-start(f32[128,384]{1,0:T(8,128)S(1)} %slice.98), channel_id=1, source_target_pairs={{0,2},{2,4},{4,6},{6,8},{8,10},{10,12},{12,14},{14,0},{1,3},{3,5},... | collective-permute-start | bytes 589832 | tf_op jit(solution)/shard_map/ppermute | solution.py:53
  108.0 7.4 %collective-permute-start.9 = (f32[128,384]{1,0:T(8,128)S(1)}, f32[128,384]{1,0:T(8,128)S(1)}, u32[]{:S(2)}, u32[]{:S(2)}) collective-permute-start(f32[128,384]{1,0:T(8,128)S(1)} %slice_add_fusion.6), channel_id=1, source_target_pairs={{0,14},{2,0},{4,2},{6,4},{8,6},{10,8},{12,10},{14,12},{1,15},{3,1}... | collective-permute-start | bytes 589832 | tf_op jit(solution)/shard_map/ppermute | solution.py:54
  112.8 7.4 %collective-permute-start.2 = (f32[128,384]{1,0:T(8,128)S(1)}, f32[128,384]{1,0:T(8,128)S(1)}, u32[]{:S(2)}, u32[]{:S(2)}) collective-permute-start(f32[128,384]{1,0:T(8,128)S(1)} %slice_add_fusion.13), channel_id=1, source_target_pairs={{0,2},{2,4},{4,6},{6,8},{8,10},{10,12},{12,14},{14,0},{1,3},{3,5},... | collective-permute-start | bytes 589832 | tf_op jit(solution)/shard_map/ppermute | solution.py:53
  116.4 7.0 %collective-permute-start.10 = (f32[128,384]{1,0:T(8,128)S(1)}, f32[128,384]{1,0:T(8,128)S(1)}, u32[]{:S(2)}, u32[]{:S(2)}) collective-permute-start(f32[128,384]{1,0:T(8,128)S(1)} %slice_add_fusion.5), channel_id=1, source_target_pairs={{0,14},{2,0},{4,2},{6,4},{8,6},{10,8},{12,10},{14,12},{1,15},{3,1}... | collective-permute-start | bytes 589832 | tf_op jit(solution)/shard_map/ppermute | solution.py:54
  121.1 42.9 %copy-start = (bf16[512,1024]{0,1:T(8,128)(2,1)S(1)}, bf16[512,1024]{0,1:T(8,128)(2,1)}, u32[]{:S(2)}) copy-start(bf16[512,1024]{0,1:T(8,128)(2,1)} %all-gather.2.cloned.1.call-done) | copy-start | bytes 3145732
  121.1 7.0 %collective-permute-start.3 = (f32[128,384]{1,0:T(8,128)S(1)}, f32[128,384]{1,0:T(8,128)S(1)}, u32[]{:S(2)}, u32[]{:S(2)}) collective-permute-start(f32[128,384]{1,0:T(8,128)S(1)} %slice_add_fusion.12), channel_id=1, source_target_pairs={{0,2},{2,4},{4,6},{6,8},{8,10},{10,12},{12,14},{14,0},{1,3},{3,5},... | collective-permute-start | bytes 589832 | tf_op jit(solution)/shard_map/ppermute | solution.py:53
  124.3 7.0 %collective-permute-start.11 = (f32[128,384]{1,0:T(8,128)S(1)}, f32[128,384]{1,0:T(8,128)S(1)}, u32[]{:S(2)}, u32[]{:S(2)}) collective-permute-start(f32[128,384]{1,0:T(8,128)S(1)} %slice_add_fusion.4), channel_id=1, source_target_pairs={{0,14},{2,0},{4,2},{6,4},{8,6},{10,8},{12,10},{14,12},{1,15},{3,1}... | collective-permute-start | bytes 589832 | tf_op jit(solution)/shard_map/ppermute | solution.py:54
  129.0 7.2 %collective-permute-start.4 = (f32[128,384]{1,0:T(8,128)S(1)}, f32[128,384]{1,0:T(8,128)S(1)}, u32[]{:S(2)}, u32[]{:S(2)}) collective-permute-start(f32[128,384]{1,0:T(8,128)S(1)} %slice_add_fusion.11), channel_id=1, source_target_pairs={{0,2},{2,4},{4,6},{6,8},{8,10},{10,12},{12,14},{14,0},{1,3},{3,5},... | collective-permute-start | bytes 589832 | tf_op jit(solution)/shard_map/ppermute | solution.py:53
  131.3 8.1 %collective-permute-start.12 = (f32[128,384]{1,0:T(8,128)S(1)}, f32[128,384]{1,0:T(8,128)S(1)}, u32[]{:S(2)}, u32[]{:S(2)}) collective-permute-start(f32[128,384]{1,0:T(8,128)S(1)} %slice_add_fusion.3), channel_id=1, source_target_pairs={{0,14},{2,0},{4,2},{6,4},{8,6},{10,8},{12,10},{14,12},{1,15},{3,1}... | collective-permute-start | bytes 589832 | tf_op jit(solution)/shard_map/ppermute | solution.py:54
  136.3 8.4 %collective-permute-start.5 = (f32[128,384]{1,0:T(8,128)S(1)}, f32[128,384]{1,0:T(8,128)S(1)}, u32[]{:S(2)}, u32[]{:S(2)}) collective-permute-start(f32[128,384]{1,0:T(8,128)S(1)} %slice_add_fusion.10), channel_id=1, source_target_pairs={{0,2},{2,4},{4,6},{6,8},{8,10},{10,12},{12,14},{14,0},{1,3},{3,5},... | collective-permute-start | bytes 589832 | tf_op jit(solution)/shard_map/ppermute | solution.py:53
  139.4 8.9 %collective-permute-start.13 = (f32[128,384]{1,0:T(8,128)S(1)}, f32[128,384]{1,0:T(8,128)S(1)}, u32[]{:S(2)}, u32[]{:S(2)}) collective-permute-start(f32[128,384]{1,0:T(8,128)S(1)} %slice_add_fusion.2), channel_id=1, source_target_pairs={{0,14},{2,0},{4,2},{6,4},{8,6},{10,8},{12,10},{14,12},{1,15},{3,1}... | collective-permute-start | bytes 589832 | tf_op jit(solution)/shard_map/ppermute | solution.py:54
  144.7 8.8 %collective-permute-start.6 = (f32[128,384]{1,0:T(8,128)S(1)}, f32[128,384]{1,0:T(8,128)S(1)}, u32[]{:S(2)}, u32[]{:S(2)}) collective-permute-start(f32[128,384]{1,0:T(8,128)S(1)} %slice_add_fusion.9), channel_id=1, source_target_pairs={{0,2},{2,4},{4,6},{6,8},{8,10},{10,12},{12,14},{14,0},{1,3},{3,5},... | collective-permute-start | bytes 589832 | tf_op jit(solution)/shard_map/ppermute | solution.py:53
  148.3 7.0 %collective-permute-start.14 = (f32[128,384]{1,0:T(8,128)S(1)}, f32[128,384]{1,0:T(8,128)S(1)}, u32[]{:S(2)}, u32[]{:S(2)}) collective-permute-start(f32[128,384]{1,0:T(8,128)S(1)} %slice_add_fusion.1), channel_id=1, source_target_pairs={{0,14},{2,0},{4,2},{6,4},{8,6},{10,8},{12,10},{14,12},{1,15},{3,1}... | collective-permute-start | bytes 589832 | tf_op jit(solution)/shard_map/ppermute | solution.py:54
  153.5 7.2 %collective-permute-start.7 = (f32[128,384]{1,0:T(8,128)S(1)}, f32[128,384]{1,0:T(8,128)S(1)}, u32[]{:S(2)}, u32[]{:S(2)}) collective-permute-start(f32[128,384]{1,0:T(8,128)S(1)} %slice_add_fusion.8), channel_id=1, source_target_pairs={{0,2},{2,4},{4,6},{6,8},{8,10},{10,12},{12,14},{14,0},{1,3},{3,5},... | collective-permute-start | bytes 589832 | tf_op jit(solution)/shard_map/ppermute | solution.py:53
  160.9 8.7 %collective-permute-start.18 = (f32[32,384]{1,0:T(8,128)S(1)}, f32[32,384]{1,0:T(8,128)S(1)}, u32[]{:S(2)}, u32[]{:S(2)}) collective-permute-start(f32[32,384]{1,0:T(8,128)S(1)} %slice.118), channel_id=1, source_target_pairs={{0,48},{16,0},{32,16},{48,32},{1,49},{17,1},{33,17},{49,33},{2,50}... | collective-permute-start | bytes 147464 | tf_op jit(solution)/shard_map/ppermute | solution.py:54
  169.6 5.7 %collective-permute-start.15 = (f32[32,384]{1,0:T(8,128)S(1)}, f32[32,384]{1,0:T(8,128)S(1)}, u32[]{:S(2)}, u32[]{:S(2)}) collective-permute-start(f32[32,384]{1,0:T(8,128)S(1)} %slice.114), channel_id=1, source_target_pairs={{0,16},{16,32},{32,48},{48,0},{1,17},{17,33},{33,49},{49,1},{2,18}... | collective-permute-start | bytes 147464 | tf_op jit(solution)/shard_map/ppermute | solution.py:53
  169.6 5.8 %collective-permute-start.19 = (f32[32,384]{1,0:T(8,128)S(1)}, f32[32,384]{1,0:T(8,128)S(1)}, u32[]{:S(2)}, u32[]{:S(2)}) collective-permute-start(f32[32,384]{1,0:T(8,128)S(1)} %slice_add_fusion.16), channel_id=1, source_target_pairs={{0,48},{16,0},{32,16},{48,32},{1,49},{17,1},{33,17},{49,33},{2,50}... | collective-permute-start | bytes 147464 | tf_op jit(solution)/shard_map/ppermute | solution.py:54
  175.3 5.4 %collective-permute-start.16 = (f32[32,384]{1,0:T(8,128)S(1)}, f32[32,384]{1,0:T(8,128)S(1)}, u32[]{:S(2)}, u32[]{:S(2)}) collective-permute-start(f32[32,384]{1,0:T(8,128)S(1)} %slice_add_fusion.19), channel_id=1, source_target_pairs={{0,16},{16,32},{32,48},{48,0},{1,17},{17,33},{33,49},{49,1},{2,18}... | collective-permute-start | bytes 147464 | tf_op jit(solution)/shard_map/ppermute | solution.py:53
  175.4 5.4 %collective-permute-start.20 = (f32[32,384]{1,0:T(8,128)S(1)}, f32[32,384]{1,0:T(8,128)S(1)}, u32[]{:S(2)}, u32[]{:S(2)}) collective-permute-start(f32[32,384]{1,0:T(8,128)S(1)} %slice_add_fusion.15), channel_id=1, source_target_pairs={{0,48},{16,0},{32,16},{48,32},{1,49},{17,1},{33,17},{49,33},{2,50}... | collective-permute-start | bytes 147464 | tf_op jit(solution)/shard_map/ppermute | solution.py:54
  180.7 5.4 %collective-permute-start.17 = (f32[32,384]{1,0:T(8,128)S(1)}, f32[32,384]{1,0:T(8,128)S(1)}, u32[]{:S(2)}, u32[]{:S(2)}) collective-permute-start(f32[32,384]{1,0:T(8,128)S(1)} %slice_add_fusion.18), channel_id=1, source_target_pairs={{0,16},{16,32},{32,48},{48,0},{1,17},{17,33},{33,49},{49,1},{2,18}... | collective-permute-start | bytes 147464 | tf_op jit(solution)/shard_map/ppermute | solution.py:53
  (6 other events, 93.6 us)
Sparse Core Ops, SparseCore 0:
  10.3 30.2 all-gather.1
  102.4 28.5 reduce-scatter.1

commit v4 on v3

--- a/solution.py
+++ b/solution.py
@@ -55,6 +55,22 @@
     return jnp.concatenate([a, b], axis=1)
 
 
+def direct_scatter(value, axis):
+    n = lax.axis_size(axis)
+    idx = lax.axis_index(axis)
+    rows = value.shape[0] // n
+    chunks = value.reshape(n, rows, value.shape[1])
+
+    def take(j):
+        return lax.dynamic_index_in_dim(chunks, j % n, 0, keepdims=False)
+
+    total = take(idx)
+    for shift in range(1, n):
+        perm = [(i, (i + shift) % n) for i in range(n)]
+        total = total + lax.ppermute(take(idx + shift), axis, perm)
+    return total
+
+
 def per_device(tokens, block_values, column_blocks, counts, cotangent):
     local_rows, features = tokens.shape
     width = cotangent.shape[1]
@@ -84,7 +100,7 @@
     )
     staged = ring_scatter(staged, "core")
     staged = ring_scatter(staged, "z")
-    weight_grad = ring_scatter(staged, "y")
+    weight_grad = direct_scatter(staged, "y")
     input_grad = lax.dot_general(
         cotangent_all, weight, (((1,), (1,)), ((), ())), preferred_element_type=jnp.float32
     ).astype(jnp.bfloat16)

time: 194 us -> 180 us (0.928)
  waiting for transfers between devices: 44.1 us -> 34.4 us
  starting transfers between devices: 39.6 us -> 34.5 us
    ppermute x10 -> x7, waiting for transfers between devices: 19.2 us -> 9.48 us  [ring_scatter(): a = lax.ppermute(a, axis, fwd) + take(idx - s - 2)[:, :half]]
    ppermute x10 -> x7, starting transfers between devices: 38.3 us -> 28.6 us  [ring_scatter(): b = lax.ppermute(b, axis, bwd) + take(idx + s + 2)[:, half:]]
    ppermute x0 -> x3, starting transfers between devices: none -> 4.67 us  [direct_scatter(): total = total + lax.ppermute(take(idx + shift), axis, perm)]
    ppermute x10 -> x7, waiting for transfers between devices: 19.3 us -> 19.4 us  [ring_scatter(): b = lax.ppermute(b, axis, bwd) + take(idx + s + 2)[:, half:]]
  transfers between devices with their start and end apart: 23 -> 20, of which waited for: 15 -> 12; matrix products, arithmetic and copies ran while one was open for 27% -> 29% of each run, Pallas kernels for 0% -> 0%
where the time goes in v4:
time: 180 us; the launch traced here: 179 us
  local copies, waits for them, and re-layouts  51.5 us (29%)
  starting transfers between devices  34.5 us (19%)
  waiting for transfers between devices  34.4 us (19%)
  matrix products  32.6 us (18%)
  between operations  14.6 us (8%)
  other arithmetic  11.3 us (6%)
    ppermute x7, starting transfers between devices, ring_scatter(): b = lax.ppermute(b, axis, bwd) + take(idx + s + 2)[:, half:]  28.6 us
    ppermute x7, waiting for transfers between devices, ring_scatter(): b = lax.ppermute(b, axis, bwd) + take(idx + s + 2)[:, half:]  19.4 us
    gather x1, local copies, waits for them, and re-layouts, slot_grad(): picked = jnp.take(cot_rows, column_blocks, axis=0, mode='clip')  14.3 us
    dot_general x1, matrix products, slot_grad(): lax.dot_general(tok_rows, picked, (((2,), (2,)), ((0,), (0,))), preferred...  14 us
    reshape x1, local copies, waits for them, and re-layouts, per_device(): weight = jnp.einsum('bkc,bikj->bicj', onehot, blocks_view, preferred_elem...  12.1 us
    reshape x1, local copies, waits for them, and re-layouts, per_device(): blocks_view = block_values.reshape(row_blocks, block, slots, block)  10.6 us
    ppermute x7, waiting for transfers between devices, ring_scatter(): a = lax.ppermute(a, axis, fwd) + take(idx - s - 2)[:, :half]  9.48 us
    dot_general x1, matrix products, per_device(): jnp.einsum('bkc,bikj->bicj', onehot, blocks_view, preferred_element_type=...  8.97 us
  transfers between devices with their start and end apart: 20, of which 12 were waited for; matrix products, arithmetic and copies ran while one was open for 29% of the time, Pallas kernels for 0%

profile of v4, /device:TPU:2, one launch (start us, length us, event | category | flops | bytes accessed | tf_op | source)
XLA Modules:
  0.0 178.9 jit_solution(15395052481290198177)
XLA Ops:
  9.1 10.6 %reshape.78 = bf16[32,64,12,64]{3,2,1,0:T(8,128)(2,1)} reshape(bf16[2048,768]{1,0:T(8,128)(2,1)} %param.6) | data formatting | bytes 6291456 | tf_op jit(solution)/shard_map/reshape | solution.py:83
  20.0 9.0 %convert_bitcast_fusion = bf16[32,64,16,64]{3,2,1,0:T(8,128)(2,1)} fusion(bf16[32,64,12,64]{3,2,1,0:T(8,128)(2,1)} %reshape.78, s32[32,12]{1,0:T(8,128)S(1)} %copy.12, pred[32,12]{1,0:T(8,128)(4,1)S(1)} %iota_compare_fusion.1), kind=kOutput, calls=%fused_computation.1 | convolution fusion | flops 52441088 | bytes 7341952 | tf_op jit(solution)/shard_map/bkc,bikj->bicj/dot_general | solution.py:85
  29.0 12.1 %reshape.59 = bf16[2048,1024]{1,0:T(8,128)(2,1)} reshape(bf16[32,64,16,64]{3,2,1,0:T(8,128)(2,1)} %convert_bitcast_fusion) | data formatting | bytes 8388608 | tf_op jit(solution)/shard_map/reshape | solution.py:87
  43.8 5.9 %convolution_bitcast_fusion = f32[512,1024]{0,1:T(8,128)} fusion(bf16[2048,1024]{1,0:T(8,128)(2,1)} %reshape.59, bf16[512,2048]{1,0:T(8,128)(2,1)S(1)} %copy-done.3), kind=kOutput, calls=%fused_computation.6 | convolution fusion | flops 2147483648 | bytes 8388608 | tf_op jit(solution)/shard_map/dot_general | solution.py:89
  49.8 14.3 %gather_fusion = bf16[384,64,512]{2,1,0:T(8,128)(2,1)} fusion(bf16[16,64,512]{2,1,0:T(8,128)(2,1)} %bitcast.81, s32[1024]{0:T(1024)S(1)} %pad_clamp_fusion), kind=kCustom, calls=%fused_computation | custom fusion | bytes 50333184 | tf_op jit(solution)/shard_map/jit(_take)/gather | solution.py:23
  64.1 14.0 %multiply_select_fusion = f32[32,768,64]{1,2,0:T(8,128)} fusion(pred[32,768]{1,0:T(8,128)(4,1)S(1)} %broadcast_in_dim.28, bf16[32,768,512]{2,1,0:T(8,128)(2,1)} %bitcast.83, bf16[32,64,512]{2,1,0:T(8,128)(2,1)S(1)} %bitcast.87), kind=kOutput, calls=%fused_computation.2 | convolution fusion | flops 1613758464 | bytes 33579008 | tf_op jit(solution)/shard_map/dot_general | solution.py:26
  78.1 3.5 %copy.18 = f32[4,8,2,32,768]{4,3,0,1,2:T(8,128)S(1)} copy(f32[4,8,2,32,768]{4,3,2,1,0:T(8,128)} %bitcast.86) | data formatting | bytes 12582912 | tf_op jit(solution)/shard_map/reshape | solution.py:97
  81.7 2.6 %copy-done.1 = f32[4,8,2,32,768]{4,3,0,1,2:T(8,128)} copy-done((f32[4,8,2,32,768]{4,3,0,1,2:T(8,128)}, f32[4,8,2,32,768]{4,3,0,1,2:T(8,128)S(1)}, u32[]{:S(2)}) %copy-start.1) | copy-done | bytes 6291480
  85.1 5.5 %collective-permute-done = f32[1024,768]{1,0:T(8,128)} collective-permute-done((f32[1024,768]{1,0:T(8,128)S(1)}, f32[1024,768]{1,0:T(8,128)}, u32[]{:S(2)}, u32[]{:S(2)}) %collective-permute-start) | collective-permute-done | bytes 3145760 | tf_op jit(solution)/shard_map/ppermute | solution.py:46
  90.6 3.2 %bitcast_add_fusion = f32[1024,768]{1,0:T(8,128)S(1)} fusion(f32[1024,768]{1,0:T(8,128)} %collective-permute-done, f32[2,1024,768]{2,1,0:T(8,128)} %bitcast.85, s32[]{:T(128)S(6)} %select_n.170), kind=kLoop, calls=%fused_computation.3 | loop fusion | flops 786432 | bytes 9437188 | tf_op jit(solution)/shard_map/add | solution.py:46
  96.3 6.0 %collective-permute-start.8 = (f32[128,384]{1,0:T(8,128)}, f32[128,384]{1,0:T(8,128)}, u32[]{:S(2)}, u32[]{:S(2)}) collective-permute-start(f32[128,384]{1,0:T(8,128)} %slice.74), channel_id=1, source_target_pairs={{0,14},{2,0},{4,2},{6,4},{8,6},{10,8},{12,10},{14,12},{1,15},{3,1}... | collective-permute-start | bytes 589832 | tf_op jit(solution)/shard_map/ppermute | solution.py:54
  102.5 4.6 %collective-permute-done.8 = f32[128,384]{1,0:T(8,128)} collective-permute-done((f32[128,384]{1,0:T(8,128)}, f32[128,384]{1,0:T(8,128)}, u32[]{:S(2)}, u32[]{:S(2)}) %collective-permute-start.8) | collective-permute-done | bytes 196640 | tf_op jit(solution)/shard_map/ppermute | solution.py:54
  108.1 3.8 %collective-permute-start.9 = (f32[128,384]{1,0:T(8,128)S(1)}, f32[128,384]{1,0:T(8,128)S(1)}, u32[]{:S(2)}, u32[]{:S(2)}) collective-permute-start(f32[128,384]{1,0:T(8,128)S(1)} %slice_add_fusion.6), channel_id=1, source_target_pairs={{0,14},{2,0},{4,2},{6,4},{8,6},{10,8},{12,10},{14,12},{1,15},{3,1}... | collective-permute-start | bytes 589832 | tf_op jit(solution)/shard_map/ppermute | solution.py:54
  112.9 2.6 %collective-permute-done.9 = f32[128,384]{1,0:T(8,128)S(1)} collective-permute-done((f32[128,384]{1,0:T(8,128)S(1)}, f32[128,384]{1,0:T(8,128)S(1)}, u32[]{:S(2)}, u32[]{:S(2)}) %collective-permute-start.9) | collective-permute-done | bytes 196640 | tf_op jit(solution)/shard_map/ppermute | solution.py:54
  116.6 3.8 %collective-permute-start.10 = (f32[128,384]{1,0:T(8,128)S(1)}, f32[128,384]{1,0:T(8,128)S(1)}, u32[]{:S(2)}, u32[]{:S(2)}) collective-permute-start(f32[128,384]{1,0:T(8,128)S(1)} %slice_add_fusion.5), channel_id=1, source_target_pairs={{0,14},{2,0},{4,2},{6,4},{8,6},{10,8},{12,10},{14,12},{1,15},{3,1}... | collective-permute-start | bytes 589832 | tf_op jit(solution)/shard_map/ppermute | solution.py:54
  124.5 3.8 %collective-permute-start.11 = (f32[128,384]{1,0:T(8,128)S(1)}, f32[128,384]{1,0:T(8,128)S(1)}, u32[]{:S(2)}, u32[]{:S(2)}) collective-permute-start(f32[128,384]{1,0:T(8,128)S(1)} %slice_add_fusion.4), channel_id=1, source_target_pairs={{0,14},{2,0},{4,2},{6,4},{8,6},{10,8},{12,10},{14,12},{1,15},{3,1}... | collective-permute-start | bytes 589832 | tf_op jit(solution)/shard_map/ppermute | solution.py:54
  131.5 3.8 %collective-permute-start.12 = (f32[128,384]{1,0:T(8,128)S(1)}, f32[128,384]{1,0:T(8,128)S(1)}, u32[]{:S(2)}, u32[]{:S(2)}) collective-permute-start(f32[128,384]{1,0:T(8,128)S(1)} %slice_add_fusion.3), channel_id=1, source_target_pairs={{0,14},{2,0},{4,2},{6,4},{8,6},{10,8},{12,10},{14,12},{1,15},{3,1}... | collective-permute-start | bytes 589832 | tf_op jit(solution)/shard_map/ppermute | solution.py:54
  136.6 3.0 %collective-permute-done.12 = f32[128,384]{1,0:T(8,128)S(1)} collective-permute-done((f32[128,384]{1,0:T(8,128)S(1)}, f32[128,384]{1,0:T(8,128)S(1)}, u32[]{:S(2)}, u32[]{:S(2)}) %collective-permute-start.12) | collective-permute-done | bytes 196640 | tf_op jit(solution)/shard_map/ppermute | solution.py:54
  139.6 3.8 %collective-permute-start.13 = (f32[128,384]{1,0:T(8,128)S(1)}, f32[128,384]{1,0:T(8,128)S(1)}, u32[]{:S(2)}, u32[]{:S(2)}) collective-permute-start(f32[128,384]{1,0:T(8,128)S(1)} %slice_add_fusion.2), channel_id=1, source_target_pairs={{0,14},{2,0},{4,2},{6,4},{8,6},{10,8},{12,10},{14,12},{1,15},{3,1}... | collective-permute-start | bytes 589832 | tf_op jit(solution)/shard_map/ppermute | solution.py:54
  145.0 3.5 %collective-permute-done.13 = f32[128,384]{1,0:T(8,128)S(1)} collective-permute-done((f32[128,384]{1,0:T(8,128)S(1)}, f32[128,384]{1,0:T(8,128)S(1)}, u32[]{:S(2)}, u32[]{:S(2)}) %collective-permute-start.13) | collective-permute-done | bytes 196640 | tf_op jit(solution)/shard_map/ppermute | solution.py:54
  148.5 3.8 %collective-permute-start.14 = (f32[128,384]{1,0:T(8,128)S(1)}, f32[128,384]{1,0:T(8,128)S(1)}, u32[]{:S(2)}, u32[]{:S(2)}) collective-permute-start(f32[128,384]{1,0:T(8,128)S(1)} %slice_add_fusion.1), channel_id=1, source_target_pairs={{0,14},{2,0},{4,2},{6,4},{8,6},{10,8},{12,10},{14,12},{1,15},{3,1}... | collective-permute-start | bytes 589832 | tf_op jit(solution)/shard_map/ppermute | solution.py:54
  155.5 5.4 %collective-permute-done.7 = f32[128,384]{1,0:T(8,128)S(1)} collective-permute-done((f32[128,384]{1,0:T(8,128)S(1)}, f32[128,384]{1,0:T(8,128)S(1)}, u32[]{:S(2)}, u32[]{:S(2)}) %collective-permute-start.7) | collective-permute-done | bytes 196640 | tf_op jit(solution)/shard_map/ppermute | solution.py:53
  161.0 3.1 %collective-permute-start.17 = (f32[32,768]{1,0:T(8,128)S(1)}, f32[32,768]{1,0:T(8,128)S(1)}, u32[]{:S(2)}, u32[]{:S(2)}) collective-permute-start(f32[32,768]{1,0:T(8,128)S(1)} %get-tuple-element.30), channel_id=1, source_target_pairs={{0,48},{16,0},{32,16},{48,32},{1,49},{17,1},{33,17},{49,33},{2,50}... | collective-permute-start | bytes 294920 | tf_op jit(solution)/shard_map/ppermute | solution.py:70
  165.7 3.7 %convolution_convert_fusion = bf16[512,2048]{1,0:T(8,128)(2,1)} fusion(bf16[512,1024]{0,1:T(8,128)(2,1)S(1)} %copy-done, bf16[2048,1024]{1,0:T(8,128)(2,1)S(1)} %copy-done.2), kind=kOutput, calls=%fused_computation.5 | convolution fusion | flops 2148532224 | bytes 7340032 | tf_op jit(solution)/shard_map/dot_general | solution.py:104
  (72 shorter events, 29.0 us)
Async XLA Ops:
  7.2 42.6 %all-gather.2.cloned.1.call-start = ((), (), s32[]{:S(2)}) async-start(), calls=%async_computation.1 | async-start | bytes 1310720 | tf_op jit(solution)/shard_map/all_gather | solution.py:90
  9.0 160.4 %reduce-scatter.2.cloned.1.call-start = ((), (), s32[]{:S(2)}) async-start(), calls=%async_computation.2 | async-start | bytes 2621440 | tf_op jit(solution)/shard_map/reduce_scatter | solution.py:92
  29.0 12.3 %copy-start.3 = (bf16[512,2048]{1,0:T(8,128)(2,1)S(1)}, bf16[512,2048]{1,0:T(8,128)(2,1)}, u32[]{:S(2)}) copy-start(bf16[512,2048]{1,0:T(8,128)(2,1)} %param.5) | copy-start | bytes 6291460
  49.8 14.3 %copy-start.4 = (bf16[512,2048]{0,1:T(8,128)(2,1)S(1)}, bf16[512,2048]{0,1:T(8,128)(2,1)}, u32[]{:S(2)}) copy-start(bf16[512,2048]{0,1:T(8,128)(2,1)} %copy.17) | copy-start | bytes 6291460
  84.5 6.1 %collective-permute-start = (f32[1024,768]{1,0:T(8,128)S(1)}, f32[1024,768]{1,0:T(8,128)}, u32[]{:S(2)}, u32[]{:S(2)}) collective-permute-start(f32[1024,768]{1,0:T(8,128)S(1)} %dynamic-slice_bitcast_fusion), channel_id=1, source_target_pairs={{0,1},{1,0},{2,3},{3,2},{4,5},{5,4},{6,7},{7,6},{8,9},{9,8},{10,11... | collective-permute-start | bytes 9437192 | tf_op jit(solution)/shard_map/ppermute | solution.py:46
  96.3 10.8 %collective-permute-start.8 = (f32[128,384]{1,0:T(8,128)}, f32[128,384]{1,0:T(8,128)}, u32[]{:S(2)}, u32[]{:S(2)}) collective-permute-start(f32[128,384]{1,0:T(8,128)} %slice.74), channel_id=1, source_target_pairs={{0,14},{2,0},{4,2},{6,4},{8,6},{10,8},{12,10},{14,12},{1,15},{3,1}... | collective-permute-start | bytes 589832 | tf_op jit(solution)/shard_map/ppermute | solution.py:54
  102.4 9.5 %collective-permute-start.1 = (f32[128,384]{1,0:T(8,128)S(1)}, f32[128,384]{1,0:T(8,128)S(1)}, u32[]{:S(2)}, u32[]{:S(2)}) collective-permute-start(f32[128,384]{1,0:T(8,128)S(1)} %slice.66), channel_id=1, source_target_pairs={{0,2},{2,4},{4,6},{6,8},{8,10},{10,12},{12,14},{14,0},{1,3},{3,5},... | collective-permute-start | bytes 589832 | tf_op jit(solution)/shard_map/ppermute | solution.py:53
  108.1 7.4 %collective-permute-start.9 = (f32[128,384]{1,0:T(8,128)S(1)}, f32[128,384]{1,0:T(8,128)S(1)}, u32[]{:S(2)}, u32[]{:S(2)}) collective-permute-start(f32[128,384]{1,0:T(8,128)S(1)} %slice_add_fusion.6), channel_id=1, source_target_pairs={{0,14},{2,0},{4,2},{6,4},{8,6},{10,8},{12,10},{14,12},{1,15},{3,1}... | collective-permute-start | bytes 589832 | tf_op jit(solution)/shard_map/ppermute | solution.py:54
  112.8 7.5 %collective-permute-start.2 = (f32[128,384]{1,0:T(8,128)S(1)}, f32[128,384]{1,0:T(8,128)S(1)}, u32[]{:S(2)}, u32[]{:S(2)}) collective-permute-start(f32[128,384]{1,0:T(8,128)S(1)} %slice_add_fusion.13), channel_id=1, source_target_pairs={{0,2},{2,4},{4,6},{6,8},{8,10},{10,12},{12,14},{14,0},{1,3},{3,5},... | collective-permute-start | bytes 589832 | tf_op jit(solution)/shard_map/ppermute | solution.py:53
  115.5 50.2 %copy-start = (bf16[512,1024]{0,1:T(8,128)(2,1)S(1)}, bf16[512,1024]{0,1:T(8,128)(2,1)}, u32[]{:S(2)}) copy-start(bf16[512,1024]{0,1:T(8,128)(2,1)} %all-gather.2.cloned.1.call-done) | copy-start | bytes 3145732
  115.5 50.2 %copy-start.2 = (bf16[2048,1024]{1,0:T(8,128)(2,1)S(1)}, bf16[2048,1024]{1,0:T(8,128)(2,1)}, u32[]{:S(2)}) copy-start(bf16[2048,1024]{1,0:T(8,128)(2,1)} %reshape.59) | copy-start | bytes 12582916
  116.6 7.0 %collective-permute-start.10 = (f32[128,384]{1,0:T(8,128)S(1)}, f32[128,384]{1,0:T(8,128)S(1)}, u32[]{:S(2)}, u32[]{:S(2)}) collective-permute-start(f32[128,384]{1,0:T(8,128)S(1)} %slice_add_fusion.5), channel_id=1, source_target_pairs={{0,14},{2,0},{4,2},{6,4},{8,6},{10,8},{12,10},{14,12},{1,15},{3,1}... | collective-permute-start | bytes 589832 | tf_op jit(solution)/shard_map/ppermute | solution.py:54
  121.3 7.0 %collective-permute-start.3 = (f32[128,384]{1,0:T(8,128)S(1)}, f32[128,384]{1,0:T(8,128)S(1)}, u32[]{:S(2)}, u32[]{:S(2)}) collective-permute-start(f32[128,384]{1,0:T(8,128)S(1)} %slice_add_fusion.12), channel_id=1, source_target_pairs={{0,2},{2,4},{4,6},{6,8},{8,10},{10,12},{12,14},{14,0},{1,3},{3,5},... | collective-permute-start | bytes 589832 | tf_op jit(solution)/shard_map/ppermute | solution.py:53
  124.5 7.0 %collective-permute-start.11 = (f32[128,384]{1,0:T(8,128)S(1)}, f32[128,384]{1,0:T(8,128)S(1)}, u32[]{:S(2)}, u32[]{:S(2)}) collective-permute-start(f32[128,384]{1,0:T(8,128)S(1)} %slice_add_fusion.4), channel_id=1, source_target_pairs={{0,14},{2,0},{4,2},{6,4},{8,6},{10,8},{12,10},{14,12},{1,15},{3,1}... | collective-permute-start | bytes 589832 | tf_op jit(solution)/shard_map/ppermute | solution.py:54
  129.2 7.2 %collective-permute-start.4 = (f32[128,384]{1,0:T(8,128)S(1)}, f32[128,384]{1,0:T(8,128)S(1)}, u32[]{:S(2)}, u32[]{:S(2)}) collective-permute-start(f32[128,384]{1,0:T(8,128)S(1)} %slice_add_fusion.11), channel_id=1, source_target_pairs={{0,2},{2,4},{4,6},{6,8},{8,10},{10,12},{12,14},{14,0},{1,3},{3,5},... | collective-permute-start | bytes 589832 | tf_op jit(solution)/shard_map/ppermute | solution.py:53
  131.5 8.1 %collective-permute-start.12 = (f32[128,384]{1,0:T(8,128)S(1)}, f32[128,384]{1,0:T(8,128)S(1)}, u32[]{:S(2)}, u32[]{:S(2)}) collective-permute-start(f32[128,384]{1,0:T(8,128)S(1)} %slice_add_fusion.3), channel_id=1, source_target_pairs={{0,14},{2,0},{4,2},{6,4},{8,6},{10,8},{12,10},{14,12},{1,15},{3,1}... | collective-permute-start | bytes 589832 | tf_op jit(solution)/shard_map/ppermute | solution.py:54
  136.5 8.4 %collective-permute-start.5 = (f32[128,384]{1,0:T(8,128)S(1)}, f32[128,384]{1,0:T(8,128)S(1)}, u32[]{:S(2)}, u32[]{:S(2)}) collective-permute-start(f32[128,384]{1,0:T(8,128)S(1)} %slice_add_fusion.10), channel_id=1, source_target_pairs={{0,2},{2,4},{4,6},{6,8},{8,10},{10,12},{12,14},{14,0},{1,3},{3,5},... | collective-permute-start | bytes 589832 | tf_op jit(solution)/shard_map/ppermute | solution.py:53
  139.6 8.9 %collective-permute-start.13 = (f32[128,384]{1,0:T(8,128)S(1)}, f32[128,384]{1,0:T(8,128)S(1)}, u32[]{:S(2)}, u32[]{:S(2)}) collective-permute-start(f32[128,384]{1,0:T(8,128)S(1)} %slice_add_fusion.2), channel_id=1, source_target_pairs={{0,14},{2,0},{4,2},{6,4},{8,6},{10,8},{12,10},{14,12},{1,15},{3,1}... | collective-permute-start | bytes 589832 | tf_op jit(solution)/shard_map/ppermute | solution.py:54
  144.9 8.8 %collective-permute-start.6 = (f32[128,384]{1,0:T(8,128)S(1)}, f32[128,384]{1,0:T(8,128)S(1)}, u32[]{:S(2)}, u32[]{:S(2)}) collective-permute-start(f32[128,384]{1,0:T(8,128)S(1)} %slice_add_fusion.9), channel_id=1, source_target_pairs={{0,2},{2,4},{4,6},{6,8},{8,10},{10,12},{12,14},{14,0},{1,3},{3,5},... | collective-permute-start | bytes 589832 | tf_op jit(solution)/shard_map/ppermute | solution.py:53
  148.5 7.0 %collective-permute-start.14 = (f32[128,384]{1,0:T(8,128)S(1)}, f32[128,384]{1,0:T(8,128)S(1)}, u32[]{:S(2)}, u32[]{:S(2)}) collective-permute-start(f32[128,384]{1,0:T(8,128)S(1)} %slice_add_fusion.1), channel_id=1, source_target_pairs={{0,14},{2,0},{4,2},{6,4},{8,6},{10,8},{12,10},{14,12},{1,15},{3,1}... | collective-permute-start | bytes 589832 | tf_op jit(solution)/shard_map/ppermute | solution.py:54
  153.8 7.2 %collective-permute-start.7 = (f32[128,384]{1,0:T(8,128)S(1)}, f32[128,384]{1,0:T(8,128)S(1)}, u32[]{:S(2)}, u32[]{:S(2)}) collective-permute-start(f32[128,384]{1,0:T(8,128)S(1)} %slice_add_fusion.8), channel_id=1, source_target_pairs={{0,2},{2,4},{4,6},{6,8},{8,10},{10,12},{12,14},{14,0},{1,3},{3,5},... | collective-permute-start | bytes 589832 | tf_op jit(solution)/shard_map/ppermute | solution.py:53
  161.0 10.3 %collective-permute-start.17 = (f32[32,768]{1,0:T(8,128)S(1)}, f32[32,768]{1,0:T(8,128)S(1)}, u32[]{:S(2)}, u32[]{:S(2)}) collective-permute-start(f32[32,768]{1,0:T(8,128)S(1)} %get-tuple-element.30), channel_id=1, source_target_pairs={{0,48},{16,0},{32,16},{48,32},{1,49},{17,1},{33,17},{49,33},{2,50}... | collective-permute-start | bytes 294920 | tf_op jit(solution)/shard_map/ppermute | solution.py:70
  164.1 7.3 %collective-permute-start.16 = (f32[32,768]{1,0:T(8,128)S(1)}, f32[32,768]{1,0:T(8,128)S(1)}, u32[]{:S(2)}, u32[]{:S(2)}) collective-permute-start(f32[32,768]{1,0:T(8,128)S(1)} %get-tuple-element.31), channel_id=1, source_target_pairs={{0,32},{16,48},{32,0},{48,16},{1,33},{17,49},{33,1},{49,17},{2,34}... | collective-permute-start | bytes 294920 | tf_op jit(solution)/shard_map/ppermute | solution.py:70
  164.7 6.6 %collective-permute-start.15 = (f32[32,768]{1,0:T(8,128)S(1)}, f32[32,768]{1,0:T(8,128)S(1)}, u32[]{:S(2)}, u32[]{:S(2)}) collective-permute-start(f32[32,768]{1,0:T(8,128)S(1)} %get-tuple-element.29), channel_id=1, source_target_pairs={{0,16},{16,32},{32,48},{48,0},{1,17},{17,33},{33,49},{49,1},{2,18}... | collective-permute-start | bytes 294920 | tf_op jit(solution)/shard_map/ppermute | solution.py:70
  (3 other events, 24.1 us)
Sparse Core Ops, SparseCore 0:
  10.3 30.2 all-gather.1
  102.4 28.5 reduce-scatter.1

commit v5 on v4

--- a/solution.py
+++ b/solution.py
@@ -71,6 +71,32 @@
     return total
 
 
+def meeting_scatter(value, axis):
+    n = lax.axis_size(axis)
+    idx = lax.axis_index(axis)
+    rows = value.shape[0] // n
+    chunks = value.reshape(n, rows, value.shape[1])
+
+    def take(j):
+        return lax.dynamic_index_in_dim(chunks, j % n, 0, keepdims=False)
+
+    ahead = n // 2
+    behind = n - 1 - ahead
+    fwd = [(i, (i + 1) % n) for i in range(n)]
+    bwd = [(i, (i - 1) % n) for i in range(n)]
+    a = take(idx + ahead)
+    for s in range(1, ahead + 1):
+        a = lax.ppermute(a, axis, fwd) + take(idx + ahead - s)
+    if behind == 0:
+        return a
+    b = take(idx - behind)
+    for s in range(1, behind + 1):
+        b = lax.ppermute(b, axis, bwd)
+        if s < behind:
+            b = b + take(idx - behind + s)
+    return a + b
+
+
 def per_device(tokens, block_values, column_blocks, counts, cotangent):
     local_rows, features = tokens.shape
     width = cotangent.shape[1]
@@ -99,7 +125,7 @@
         .reshape(features, slots * block)
     )
     staged = ring_scatter(staged, "core")
-    staged = ring_scatter(staged, "z")
+    staged = meeting_scatter(staged, "z")
     weight_grad = direct_scatter(staged, "y")
     input_grad = lax.dot_general(
         cotangent_all, weight, (((1,), (1,)), ((), ())), preferred_element_type=jnp.float32

time: 180 us -> 174 us (0.967)
  starting transfers between devices: 34.5 us -> 17.4 us
  waiting for transfers between devices: 34.4 us -> 44.2 us
  matrix products: 32.6 us -> 34.9 us
    ppermute x14 -> x7, starting transfers between devices: 29.4 us -> 12.6 us  [the longest x3 10.5 us: meeting_scatter(): b = lax.ppermute(b, axis, bwd)]
    ppermute x14 -> x7, waiting for transfers between devices: 28.9 us -> 38.3 us  [the longest x4 32.2 us: meeting_scatter(): a = lax.ppermute(a, axis, fwd) + take(idx + ahead - s)]
    dot_general x1, matrix products: 3.71 us -> 5.89 us  [per_device(): lax.dot_general(cotangent_all, weight, (((1,), (1,)), ((), ())), preferre...]
    add x14 -> x4, other arithmetic: 6.21 us -> 4.49 us  [the longest x3 3.44 us: meeting_scatter(): a = lax.ppermute(a, axis, fwd) + take(idx + ahead - s)]
  transfers between devices with their start and end apart: 20 -> 13, of which waited for: 12 -> 6; matrix products, arithmetic and copies ran while one was open for 29% -> 33% of each run, Pallas kernels for 0% -> 0%
where the time goes in v5:
time: 174 us; the launch traced here: 173 us
  local copies, waits for them, and re-layouts  52.3 us (30%)
  waiting for transfers between devices  44.2 us (25%)
  matrix products  34.9 us (20%)
  starting transfers between devices  17.4 us (10%)
  between operations  14.3 us (8%)
  other arithmetic  9.54 us (5%)
    ppermute x4, waiting for transfers between devices, meeting_scatter(): a = lax.ppermute(a, axis, fwd) + take(idx + ahead - s)  32.2 us
    gather x1, local copies, waits for them, and re-layouts, slot_grad(): picked = jnp.take(cot_rows, column_blocks, axis=0, mode='clip')  14.3 us
    dot_general x1, matrix products, slot_grad(): lax.dot_general(tok_rows, picked, (((2,), (2,)), ((0,), (0,))), preferred...  14.1 us
    reshape x1, local copies, waits for them, and re-layouts, per_device(): weight = jnp.einsum('bkc,bikj->bicj', onehot, blocks_view, preferred_elem...  12 us
    reshape x1, local copies, waits for them, and re-layouts, per_device(): blocks_view = block_values.reshape(row_blocks, block, slots, block)  10.6 us
    ppermute x3, starting transfers between devices, meeting_scatter(): b = lax.ppermute(b, axis, bwd)  10.5 us
    unnamed x18, local copies, waits for them, and re-layouts  9.53 us
    dot_general x1, matrix products, per_device(): jnp.einsum('bkc,bikj->bicj', onehot, blocks_view, preferred_element_type=...  8.96 us
  transfers between devices with their start and end apart: 13, of which 6 were waited for; matrix products, arithmetic and copies ran while one was open for 33% of the time, Pallas kernels for 0%

profile of v5, /device:TPU:2, one launch (start us, length us, event | category | flops | bytes accessed | tf_op | source)
XLA Modules:
  0.0 172.7 jit_solution(6483046358435187266)
XLA Ops:
  7.2 1.8 %copy.15 = bf16[128,1024]{0,1:T(8,128)(2,1)} copy(bf16[128,1024]{1,0:T(8,128)(2,1)} %param.9) | data formatting | bytes 524288 | tf_op args[4]
  9.1 10.6 %reshape.78 = bf16[32,64,12,64]{3,2,1,0:T(8,128)(2,1)} reshape(bf16[2048,768]{1,0:T(8,128)(2,1)} %param.6) | data formatting | bytes 6291456 | tf_op jit(solution)/shard_map/reshape | solution.py:109
  20.0 9.0 %convert_bitcast_fusion = bf16[32,64,16,64]{3,2,1,0:T(8,128)(2,1)} fusion(bf16[32,64,12,64]{3,2,1,0:T(8,128)(2,1)} %reshape.78, s32[32,12]{1,0:T(8,128)S(1)} %copy.12, pred[32,12]{1,0:T(8,128)(4,1)S(1)} %iota_compare_fusion.1), kind=kOutput, calls=%fused_computation.1 | convolution fusion | flops 52441088 | bytes 7341952 | tf_op jit(solution)/shard_map/bkc,bikj->bicj/dot_general | solution.py:111
  29.0 12.0 %reshape.59 = bf16[2048,1024]{1,0:T(8,128)(2,1)} reshape(bf16[32,64,16,64]{3,2,1,0:T(8,128)(2,1)} %convert_bitcast_fusion) | data formatting | bytes 8388608 | tf_op jit(solution)/shard_map/reshape | solution.py:113
  41.3 2.5 %copy.17 = bf16[512,2048]{0,1:T(8,128)(2,1)} copy(bf16[512,2048]{1,0:T(8,128)(2,1)S(1)} %copy-done.3) | data formatting | bytes 4194304 | tf_op args[0]
  43.8 6.0 %convolution_bitcast_fusion = f32[512,1024]{0,1:T(8,128)} fusion(bf16[2048,1024]{1,0:T(8,128)(2,1)} %reshape.59, bf16[512,2048]{1,0:T(8,128)(2,1)S(1)} %copy-done.3), kind=kOutput, calls=%fused_computation.6 | convolution fusion | flops 2147483648 | bytes 8388608 | tf_op jit(solution)/shard_map/dot_general | solution.py:115
  49.8 14.3 %gather_fusion = bf16[384,64,512]{2,1,0:T(8,128)(2,1)} fusion(bf16[16,64,512]{2,1,0:T(8,128)(2,1)} %bitcast.67, s32[1024]{0:T(1024)S(1)} %pad_clamp_fusion), kind=kCustom, calls=%fused_computation | custom fusion | bytes 50333184 | tf_op jit(solution)/shard_map/jit(_take)/gather | solution.py:23
  64.1 14.1 %multiply_select_fusion = f32[32,768,64]{1,2,0:T(8,128)} fusion(pred[32,768]{1,0:T(8,128)(4,1)S(1)} %broadcast_in_dim.28, bf16[32,768,512]{2,1,0:T(8,128)(2,1)} %bitcast.68, bf16[32,64,512]{2,1,0:T(8,128)(2,1)S(1)} %bitcast.77), kind=kOutput, calls=%fused_computation.2 | convolution fusion | flops 1613758464 | bytes 33579008 | tf_op jit(solution)/shard_map/dot_general | solution.py:26
  78.1 3.5 %copy.18 = f32[4,8,2,32,768]{4,3,0,1,2:T(8,128)S(1)} copy(f32[4,8,2,32,768]{4,3,2,1,0:T(8,128)} %bitcast.76) | data formatting | bytes 12582912 | tf_op jit(solution)/shard_map/reshape | solution.py:123
  81.7 2.7 %copy-done.1 = f32[4,8,2,32,768]{4,3,0,1,2:T(8,128)} copy-done((f32[4,8,2,32,768]{4,3,0,1,2:T(8,128)}, f32[4,8,2,32,768]{4,3,0,1,2:T(8,128)S(1)}, u32[]{:S(2)}) %copy-start.1) | copy-done | bytes 6291480
  84.3 1.9 %dynamic-slice_bitcast_fusion = f32[1024,768]{1,0:T(8,128)} fusion(f32[2,1024,768]{2,1,0:T(8,128)S(1)} %bitcast.69, s32[]{:T(128)S(6)} %select_n.116), kind=kLoop, calls=%fused_computation.4 | loop fusion | bytes 6291460 | tf_op jit(solution)/shard_map/jit(dynamic_index_in_dim)/squeeze | solution.py:43
  86.3 5.9 %collective-permute-done = f32[1024,768]{1,0:T(8,128)} collective-permute-done((f32[1024,768]{1,0:T(8,128)}, f32[1024,768]{1,0:T(8,128)}, u32[]{:S(2)}, u32[]{:S(2)}) %collective-permute-start) | collective-permute-done | bytes 3145760 | tf_op jit(solution)/shard_map/ppermute | solution.py:46
  92.2 3.2 %bitcast_add_fusion = f32[1024,768]{1,0:T(8,128)S(1)} fusion(f32[1024,768]{1,0:T(8,128)} %collective-permute-done, f32[2,1024,768]{2,1,0:T(8,128)} %bitcast.70, s32[]{:T(128)S(6)} %select_n.114), kind=kLoop, calls=%fused_computation.3 | loop fusion | flops 786432 | bytes 9437188 | tf_op jit(solution)/shard_map/add | solution.py:46
  97.1 2.0 %collective-permute-start.1 = (f32[128,768]{1,0:T(8,128)S(1)}, f32[128,768]{1,0:T(8,128)S(1)}, u32[]{:S(2)}, u32[]{:S(2)}) collective-permute-start(f32[128,768]{1,0:T(8,128)S(1)} %get-tuple-element.17), channel_id=1, source_target_pairs={{0,2},{2,4},{4,6},{6,8},{8,10},{10,12},{12,14},{14,0},{1,3},{3,5},... | collective-permute-start | bytes 1179656 | tf_op jit(solution)/shard_map/ppermute | solution.py:89
  99.1 4.2 %collective-permute-start.5 = (f32[128,768]{1,0:T(8,128)S(1)}, f32[128,768]{1,0:T(8,128)S(1)}, u32[]{:S(2)}, u32[]{:S(2)}) collective-permute-start(f32[128,768]{1,0:T(8,128)S(1)} %get-tuple-element.18), channel_id=1, source_target_pairs={{0,14},{2,0},{4,2},{6,4},{8,6},{10,8},{12,10},{14,12},{1,15},{3,1}... | collective-permute-start | bytes 1179656 | tf_op jit(solution)/shard_map/ppermute | solution.py:94
  103.3 9.3 %collective-permute-done.1 = f32[128,768]{1,0:T(8,128)S(1)} collective-permute-done((f32[128,768]{1,0:T(8,128)S(1)}, f32[128,768]{1,0:T(8,128)S(1)}, u32[]{:S(2)}, u32[]{:S(2)}) %collective-permute-start.1) | collective-permute-done | bytes 393248 | tf_op jit(solution)/shard_map/ppermute | solution.py:89
  113.8 11.7 %collective-permute-done.2 = f32[128,768]{1,0:T(8,128)S(1)} collective-permute-done((f32[128,768]{1,0:T(8,128)S(1)}, f32[128,768]{1,0:T(8,128)S(1)}, u32[]{:S(2)}, u32[]{:S(2)}) %collective-permute-start.2) | collective-permute-done | bytes 393248 | tf_op jit(solution)/shard_map/ppermute | solution.py:89
  126.9 3.2 %collective-permute-start.6 = (f32[128,768]{1,0:T(8,128)S(1)}, f32[128,768]{1,0:T(8,128)S(1)}, u32[]{:S(2)}, u32[]{:S(2)}) collective-permute-start(f32[128,768]{1,0:T(8,128)S(1)} %get-tuple-element.16), channel_id=1, source_target_pairs={{0,14},{2,0},{4,2},{6,4},{8,6},{10,8},{12,10},{14,12},{1,15},{3,1}... | collective-permute-start | bytes 1179656 | tf_op jit(solution)/shard_map/ppermute | solution.py:94
  130.1 7.7 %collective-permute-done.3 = f32[128,768]{1,0:T(8,128)S(1)} collective-permute-done((f32[128,768]{1,0:T(8,128)S(1)}, f32[128,768]{1,0:T(8,128)S(1)}, u32[]{:S(2)}, u32[]{:S(2)}) %collective-permute-start.3) | collective-permute-done | bytes 393248 | tf_op jit(solution)/shard_map/ppermute | solution.py:89
  139.0 3.0 %collective-permute-start.7 = (f32[128,768]{1,0:T(8,128)S(1)}, f32[128,768]{1,0:T(8,128)S(1)}, u32[]{:S(2)}, u32[]{:S(2)}) collective-permute-start(f32[128,768]{1,0:T(8,128)S(1)} %get-tuple-element.14), channel_id=1, source_target_pairs={{0,14},{2,0},{4,2},{6,4},{8,6},{10,8},{12,10},{14,12},{1,15},{3,1}... | collective-permute-start | bytes 1179656 | tf_op jit(solution)/shard_map/ppermute | solution.py:94
  142.0 6.1 %collective-permute-done.7 = f32[128,768]{1,0:T(8,128)S(1)} collective-permute-done((f32[128,768]{1,0:T(8,128)S(1)}, f32[128,768]{1,0:T(8,128)S(1)}, u32[]{:S(2)}, u32[]{:S(2)}) %collective-permute-start.7) | collective-permute-done | bytes 393248 | tf_op jit(solution)/shard_map/ppermute | solution.py:94
  148.1 3.4 %collective-permute-done.4 = f32[128,768]{1,0:T(8,128)S(1)} collective-permute-done((f32[128,768]{1,0:T(8,128)S(1)}, f32[128,768]{1,0:T(8,128)S(1)}, u32[]{:S(2)}, u32[]{:S(2)}) %collective-permute-start.4) | collective-permute-done | bytes 393248 | tf_op jit(solution)/shard_map/ppermute | solution.py:89
  152.6 3.1 %collective-permute-start.10 = (f32[32,768]{1,0:T(8,128)S(1)}, f32[32,768]{1,0:T(8,128)S(1)}, u32[]{:S(2)}, u32[]{:S(2)}) collective-permute-start(f32[32,768]{1,0:T(8,128)S(1)} %get-tuple-element.20), channel_id=1, source_target_pairs={{0,48},{16,0},{32,16},{48,32},{1,49},{17,1},{33,17},{49,33},{2,50}... | collective-permute-start | bytes 294920 | tf_op jit(solution)/shard_map/ppermute | solution.py:70
  157.3 5.9 %convolution_convert_fusion = bf16[512,2048]{1,0:T(8,128)(2,1)} fusion(bf16[512,1024]{0,1:T(8,128)(2,1)S(1)} %copy-done, bf16[2048,1024]{1,0:T(8,128)(2,1)} %reshape.59), kind=kOutput, calls=%fused_computation.5 | convolution fusion | flops 2148532224 | bytes 7340032 | tf_op jit(solution)/shard_map/dot_general | solution.py:130
  (45 shorter events, 11.2 us)
Async XLA Ops:
  7.2 42.6 %all-gather.2.cloned.1.call-start = ((), (), s32[]{:S(2)}) async-start(), calls=%async_computation.1 | async-start | bytes 1310720 | tf_op jit(solution)/shard_map/all_gather | solution.py:116
  9.0 154.2 %reduce-scatter.2.cloned.1.call-start = ((), (), s32[]{:S(2)}) async-start(), calls=%async_computation.2 | async-start | bytes 2621440 | tf_op jit(solution)/shard_map/reduce_scatter | solution.py:118
  9.1 10.7 %copy-start.5 = (s32[32,12]{0,1:T(8,128)S(1)}, s32[32,12]{0,1:T(8,128)}, u32[]{:S(2)}) copy-start(s32[32,12]{0,1:T(8,128)} %param.7) | copy-start | bytes 4612
  9.1 10.8 %copy-start.6 = (s32[32]{0:T(128)S(1)}, s32[32]{0:T(128)}, u32[]{:S(2)}) copy-start(s32[32]{0:T(128)} %param.8) | copy-start | bytes 388
  29.0 12.3 %copy-start.3 = (bf16[512,2048]{1,0:T(8,128)(2,1)S(1)}, bf16[512,2048]{1,0:T(8,128)(2,1)}, u32[]{:S(2)}) copy-start(bf16[512,2048]{1,0:T(8,128)(2,1)} %param.5) | copy-start | bytes 6291460
  49.8 14.3 %copy-start.4 = (bf16[512,2048]{0,1:T(8,128)(2,1)S(1)}, bf16[512,2048]{0,1:T(8,128)(2,1)}, u32[]{:S(2)}) copy-start(bf16[512,2048]{0,1:T(8,128)(2,1)} %copy.17) | copy-start | bytes 6291460
  81.7 2.7 %copy-start.1 = (f32[4,8,2,32,768]{4,3,0,1,2:T(8,128)}, f32[4,8,2,32,768]{4,3,0,1,2:T(8,128)S(1)}, u32[]{:S(2)}) copy-start(f32[4,8,2,32,768]{4,3,0,1,2:T(8,128)S(1)} %copy.18) | copy-start | bytes 18874372
  86.2 6.0 %collective-permute-start = (f32[1024,768]{1,0:T(8,128)}, f32[1024,768]{1,0:T(8,128)}, u32[]{:S(2)}, u32[]{:S(2)}) collective-permute-start(f32[1024,768]{1,0:T(8,128)} %dynamic-slice_bitcast_fusion), channel_id=1, source_target_pairs={{0,1},{1,0},{2,3},{3,2},{4,5},{5,4},{6,7},{7,6},{8,9},{9,8},{10,11... | collective-permute-start | bytes 9437192 | tf_op jit(solution)/shard_map/ppermute | solution.py:46
  95.4 1.6 copy-start.2
  97.1 60.2 %copy-start = (bf16[512,1024]{0,1:T(8,128)(2,1)S(1)}, bf16[512,1024]{0,1:T(8,128)(2,1)}, u32[]{:S(2)}) copy-start(bf16[512,1024]{0,1:T(8,128)(2,1)} %all-gather.2.cloned.1.call-done) | copy-start | bytes 3145732
  97.1 15.5 %collective-permute-start.1 = (f32[128,768]{1,0:T(8,128)S(1)}, f32[128,768]{1,0:T(8,128)S(1)}, u32[]{:S(2)}, u32[]{:S(2)}) collective-permute-start(f32[128,768]{1,0:T(8,128)S(1)} %get-tuple-element.17), channel_id=1, source_target_pairs={{0,2},{2,4},{4,6},{6,8},{8,10},{10,12},{12,14},{14,0},{1,3},{3,5},... | collective-permute-start | bytes 1179656 | tf_op jit(solution)/shard_map/ppermute | solution.py:89
  99.1 14.7 %collective-permute-start.5 = (f32[128,768]{1,0:T(8,128)S(1)}, f32[128,768]{1,0:T(8,128)S(1)}, u32[]{:S(2)}, u32[]{:S(2)}) collective-permute-start(f32[128,768]{1,0:T(8,128)S(1)} %get-tuple-element.18), channel_id=1, source_target_pairs={{0,14},{2,0},{4,2},{6,4},{8,6},{10,8},{12,10},{14,12},{1,15},{3,1}... | collective-permute-start | bytes 1179656 | tf_op jit(solution)/shard_map/ppermute | solution.py:94
  113.7 11.9 %collective-permute-start.2 = (f32[128,768]{1,0:T(8,128)S(1)}, f32[128,768]{1,0:T(8,128)S(1)}, u32[]{:S(2)}, u32[]{:S(2)}) collective-permute-start(f32[128,768]{1,0:T(8,128)S(1)} %bitcast_add_fusion.6), channel_id=1, source_target_pairs={{0,2},{2,4},{4,6},{6,8},{8,10},{10,12},{12,14},{14,0},{1,3},{3,5},... | collective-permute-start | bytes 1179656 | tf_op jit(solution)/shard_map/ppermute | solution.py:89
  126.8 11.0 %collective-permute-start.3 = (f32[128,768]{1,0:T(8,128)S(1)}, f32[128,768]{1,0:T(8,128)S(1)}, u32[]{:S(2)}, u32[]{:S(2)}) collective-permute-start(f32[128,768]{1,0:T(8,128)S(1)} %get-tuple-element.15), channel_id=1, source_target_pairs={{0,2},{2,4},{4,6},{6,8},{8,10},{10,12},{12,14},{14,0},{1,3},{3,5},... | collective-permute-start | bytes 1179656 | tf_op jit(solution)/shard_map/ppermute | solution.py:89
  126.9 10.9 %collective-permute-start.6 = (f32[128,768]{1,0:T(8,128)S(1)}, f32[128,768]{1,0:T(8,128)S(1)}, u32[]{:S(2)}, u32[]{:S(2)}) collective-permute-start(f32[128,768]{1,0:T(8,128)S(1)} %get-tuple-element.16), channel_id=1, source_target_pairs={{0,14},{2,0},{4,2},{6,4},{8,6},{10,8},{12,10},{14,12},{1,15},{3,1}... | collective-permute-start | bytes 1179656 | tf_op jit(solution)/shard_map/ppermute | solution.py:94
  139.0 9.1 %collective-permute-start.7 = (f32[128,768]{1,0:T(8,128)S(1)}, f32[128,768]{1,0:T(8,128)S(1)}, u32[]{:S(2)}, u32[]{:S(2)}) collective-permute-start(f32[128,768]{1,0:T(8,128)S(1)} %get-tuple-element.14), channel_id=1, source_target_pairs={{0,14},{2,0},{4,2},{6,4},{8,6},{10,8},{12,10},{14,12},{1,15},{3,1}... | collective-permute-start | bytes 1179656 | tf_op jit(solution)/shard_map/ppermute | solution.py:94
  142.0 9.5 %collective-permute-start.4 = (f32[128,768]{1,0:T(8,128)S(1)}, f32[128,768]{1,0:T(8,128)S(1)}, u32[]{:S(2)}, u32[]{:S(2)}) collective-permute-start(f32[128,768]{1,0:T(8,128)S(1)} %get-tuple-element.13), channel_id=1, source_target_pairs={{0,2},{2,4},{4,6},{6,8},{8,10},{10,12},{12,14},{14,0},{1,3},{3,5},... | collective-permute-start | bytes 1179656 | tf_op jit(solution)/shard_map/ppermute | solution.py:89
  152.6 12.5 %collective-permute-start.10 = (f32[32,768]{1,0:T(8,128)S(1)}, f32[32,768]{1,0:T(8,128)S(1)}, u32[]{:S(2)}, u32[]{:S(2)}) collective-permute-start(f32[32,768]{1,0:T(8,128)S(1)} %get-tuple-element.20), channel_id=1, source_target_pairs={{0,48},{16,0},{32,16},{48,32},{1,49},{17,1},{33,17},{49,33},{2,50}... | collective-permute-start | bytes 294920 | tf_op jit(solution)/shard_map/ppermute | solution.py:70
  155.8 9.4 %collective-permute-start.9 = (f32[32,768]{1,0:T(8,128)S(1)}, f32[32,768]{1,0:T(8,128)S(1)}, u32[]{:S(2)}, u32[]{:S(2)}) collective-permute-start(f32[32,768]{1,0:T(8,128)S(1)} %get-tuple-element.21), channel_id=1, source_target_pairs={{0,32},{16,48},{32,0},{48,16},{1,33},{17,49},{33,1},{49,17},{2,34}... | collective-permute-start | bytes 294920 | tf_op jit(solution)/shard_map/ppermute | solution.py:70
  156.4 8.8 %collective-permute-start.8 = (f32[32,768]{1,0:T(8,128)S(1)}, f32[32,768]{1,0:T(8,128)S(1)}, u32[]{:S(2)}, u32[]{:S(2)}) collective-permute-start(f32[32,768]{1,0:T(8,128)S(1)} %get-tuple-element.19), channel_id=1, source_target_pairs={{0,16},{16,32},{32,48},{48,0},{1,17},{17,33},{33,49},{49,1},{2,18}... | collective-permute-start | bytes 294920 | tf_op jit(solution)/shard_map/ppermute | solution.py:70
Sparse Core Ops, SparseCore 0:
  10.3 30.2 all-gather.1
  86.4 34.1 reduce-scatter.1

commit v6 on v5

--- a/solution.py
+++ b/solution.py
@@ -112,9 +112,9 @@
         .astype(jnp.bfloat16)
         .reshape(features, width)
     )
+    cotangent_all = lax.all_gather(cotangent, "x", axis=0, tiled=True)
+    weight, cotangent_all = lax.optimization_barrier((weight, cotangent_all))
     partial_value = jnp.dot(tokens, weight, preferred_element_type=jnp.float32)
-    cotangent_all = lax.all_gather(cotangent, "x", axis=0, tiled=True)
-    partial_value, cotangent_all = lax.optimization_barrier((partial_value, cotangent_all))
     preact_own = lax.psum_scatter(partial_value, "x", scatter_dimension=0, tiled=True)
     activation = preact_own.astype(jnp.bfloat16)
     picked = slot_grad(tokens, cotangent_all, column_blocks, counts, block, replicas)

time: 174 us -> 169 us (0.971)
  waiting for transfers between devices: 44.2 us -> 40.5 us
    ppermute x1, waiting for transfers between devices: 5.92 us -> 2.2 us  [ring_scatter(): return take(idx) + lax.ppermute(take(idx + 1), axis, [(0, 1), (1, 0)])]
    dot_general x1, matrix products: 5.96 us -> 3.72 us  [per_device(): partial_value = jnp.dot(tokens, weight, preferred_element_type=jnp.float32)]
  transfers between devices with their start and end apart: 13 -> 13, of which waited for: 6 -> 6; matrix products, arithmetic and copies ran while one was open for 33% -> 32% of each run, Pallas kernels for 0% -> 0%
where the time goes in v6:
time: 169 us; the launch traced here: 168 us
  local copies, waits for them, and re-layouts  52.7 us (31%)
  waiting for transfers between devices  40.5 us (24%)
  matrix products  33.4 us (20%)
  starting transfers between devices  17.4 us (10%)
  between operations  14.3 us (8%)
  other arithmetic  9.55 us (6%)
    ppermute x4, waiting for transfers between devices, meeting_scatter(): a = lax.ppermute(a, axis, fwd) + take(idx + ahead - s)  32.2 us
    dot_general x1, matrix products, slot_grad(): lax.dot_general(tok_rows, picked, (((2,), (2,)), ((0,), (0,))), preferred...  14.8 us
    gather x1, local copies, waits for them, and re-layouts, slot_grad(): picked = jnp.take(cot_rows, column_blocks, axis=0, mode='clip')  14.2 us
    reshape x1, local copies, waits for them, and re-layouts, per_device(): weight = jnp.einsum('bkc,bikj->bicj', onehot, blocks_view, preferred_elem...  12 us
    reshape x1, local copies, waits for them, and re-layouts, per_device(): blocks_view = block_values.reshape(row_blocks, block, slots, block)  10.6 us
    ppermute x3, starting transfers between devices, meeting_scatter(): b = lax.ppermute(b, axis, bwd)  10.5 us
    unnamed x18, local copies, waits for them, and re-layouts  10.1 us
    dot_general x1, matrix products, per_device(): jnp.einsum('bkc,bikj->bicj', onehot, blocks_view, preferred_element_type=...  8.96 us
  transfers between devices with their start and end apart: 13, of which 6 were waited for; matrix products, arithmetic and copies ran while one was open for 32% of the time, Pallas kernels for 0%

profile of v6, /device:TPU:2, one launch (start us, length us, event | category | flops | bytes accessed | tf_op | source)
XLA Modules:
  0.0 167.9 jit_solution(2114069366162508614)
XLA Ops:
  7.2 1.8 %copy.15 = bf16[128,1024]{0,1:T(8,128)(2,1)} copy(bf16[128,1024]{1,0:T(8,128)(2,1)} %param.9) | data formatting | bytes 524288 | tf_op args[4]
  9.1 10.6 %reshape.78 = bf16[32,64,12,64]{3,2,1,0:T(8,128)(2,1)} reshape(bf16[2048,768]{1,0:T(8,128)(2,1)} %param.6) | data formatting | bytes 6291456 | tf_op jit(solution)/shard_map/reshape | solution.py:109
  20.0 9.0 %convert_bitcast_fusion = bf16[32,64,16,64]{3,2,1,0:T(8,128)(2,1)} fusion(bf16[32,64,12,64]{3,2,1,0:T(8,128)(2,1)} %reshape.78, s32[32,12]{1,0:T(8,128)S(1)} %copy.12, pred[32,12]{1,0:T(8,128)(4,1)S(1)} %iota_compare_fusion.1), kind=kOutput, calls=%fused_computation.1 | convolution fusion | flops 52441088 | bytes 7341952 | tf_op jit(solution)/shard_map/bkc,bikj->bicj/dot_general | solution.py:111
  29.0 12.0 %reshape.59 = bf16[2048,1024]{1,0:T(8,128)(2,1)} reshape(bf16[32,64,16,64]{3,2,1,0:T(8,128)(2,1)} %convert_bitcast_fusion) | data formatting | bytes 8388608 | tf_op jit(solution)/shard_map/reshape | solution.py:113
  41.3 2.5 %copy.17 = bf16[512,2048]{0,1:T(8,128)(2,1)} copy(bf16[512,2048]{1,0:T(8,128)(2,1)S(1)} %copy-done.4) | data formatting | bytes 4194304 | tf_op args[0]
  43.8 14.2 %gather_fusion = bf16[384,64,512]{2,1,0:T(8,128)(2,1)} fusion(bf16[16,64,512]{2,1,0:T(8,128)(2,1)} %bitcast.67, s32[1024]{0:T(1024)S(1)} %pad_clamp_fusion), kind=kCustom, calls=%fused_computation | custom fusion | bytes 50333184 | tf_op jit(solution)/shard_map/jit(_take)/gather | solution.py:23
  58.0 14.8 %multiply_select_fusion = f32[32,768,64]{1,2,0:T(8,128)} fusion(pred[32,768]{1,0:T(8,128)(4,1)S(1)} %broadcast_in_dim.28, bf16[32,768,512]{2,1,0:T(8,128)(2,1)} %bitcast.68, bf16[32,64,512]{2,1,0:T(8,128)(2,1)} %bitcast.77), kind=kOutput, calls=%fused_computation.2 | convolution fusion | flops 1613758464 | bytes 33579008 | tf_op jit(solution)/shard_map/dot_general | solution.py:26
  72.8 3.5 %copy.18 = f32[4,8,2,32,768]{4,3,0,1,2:T(8,128)S(1)} copy(f32[4,8,2,32,768]{4,3,2,1,0:T(8,128)} %bitcast.76) | data formatting | bytes 12582912 | tf_op jit(solution)/shard_map/reshape | solution.py:123
  76.3 3.2 %copy-done.1 = f32[4,8,2,32,768]{4,3,0,1,2:T(8,128)} copy-done((f32[4,8,2,32,768]{4,3,0,1,2:T(8,128)}, f32[4,8,2,32,768]{4,3,0,1,2:T(8,128)S(1)}, u32[]{:S(2)}) %copy-start.1) | copy-done | bytes 6291480
  79.5 1.9 %dynamic-slice_bitcast_fusion = f32[1024,768]{1,0:T(8,128)} fusion(f32[2,1024,768]{2,1,0:T(8,128)S(1)} %bitcast.69, s32[]{:T(128)S(6)} %select_n.116), kind=kLoop, calls=%fused_computation.4 | loop fusion | bytes 6291460 | tf_op jit(solution)/shard_map/jit(dynamic_index_in_dim)/squeeze | solution.py:43
  81.4 3.7 %convolution_bitcast_fusion = f32[512,1024]{0,1:T(8,128)} fusion(bf16[2048,1024]{1,0:T(8,128)(2,1)S(1)} %copy-done.3, bf16[512,2048]{1,0:T(8,128)(2,1)S(1)} %copy-done.4), kind=kOutput, calls=%fused_computation.6 | convolution fusion | flops 2147483648 | bytes 8388608 | tf_op jit(solution)/shard_map/dot_general | solution.py:117
  85.2 2.2 %collective-permute-done = f32[1024,768]{1,0:T(8,128)} collective-permute-done((f32[1024,768]{1,0:T(8,128)}, f32[1024,768]{1,0:T(8,128)}, u32[]{:S(2)}, u32[]{:S(2)}) %collective-permute-start) | collective-permute-done | bytes 3145760 | tf_op jit(solution)/shard_map/ppermute | solution.py:46
  87.4 3.2 %bitcast_add_fusion = f32[1024,768]{1,0:T(8,128)S(1)} fusion(f32[1024,768]{1,0:T(8,128)} %collective-permute-done, f32[2,1024,768]{2,1,0:T(8,128)} %bitcast.70, s32[]{:T(128)S(6)} %select_n.114), kind=kLoop, calls=%fused_computation.3 | loop fusion | flops 786432 | bytes 9437188 | tf_op jit(solution)/shard_map/add | solution.py:46
  92.3 2.0 %collective-permute-start.1 = (f32[128,768]{1,0:T(8,128)S(1)}, f32[128,768]{1,0:T(8,128)S(1)}, u32[]{:S(2)}, u32[]{:S(2)}) collective-permute-start(f32[128,768]{1,0:T(8,128)S(1)} %get-tuple-element.17), channel_id=1, source_target_pairs={{0,2},{2,4},{4,6},{6,8},{8,10},{10,12},{12,14},{14,0},{1,3},{3,5},... | collective-permute-start | bytes 1179656 | tf_op jit(solution)/shard_map/ppermute | solution.py:89
  94.3 4.2 %collective-permute-start.5 = (f32[128,768]{1,0:T(8,128)S(1)}, f32[128,768]{1,0:T(8,128)S(1)}, u32[]{:S(2)}, u32[]{:S(2)}) collective-permute-start(f32[128,768]{1,0:T(8,128)S(1)} %get-tuple-element.18), channel_id=1, source_target_pairs={{0,14},{2,0},{4,2},{6,4},{8,6},{10,8},{12,10},{14,12},{1,15},{3,1}... | collective-permute-start | bytes 1179656 | tf_op jit(solution)/shard_map/ppermute | solution.py:94
  98.5 9.3 %collective-permute-done.1 = f32[128,768]{1,0:T(8,128)S(1)} collective-permute-done((f32[128,768]{1,0:T(8,128)S(1)}, f32[128,768]{1,0:T(8,128)S(1)}, u32[]{:S(2)}, u32[]{:S(2)}) %collective-permute-start.1) | collective-permute-done | bytes 393248 | tf_op jit(solution)/shard_map/ppermute | solution.py:89
  109.0 11.7 %collective-permute-done.2 = f32[128,768]{1,0:T(8,128)S(1)} collective-permute-done((f32[128,768]{1,0:T(8,128)S(1)}, f32[128,768]{1,0:T(8,128)S(1)}, u32[]{:S(2)}, u32[]{:S(2)}) %collective-permute-start.2) | collective-permute-done | bytes 393248 | tf_op jit(solution)/shard_map/ppermute | solution.py:89
  122.1 3.2 %collective-permute-start.6 = (f32[128,768]{1,0:T(8,128)S(1)}, f32[128,768]{1,0:T(8,128)S(1)}, u32[]{:S(2)}, u32[]{:S(2)}) collective-permute-start(f32[128,768]{1,0:T(8,128)S(1)} %get-tuple-element.16), channel_id=1, source_target_pairs={{0,14},{2,0},{4,2},{6,4},{8,6},{10,8},{12,10},{14,12},{1,15},{3,1}... | collective-permute-start | bytes 1179656 | tf_op jit(solution)/shard_map/ppermute | solution.py:94
  125.3 7.7 %collective-permute-done.3 = f32[128,768]{1,0:T(8,128)S(1)} collective-permute-done((f32[128,768]{1,0:T(8,128)S(1)}, f32[128,768]{1,0:T(8,128)S(1)}, u32[]{:S(2)}, u32[]{:S(2)}) %collective-permute-start.3) | collective-permute-done | bytes 393248 | tf_op jit(solution)/shard_map/ppermute | solution.py:89
  134.2 3.0 %collective-permute-start.7 = (f32[128,768]{1,0:T(8,128)S(1)}, f32[128,768]{1,0:T(8,128)S(1)}, u32[]{:S(2)}, u32[]{:S(2)}) collective-permute-start(f32[128,768]{1,0:T(8,128)S(1)} %get-tuple-element.14), channel_id=1, source_target_pairs={{0,14},{2,0},{4,2},{6,4},{8,6},{10,8},{12,10},{14,12},{1,15},{3,1}... | collective-permute-start | bytes 1179656 | tf_op jit(solution)/shard_map/ppermute | solution.py:94
  137.2 6.1 %collective-permute-done.7 = f32[128,768]{1,0:T(8,128)S(1)} collective-permute-done((f32[128,768]{1,0:T(8,128)S(1)}, f32[128,768]{1,0:T(8,128)S(1)}, u32[]{:S(2)}, u32[]{:S(2)}) %collective-permute-start.7) | collective-permute-done | bytes 393248 | tf_op jit(solution)/shard_map/ppermute | solution.py:94
  143.3 3.4 %collective-permute-done.4 = f32[128,768]{1,0:T(8,128)S(1)} collective-permute-done((f32[128,768]{1,0:T(8,128)S(1)}, f32[128,768]{1,0:T(8,128)S(1)}, u32[]{:S(2)}, u32[]{:S(2)}) %collective-permute-start.4) | collective-permute-done | bytes 393248 | tf_op jit(solution)/shard_map/ppermute | solution.py:89
  147.8 3.1 %collective-permute-start.10 = (f32[32,768]{1,0:T(8,128)S(1)}, f32[32,768]{1,0:T(8,128)S(1)}, u32[]{:S(2)}, u32[]{:S(2)}) collective-permute-start(f32[32,768]{1,0:T(8,128)S(1)} %get-tuple-element.20), channel_id=1, source_target_pairs={{0,48},{16,0},{32,16},{48,32},{1,49},{17,1},{33,17},{49,33},{2,50}... | collective-permute-start | bytes 294920 | tf_op jit(solution)/shard_map/ppermute | solution.py:70
  152.5 5.9 %convolution_convert_fusion = bf16[512,2048]{1,0:T(8,128)(2,1)} fusion(bf16[512,1024]{0,1:T(8,128)(2,1)S(1)} %copy-done, bf16[2048,1024]{1,0:T(8,128)(2,1)} %reshape.59), kind=kOutput, calls=%fused_computation.5 | convolution fusion | flops 2148532224 | bytes 7340032 | tf_op jit(solution)/shard_map/dot_general | solution.py:130
  (45 shorter events, 11.2 us)
Async XLA Ops:
  7.2 36.6 %all-gather.2.cloned.1.call-start = ((), (), s32[]{:S(2)}) async-start(), calls=%async_computation.1 | async-start | bytes 1310720 | tf_op jit(solution)/shard_map/all_gather | solution.py:115
  9.0 149.4 %reduce-scatter.2.cloned.1.call-start = ((), (), s32[]{:S(2)}) async-start(), calls=%async_computation.2 | async-start | bytes 2621440 | tf_op jit(solution)/shard_map/reduce_scatter | solution.py:118
  9.1 10.7 %copy-start.5 = (s32[32,12]{0,1:T(8,128)S(1)}, s32[32,12]{0,1:T(8,128)}, u32[]{:S(2)}) copy-start(s32[32,12]{0,1:T(8,128)} %param.7) | copy-start | bytes 4612
  9.1 10.8 %copy-start.6 = (s32[32]{0:T(128)S(1)}, s32[32]{0:T(128)}, u32[]{:S(2)}) copy-start(s32[32]{0:T(128)} %param.8) | copy-start | bytes 388
  29.0 12.3 %copy-start.4 = (bf16[512,2048]{1,0:T(8,128)(2,1)S(1)}, bf16[512,2048]{1,0:T(8,128)(2,1)}, u32[]{:S(2)}) copy-start(bf16[512,2048]{1,0:T(8,128)(2,1)} %param.5) | copy-start | bytes 6291460
  76.3 3.2 %copy-start.1 = (f32[4,8,2,32,768]{4,3,0,1,2:T(8,128)}, f32[4,8,2,32,768]{4,3,0,1,2:T(8,128)S(1)}, u32[]{:S(2)}) copy-start(f32[4,8,2,32,768]{4,3,0,1,2:T(8,128)S(1)} %copy.18) | copy-start | bytes 18874372
  76.3 5.1 %copy-start.3 = (bf16[2048,1024]{1,0:T(8,128)(2,1)S(1)}, bf16[2048,1024]{1,0:T(8,128)(2,1)}, u32[]{:S(2)}) copy-start(bf16[2048,1024]{1,0:T(8,128)(2,1)} %reshape.59) | copy-start | bytes 12582916
  81.4 6.0 %collective-permute-start = (f32[1024,768]{1,0:T(8,128)}, f32[1024,768]{1,0:T(8,128)}, u32[]{:S(2)}, u32[]{:S(2)}) collective-permute-start(f32[1024,768]{1,0:T(8,128)} %dynamic-slice_bitcast_fusion), channel_id=1, source_target_pairs={{0,1},{1,0},{2,3},{3,2},{4,5},{5,4},{6,7},{7,6},{8,9},{9,8},{10,11... | collective-permute-start | bytes 9437192 | tf_op jit(solution)/shard_map/ppermute | solution.py:46
  90.6 1.6 copy-start.2
  92.3 60.2 %copy-start = (bf16[512,1024]{0,1:T(8,128)(2,1)S(1)}, bf16[512,1024]{0,1:T(8,128)(2,1)}, u32[]{:S(2)}) copy-start(bf16[512,1024]{0,1:T(8,128)(2,1)} %all-gather.2.cloned.1.call-done) | copy-start | bytes 3145732
  92.3 15.5 %collective-permute-start.1 = (f32[128,768]{1,0:T(8,128)S(1)}, f32[128,768]{1,0:T(8,128)S(1)}, u32[]{:S(2)}, u32[]{:S(2)}) collective-permute-start(f32[128,768]{1,0:T(8,128)S(1)} %get-tuple-element.17), channel_id=1, source_target_pairs={{0,2},{2,4},{4,6},{6,8},{8,10},{10,12},{12,14},{14,0},{1,3},{3,5},... | collective-permute-start | bytes 1179656 | tf_op jit(solution)/shard_map/ppermute | solution.py:89
  94.3 14.7 %collective-permute-start.5 = (f32[128,768]{1,0:T(8,128)S(1)}, f32[128,768]{1,0:T(8,128)S(1)}, u32[]{:S(2)}, u32[]{:S(2)}) collective-permute-start(f32[128,768]{1,0:T(8,128)S(1)} %get-tuple-element.18), channel_id=1, source_target_pairs={{0,14},{2,0},{4,2},{6,4},{8,6},{10,8},{12,10},{14,12},{1,15},{3,1}... | collective-permute-start | bytes 1179656 | tf_op jit(solution)/shard_map/ppermute | solution.py:94
  108.9 11.9 %collective-permute-start.2 = (f32[128,768]{1,0:T(8,128)S(1)}, f32[128,768]{1,0:T(8,128)S(1)}, u32[]{:S(2)}, u32[]{:S(2)}) collective-permute-start(f32[128,768]{1,0:T(8,128)S(1)} %bitcast_add_fusion.6), channel_id=1, source_target_pairs={{0,2},{2,4},{4,6},{6,8},{8,10},{10,12},{12,14},{14,0},{1,3},{3,5},... | collective-permute-start | bytes 1179656 | tf_op jit(solution)/shard_map/ppermute | solution.py:89
  122.0 11.0 %collective-permute-start.3 = (f32[128,768]{1,0:T(8,128)S(1)}, f32[128,768]{1,0:T(8,128)S(1)}, u32[]{:S(2)}, u32[]{:S(2)}) collective-permute-start(f32[128,768]{1,0:T(8,128)S(1)} %get-tuple-element.15), channel_id=1, source_target_pairs={{0,2},{2,4},{4,6},{6,8},{8,10},{10,12},{12,14},{14,0},{1,3},{3,5},... | collective-permute-start | bytes 1179656 | tf_op jit(solution)/shard_map/ppermute | solution.py:89
  122.1 10.9 %collective-permute-start.6 = (f32[128,768]{1,0:T(8,128)S(1)}, f32[128,768]{1,0:T(8,128)S(1)}, u32[]{:S(2)}, u32[]{:S(2)}) collective-permute-start(f32[128,768]{1,0:T(8,128)S(1)} %get-tuple-element.16), channel_id=1, source_target_pairs={{0,14},{2,0},{4,2},{6,4},{8,6},{10,8},{12,10},{14,12},{1,15},{3,1}... | collective-permute-start | bytes 1179656 | tf_op jit(solution)/shard_map/ppermute | solution.py:94
  134.2 9.1 %collective-permute-start.7 = (f32[128,768]{1,0:T(8,128)S(1)}, f32[128,768]{1,0:T(8,128)S(1)}, u32[]{:S(2)}, u32[]{:S(2)}) collective-permute-start(f32[128,768]{1,0:T(8,128)S(1)} %get-tuple-element.14), channel_id=1, source_target_pairs={{0,14},{2,0},{4,2},{6,4},{8,6},{10,8},{12,10},{14,12},{1,15},{3,1}... | collective-permute-start | bytes 1179656 | tf_op jit(solution)/shard_map/ppermute | solution.py:94
  137.2 9.5 %collective-permute-start.4 = (f32[128,768]{1,0:T(8,128)S(1)}, f32[128,768]{1,0:T(8,128)S(1)}, u32[]{:S(2)}, u32[]{:S(2)}) collective-permute-start(f32[128,768]{1,0:T(8,128)S(1)} %get-tuple-element.13), channel_id=1, source_target_pairs={{0,2},{2,4},{4,6},{6,8},{8,10},{10,12},{12,14},{14,0},{1,3},{3,5},... | collective-permute-start | bytes 1179656 | tf_op jit(solution)/shard_map/ppermute | solution.py:89
  147.8 12.5 %collective-permute-start.10 = (f32[32,768]{1,0:T(8,128)S(1)}, f32[32,768]{1,0:T(8,128)S(1)}, u32[]{:S(2)}, u32[]{:S(2)}) collective-permute-start(f32[32,768]{1,0:T(8,128)S(1)} %get-tuple-element.20), channel_id=1, source_target_pairs={{0,48},{16,0},{32,16},{48,32},{1,49},{17,1},{33,17},{49,33},{2,50}... | collective-permute-start | bytes 294920 | tf_op jit(solution)/shard_map/ppermute | solution.py:70
  150.9 9.4 %collective-permute-start.9 = (f32[32,768]{1,0:T(8,128)S(1)}, f32[32,768]{1,0:T(8,128)S(1)}, u32[]{:S(2)}, u32[]{:S(2)}) collective-permute-start(f32[32,768]{1,0:T(8,128)S(1)} %get-tuple-element.21), channel_id=1, source_target_pairs={{0,32},{16,48},{32,0},{48,16},{1,33},{17,49},{33,1},{49,17},{2,34}... | collective-permute-start | bytes 294920 | tf_op jit(solution)/shard_map/ppermute | solution.py:70
  151.5 8.8 %collective-permute-start.8 = (f32[32,768]{1,0:T(8,128)S(1)}, f32[32,768]{1,0:T(8,128)S(1)}, u32[]{:S(2)}, u32[]{:S(2)}) collective-permute-start(f32[32,768]{1,0:T(8,128)S(1)} %get-tuple-element.19), channel_id=1, source_target_pairs={{0,16},{16,32},{32,48},{48,0},{1,17},{17,33},{33,49},{49,1},{2,18}... | collective-permute-start | bytes 294920 | tf_op jit(solution)/shard_map/ppermute | solution.py:70
Sparse Core Ops, SparseCore 0:
  10.3 30.2 all-gather.1
  85.3 34.1 reduce-scatter.1

commit v7 on v6

--- a/solution.py
+++ b/solution.py
@@ -121,12 +121,12 @@
     owned = features // replicas
     staged = (
         picked.reshape(n_y, n_z, n_core, owned, slots * block)
-        .transpose(2, 1, 0, 3, 4)
+        .transpose(2, 0, 1, 3, 4)
         .reshape(features, slots * block)
     )
     staged = ring_scatter(staged, "core")
-    staged = meeting_scatter(staged, "z")
-    weight_grad = direct_scatter(staged, "y")
+    staged = direct_scatter(staged, "y")
+    weight_grad = meeting_scatter(staged, "z")
     input_grad = lax.dot_general(
         cotangent_all, weight, (((1,), (1,)), ((), ())), preferred_element_type=jnp.float32
     ).astype(jnp.bfloat16)

time: 169 us -> 176 us (1.041)
  waiting for transfers between devices: 40.5 us -> 49.5 us
  other arithmetic: 9.55 us -> 6.65 us
    ppermute x3, waiting for transfers between devices: 0.01 us -> 36.2 us  [direct_scatter(): total = total + lax.ppermute(take(idx + shift), axis, perm)]
    ppermute x4, waiting for transfers between devices: 32.2 us -> 11.1 us  [meeting_scatter(): a = lax.ppermute(a, axis, fwd) + take(idx + ahead - s)]
    ppermute x3, waiting for transfers between devices: 6.11 us -> 0.01 us  [meeting_scatter(): b = lax.ppermute(b, axis, bwd)]
    add x3, other arithmetic: 3.45 us -> 0.06 us  [meeting_scatter(): a = lax.ppermute(a, axis, fwd) + take(idx + ahead - s)]
  transfers between devices with their start and end apart: 13 -> 13, of which waited for: 6 -> 6; matrix products, arithmetic and copies ran while one was open for 32% -> 30% of each run, Pallas kernels for 0% -> 0%
where the time goes in v7:
time: 176 us; the launch traced here: 175 us
  local copies, waits for them, and re-layouts  53.9 us (31%)
  waiting for transfers between devices  49.5 us (28%)
  matrix products  33.4 us (19%)
  starting transfers between devices  17.6 us (10%)
  between operations  14.3 us (8%)
  other arithmetic  6.65 us (4%)
    ppermute x3, waiting for transfers between devices, direct_scatter(): total = total + lax.ppermute(take(idx + shift), axis, perm)  36.2 us
    dot_general x1, matrix products, slot_grad(): lax.dot_general(tok_rows, picked, (((2,), (2,)), ((0,), (0,))), preferred...  14.8 us
    gather x1, local copies, waits for them, and re-layouts, slot_grad(): picked = jnp.take(cot_rows, column_blocks, axis=0, mode='clip')  14.1 us
    reshape x1, local copies, waits for them, and re-layouts, per_device(): weight = jnp.einsum('bkc,bikj->bicj', onehot, blocks_view, preferred_elem...  12 us
    ppermute x4, waiting for transfers between devices, meeting_scatter(): a = lax.ppermute(a, axis, fwd) + take(idx + ahead - s)  11.1 us
    ppermute x3, starting transfers between devices, meeting_scatter(): b = lax.ppermute(b, axis, bwd)  10.7 us
    reshape x1, local copies, waits for them, and re-layouts, per_device(): blocks_view = block_values.reshape(row_blocks, block, slots, block)  10.6 us
    unnamed x18, local copies, waits for them, and re-layouts  10.1 us
  transfers between devices with their start and end apart: 13, of which 6 were waited for; matrix products, arithmetic and copies ran while one was open for 30% of the time, Pallas kernels for 0%

profile of v7, /device:TPU:2, one launch (start us, length us, event | category | flops | bytes accessed | tf_op | source)
XLA Modules:
  0.0 175.4 jit_solution(15007010119708471403)
XLA Ops:
  7.2 1.8 %copy.15 = bf16[128,1024]{0,1:T(8,128)(2,1)} copy(bf16[128,1024]{1,0:T(8,128)(2,1)} %param.9) | data formatting | bytes 524288 | tf_op args[4]
  9.1 10.6 %reshape.78 = bf16[32,64,12,64]{3,2,1,0:T(8,128)(2,1)} reshape(bf16[2048,768]{1,0:T(8,128)(2,1)} %param.6) | data formatting | bytes 6291456 | tf_op jit(solution)/shard_map/reshape | solution.py:109
  20.0 9.0 %convert_bitcast_fusion = bf16[32,64,16,64]{3,2,1,0:T(8,128)(2,1)} fusion(bf16[32,64,12,64]{3,2,1,0:T(8,128)(2,1)} %reshape.78, s32[32,12]{1,0:T(8,128)S(1)} %copy.12, pred[32,12]{1,0:T(8,128)(4,1)S(1)} %iota_compare_fusion.1), kind=kOutput, calls=%fused_computation.1 | convolution fusion | flops 52441088 | bytes 7341952 | tf_op jit(solution)/shard_map/bkc,bikj->bicj/dot_general | solution.py:111
  29.0 12.0 %reshape.59 = bf16[2048,1024]{1,0:T(8,128)(2,1)} reshape(bf16[32,64,16,64]{3,2,1,0:T(8,128)(2,1)} %convert_bitcast_fusion) | data formatting | bytes 8388608 | tf_op jit(solution)/shard_map/reshape | solution.py:113
  41.3 2.5 %copy.17 = bf16[512,2048]{0,1:T(8,128)(2,1)} copy(bf16[512,2048]{1,0:T(8,128)(2,1)S(1)} %copy-done.4) | data formatting | bytes 4194304 | tf_op args[0]
  43.8 14.1 %gather_fusion = bf16[384,64,512]{2,1,0:T(8,128)(2,1)} fusion(bf16[16,64,512]{2,1,0:T(8,128)(2,1)} %bitcast.67, s32[1024]{0:T(1024)S(1)} %pad_clamp_fusion), kind=kCustom, calls=%fused_computation | custom fusion | bytes 50333184 | tf_op jit(solution)/shard_map/jit(_take)/gather | solution.py:23
  58.0 14.8 %multiply_select_fusion = f32[32,768,64]{1,2,0:T(8,128)} fusion(pred[32,768]{1,0:T(8,128)(4,1)S(1)} %broadcast_in_dim.28, bf16[32,768,512]{2,1,0:T(8,128)(2,1)} %bitcast.68, bf16[32,64,512]{2,1,0:T(8,128)(2,1)} %bitcast.79), kind=kOutput, calls=%fused_computation.2 | convolution fusion | flops 1613758464 | bytes 33579008 | tf_op jit(solution)/shard_map/dot_general | solution.py:26
  72.8 3.5 %copy.18 = f32[4,8,2,32,768]{4,3,1,0,2:T(8,128)S(1)} copy(f32[4,8,2,32,768]{4,3,2,1,0:T(8,128)} %bitcast.73) | data formatting | bytes 12582912 | tf_op jit(solution)/shard_map/reshape | solution.py:123
  76.3 3.2 %copy-done.1 = f32[4,8,2,32,768]{4,3,1,0,2:T(8,128)} copy-done((f32[4,8,2,32,768]{4,3,1,0,2:T(8,128)}, f32[4,8,2,32,768]{4,3,1,0,2:T(8,128)S(1)}, u32[]{:S(2)}) %copy-start.1) | copy-done | bytes 6291480
  79.5 1.9 %dynamic-slice_bitcast_fusion = f32[1024,768]{1,0:T(8,128)} fusion(f32[2,1024,768]{2,1,0:T(8,128)S(1)} %bitcast.69, s32[]{:T(128)S(6)} %select_n.116), kind=kLoop, calls=%fused_computation.4 | loop fusion | bytes 6291460 | tf_op jit(solution)/shard_map/jit(dynamic_index_in_dim)/squeeze | solution.py:43
  81.3 3.7 %convolution_bitcast_fusion = f32[512,1024]{0,1:T(8,128)} fusion(bf16[2048,1024]{1,0:T(8,128)(2,1)S(1)} %copy-done.3, bf16[512,2048]{1,0:T(8,128)(2,1)S(1)} %copy-done.4), kind=kOutput, calls=%fused_computation.6 | convolution fusion | flops 2147483648 | bytes 8388608 | tf_op jit(solution)/shard_map/dot_general | solution.py:117
  85.2 2.2 %collective-permute-done = f32[1024,768]{1,0:T(8,128)} collective-permute-done((f32[1024,768]{1,0:T(8,128)}, f32[1024,768]{1,0:T(8,128)}, u32[]{:S(2)}, u32[]{:S(2)}) %collective-permute-start) | collective-permute-done | bytes 3145760 | tf_op jit(solution)/shard_map/ppermute | solution.py:46
  87.3 3.2 %bitcast_add_fusion = f32[1024,768]{1,0:T(8,128)S(1)} fusion(f32[1024,768]{1,0:T(8,128)} %collective-permute-done, f32[2,1024,768]{2,1,0:T(8,128)} %bitcast.70, s32[]{:T(128)S(6)} %select_n.114), kind=kLoop, calls=%fused_computation.3 | loop fusion | flops 786432 | bytes 9437188 | tf_op jit(solution)/shard_map/add | solution.py:46
  93.5 3.0 %collective-permute-start.3 = (f32[256,768]{1,0:T(8,128)}, f32[256,768]{1,0:T(8,128)S(1)}, u32[]{:S(2)}, u32[]{:S(2)}) collective-permute-start(f32[256,768]{1,0:T(8,128)} %get-tuple-element.14), channel_id=1, source_target_pairs={{0,48},{16,0},{32,16},{48,32},{1,49},{17,1},{33,17},{49,33},{2,50}... | collective-permute-start | bytes 2359304 | tf_op jit(solution)/shard_map/ppermute | solution.py:70
  98.2 32.7 %collective-permute-done.3 = f32[256,768]{1,0:T(8,128)S(1)} collective-permute-done((f32[256,768]{1,0:T(8,128)}, f32[256,768]{1,0:T(8,128)S(1)}, u32[]{:S(2)}, u32[]{:S(2)}) %collective-permute-start.3) | collective-permute-done | bytes 786464 | tf_op jit(solution)/shard_map/ppermute | solution.py:70
  130.8 3.5 %collective-permute-done.1 = f32[256,768]{1,0:T(8,128)} collective-permute-done((f32[256,768]{1,0:T(8,128)S(1)}, f32[256,768]{1,0:T(8,128)}, u32[]{:S(2)}, u32[]{:S(2)}) %collective-permute-start.1) | collective-permute-done | bytes 786464 | tf_op jit(solution)/shard_map/ppermute | solution.py:70
  136.0 2.0 %collective-permute-start.4 = (f32[32,768]{1,0:T(8,128)S(1)}, f32[32,768]{1,0:T(8,128)S(1)}, u32[]{:S(2)}, u32[]{:S(2)}) collective-permute-start(f32[32,768]{1,0:T(8,128)S(1)} %get-tuple-element.20), channel_id=1, source_target_pairs={{0,2},{2,4},{4,6},{6,8},{8,10},{10,12},{12,14},{14,0},{1,3},{3,5},... | collective-permute-start | bytes 294920 | tf_op jit(solution)/shard_map/ppermute | solution.py:89
  137.9 4.2 %collective-permute-start.8 = (f32[32,768]{1,0:T(8,128)S(1)}, f32[32,768]{1,0:T(8,128)S(1)}, u32[]{:S(2)}, u32[]{:S(2)}) collective-permute-start(f32[32,768]{1,0:T(8,128)S(1)} %get-tuple-element.21), channel_id=1, source_target_pairs={{0,14},{2,0},{4,2},{6,4},{8,6},{10,8},{12,10},{14,12},{1,15},{3,1}... | collective-permute-start | bytes 294920 | tf_op jit(solution)/shard_map/ppermute | solution.py:94
  142.2 2.7 %collective-permute-done.4 = f32[32,768]{1,0:T(8,128)S(1)} collective-permute-done((f32[32,768]{1,0:T(8,128)S(1)}, f32[32,768]{1,0:T(8,128)S(1)}, u32[]{:S(2)}, u32[]{:S(2)}) %collective-permute-start.4) | collective-permute-done | bytes 98336 | tf_op jit(solution)/shard_map/ppermute | solution.py:89
  145.0 5.8 %collective-permute-done.5 = f32[32,768]{1,0:T(8,128)S(1)} collective-permute-done((f32[32,768]{1,0:T(8,128)S(1)}, f32[32,768]{1,0:T(8,128)S(1)}, u32[]{:S(2)}, u32[]{:S(2)}) %collective-permute-start.5) | collective-permute-done | bytes 98336 | tf_op jit(solution)/shard_map/ppermute | solution.py:89
  150.9 3.2 %collective-permute-start.9 = (f32[32,768]{1,0:T(8,128)S(1)}, f32[32,768]{1,0:T(8,128)S(1)}, u32[]{:S(2)}, u32[]{:S(2)}) collective-permute-start(f32[32,768]{1,0:T(8,128)S(1)} %get-tuple-element.19), channel_id=1, source_target_pairs={{0,14},{2,0},{4,2},{6,4},{8,6},{10,8},{12,10},{14,12},{1,15},{3,1}... | collective-permute-start | bytes 294920 | tf_op jit(solution)/shard_map/ppermute | solution.py:94
  154.1 2.6 %collective-permute-done.6 = f32[32,768]{1,0:T(8,128)S(1)} collective-permute-done((f32[32,768]{1,0:T(8,128)S(1)}, f32[32,768]{1,0:T(8,128)S(1)}, u32[]{:S(2)}, u32[]{:S(2)}) %collective-permute-start.6) | collective-permute-done | bytes 98336 | tf_op jit(solution)/shard_map/ppermute | solution.py:89
  156.7 3.3 %collective-permute-start.10 = (f32[32,768]{1,0:T(8,128)S(1)}, f32[32,768]{1,0:T(8,128)S(1)}, u32[]{:S(2)}, u32[]{:S(2)}) collective-permute-start(f32[32,768]{1,0:T(8,128)S(1)} %get-tuple-element.17), channel_id=1, source_target_pairs={{0,14},{2,0},{4,2},{6,4},{8,6},{10,8},{12,10},{14,12},{1,15},{3,1}... | collective-permute-start | bytes 294920 | tf_op jit(solution)/shard_map/ppermute | solution.py:94
  160.1 5.9 %convolution_convert_fusion = bf16[512,2048]{1,0:T(8,128)(2,1)} fusion(bf16[512,1024]{0,1:T(8,128)(2,1)S(1)} %copy-done, bf16[2048,1024]{1,0:T(8,128)(2,1)} %reshape.59), kind=kOutput, calls=%fused_computation.5 | convolution fusion | flops 2148532224 | bytes 7340032 | tf_op jit(solution)/shard_map/dot_general | solution.py:130
  (45 shorter events, 9.6 us)
Async XLA Ops:
  7.2 36.6 %all-gather.2.cloned.1.call-start = ((), (), s32[]{:S(2)}) async-start(), calls=%async_computation.1 | async-start | bytes 1310720 | tf_op jit(solution)/shard_map/all_gather | solution.py:115
  9.0 156.9 %reduce-scatter.2.cloned.1.call-start = ((), (), s32[]{:S(2)}) async-start(), calls=%async_computation.2 | async-start | bytes 2621440 | tf_op jit(solution)/shard_map/reduce_scatter | solution.py:118
  9.1 10.7 %copy-start.5 = (s32[32,12]{0,1:T(8,128)S(1)}, s32[32,12]{0,1:T(8,128)}, u32[]{:S(2)}) copy-start(s32[32,12]{0,1:T(8,128)} %param.7) | copy-start | bytes 4612
  9.1 10.8 %copy-start.6 = (s32[32]{0:T(128)S(1)}, s32[32]{0:T(128)}, u32[]{:S(2)}) copy-start(s32[32]{0:T(128)} %param.8) | copy-start | bytes 388
  29.0 12.3 %copy-start.4 = (bf16[512,2048]{1,0:T(8,128)(2,1)S(1)}, bf16[512,2048]{1,0:T(8,128)(2,1)}, u32[]{:S(2)}) copy-start(bf16[512,2048]{1,0:T(8,128)(2,1)} %param.5) | copy-start | bytes 6291460
  76.3 3.2 %copy-start.1 = (f32[4,8,2,32,768]{4,3,1,0,2:T(8,128)}, f32[4,8,2,32,768]{4,3,1,0,2:T(8,128)S(1)}, u32[]{:S(2)}) copy-start(f32[4,8,2,32,768]{4,3,1,0,2:T(8,128)S(1)} %copy.18) | copy-start | bytes 18874372
  76.3 5.1 %copy-start.3 = (bf16[2048,1024]{1,0:T(8,128)(2,1)S(1)}, bf16[2048,1024]{1,0:T(8,128)(2,1)}, u32[]{:S(2)}) copy-start(bf16[2048,1024]{1,0:T(8,128)(2,1)} %reshape.59) | copy-start | bytes 12582916
  81.3 6.0 %collective-permute-start = (f32[1024,768]{1,0:T(8,128)}, f32[1024,768]{1,0:T(8,128)}, u32[]{:S(2)}, u32[]{:S(2)}) collective-permute-start(f32[1024,768]{1,0:T(8,128)} %dynamic-slice_bitcast_fusion), channel_id=1, source_target_pairs={{0,1},{1,0},{2,3},{3,2},{4,5},{5,4},{6,7},{7,6},{8,9},{9,8},{10,11... | collective-permute-start | bytes 9437192 | tf_op jit(solution)/shard_map/ppermute | solution.py:46
  90.6 1.6 copy-start.2
  93.5 66.5 %copy-start = (bf16[512,1024]{0,1:T(8,128)(2,1)S(1)}, bf16[512,1024]{0,1:T(8,128)(2,1)}, u32[]{:S(2)}) copy-start(bf16[512,1024]{0,1:T(8,128)(2,1)} %all-gather.2.cloned.1.call-done) | copy-start | bytes 3145732
  93.5 37.3 %collective-permute-start.3 = (f32[256,768]{1,0:T(8,128)}, f32[256,768]{1,0:T(8,128)S(1)}, u32[]{:S(2)}, u32[]{:S(2)}) collective-permute-start(f32[256,768]{1,0:T(8,128)} %get-tuple-element.14), channel_id=1, source_target_pairs={{0,48},{16,0},{32,16},{48,32},{1,49},{17,1},{33,17},{49,33},{2,50}... | collective-permute-start | bytes 2359304 | tf_op jit(solution)/shard_map/ppermute | solution.py:70
  96.5 34.3 %collective-permute-start.2 = (f32[256,768]{1,0:T(8,128)}, f32[256,768]{1,0:T(8,128)S(1)}, u32[]{:S(2)}, u32[]{:S(2)}) collective-permute-start(f32[256,768]{1,0:T(8,128)} %get-tuple-element.15), channel_id=1, source_target_pairs={{0,32},{16,48},{32,0},{48,16},{1,33},{17,49},{33,1},{49,17},{2,34}... | collective-permute-start | bytes 2359304 | tf_op jit(solution)/shard_map/ppermute | solution.py:70
  97.2 37.2 %collective-permute-start.1 = (f32[256,768]{1,0:T(8,128)S(1)}, f32[256,768]{1,0:T(8,128)}, u32[]{:S(2)}, u32[]{:S(2)}) collective-permute-start(f32[256,768]{1,0:T(8,128)S(1)} %get-tuple-element.13), channel_id=1, source_target_pairs={{0,16},{16,32},{32,48},{48,0},{1,17},{17,33},{33,49},{49,1},{2,18}... | collective-permute-start | bytes 2359304 | tf_op jit(solution)/shard_map/ppermute | solution.py:70
  136.0 8.9 %collective-permute-start.4 = (f32[32,768]{1,0:T(8,128)S(1)}, f32[32,768]{1,0:T(8,128)S(1)}, u32[]{:S(2)}, u32[]{:S(2)}) collective-permute-start(f32[32,768]{1,0:T(8,128)S(1)} %get-tuple-element.20), channel_id=1, source_target_pairs={{0,2},{2,4},{4,6},{6,8},{8,10},{10,12},{12,14},{14,0},{1,3},{3,5},... | collective-permute-start | bytes 294920 | tf_op jit(solution)/shard_map/ppermute | solution.py:89
  137.9 7.1 %collective-permute-start.8 = (f32[32,768]{1,0:T(8,128)S(1)}, f32[32,768]{1,0:T(8,128)S(1)}, u32[]{:S(2)}, u32[]{:S(2)}) collective-permute-start(f32[32,768]{1,0:T(8,128)S(1)} %get-tuple-element.21), channel_id=1, source_target_pairs={{0,14},{2,0},{4,2},{6,4},{8,6},{10,8},{12,10},{14,12},{1,15},{3,1}... | collective-permute-start | bytes 294920 | tf_op jit(solution)/shard_map/ppermute | solution.py:94
  144.9 5.9 %collective-permute-start.5 = (f32[32,768]{1,0:T(8,128)S(1)}, f32[32,768]{1,0:T(8,128)S(1)}, u32[]{:S(2)}, u32[]{:S(2)}) collective-permute-start(f32[32,768]{1,0:T(8,128)S(1)} %bitcast_add_fusion.7), channel_id=1, source_target_pairs={{0,2},{2,4},{4,6},{6,8},{8,10},{10,12},{12,14},{14,0},{1,3},{3,5},... | collective-permute-start | bytes 294920 | tf_op jit(solution)/shard_map/ppermute | solution.py:89
  150.8 5.9 %collective-permute-start.6 = (f32[32,768]{1,0:T(8,128)S(1)}, f32[32,768]{1,0:T(8,128)S(1)}, u32[]{:S(2)}, u32[]{:S(2)}) collective-permute-start(f32[32,768]{1,0:T(8,128)S(1)} %get-tuple-element.18), channel_id=1, source_target_pairs={{0,2},{2,4},{4,6},{6,8},{8,10},{10,12},{12,14},{14,0},{1,3},{3,5},... | collective-permute-start | bytes 294920 | tf_op jit(solution)/shard_map/ppermute | solution.py:89
  150.9 5.8 %collective-permute-start.9 = (f32[32,768]{1,0:T(8,128)S(1)}, f32[32,768]{1,0:T(8,128)S(1)}, u32[]{:S(2)}, u32[]{:S(2)}) collective-permute-start(f32[32,768]{1,0:T(8,128)S(1)} %get-tuple-element.19), channel_id=1, source_target_pairs={{0,14},{2,0},{4,2},{6,4},{8,6},{10,8},{12,10},{14,12},{1,15},{3,1}... | collective-permute-start | bytes 294920 | tf_op jit(solution)/shard_map/ppermute | solution.py:94
  156.7 11.1 %collective-permute-start.10 = (f32[32,768]{1,0:T(8,128)S(1)}, f32[32,768]{1,0:T(8,128)S(1)}, u32[]{:S(2)}, u32[]{:S(2)}) collective-permute-start(f32[32,768]{1,0:T(8,128)S(1)} %get-tuple-element.17), channel_id=1, source_target_pairs={{0,14},{2,0},{4,2},{6,4},{8,6},{10,8},{12,10},{14,12},{1,15},{3,1}... | collective-permute-start | bytes 294920 | tf_op jit(solution)/shard_map/ppermute | solution.py:94
  160.1 7.8 %collective-permute-start.7 = (f32[32,768]{1,0:T(8,128)S(1)}, f32[32,768]{1,0:T(8,128)S(1)}, u32[]{:S(2)}, u32[]{:S(2)}) collective-permute-start(f32[32,768]{1,0:T(8,128)S(1)} %get-tuple-element.16), channel_id=1, source_target_pairs={{0,2},{2,4},{4,6},{6,8},{8,10},{10,12},{12,14},{14,0},{1,3},{3,5},... | collective-permute-start | bytes 294920 | tf_op jit(solution)/shard_map/ppermute | solution.py:89
Sparse Core Ops, SparseCore 0:
  10.3 30.2 all-gather.1
  85.2 34.1 reduce-scatter.1

commit v8 on v7

--- a/solution.py
+++ b/solution.py
@@ -31,28 +31,11 @@
     return jnp.where(live, grad / replicas, 0.0)
 
 
-def ring_scatter(value, axis):
-    n = lax.axis_size(axis)
-    if n == 1:
-        return value
+def ring_scatter(value, axis, dim):
     idx = lax.axis_index(axis)
-    rows = value.shape[0] // n
-    chunks = value.reshape(n, rows, value.shape[1])
-
-    def take(j):
-        return lax.dynamic_index_in_dim(chunks, j % n, 0, keepdims=False)
-
-    if n == 2:
-        return take(idx) + lax.ppermute(take(idx + 1), axis, [(0, 1), (1, 0)])
-    half = value.shape[1] // 2
-    fwd = [(i, (i + 1) % n) for i in range(n)]
-    bwd = [(i, (i - 1) % n) for i in range(n)]
-    a = take(idx - 1)[:, :half]
-    b = take(idx + 1)[:, half:]
-    for s in range(n - 1):
-        a = lax.ppermute(a, axis, fwd) + take(idx - s - 2)[:, :half]
-        b = lax.ppermute(b, axis, bwd) + take(idx + s + 2)[:, half:]
-    return jnp.concatenate([a, b], axis=1)
+    mine = lax.dynamic_index_in_dim(value, idx, dim, keepdims=False)
+    other = lax.dynamic_index_in_dim(value, 1 - idx, dim, keepdims=False)
+    return mine + lax.ppermute(other, axis, [(0, 1), (1, 0)])
 
 
 def direct_scatter(value, axis):
@@ -71,14 +54,12 @@
     return total
 
 
-def meeting_scatter(value, axis):
+def meeting_scatter(value, axis, dim):
     n = lax.axis_size(axis)
     idx = lax.axis_index(axis)
-    rows = value.shape[0] // n
-    chunks = value.reshape(n, rows, value.shape[1])
 
     def take(j):
-        return lax.dynamic_index_in_dim(chunks, j % n, 0, keepdims=False)
+        return lax.dynamic_index_in_dim(value, j % n, dim, keepdims=False)
 
     ahead = n // 2
     behind = n - 1 - ahead
@@ -119,14 +100,10 @@
     activation = preact_own.astype(jnp.bfloat16)
     picked = slot_grad(tokens, cotangent_all, column_blocks, counts, block, replicas)
     owned = features // replicas
-    staged = (
-        picked.reshape(n_y, n_z, n_core, owned, slots * block)
-        .transpose(2, 0, 1, 3, 4)
-        .reshape(features, slots * block)
-    )
-    staged = ring_scatter(staged, "core")
-    staged = direct_scatter(staged, "y")
-    weight_grad = meeting_scatter(staged, "z")
+    staged = picked.reshape(n_y * n_z, n_core, owned, slots * block)
+    staged = ring_scatter(staged, "core", 1)
+    staged = meeting_scatter(staged.reshape(n_y, n_z, owned, slots * block), "z", 1)
+    weight_grad = direct_scatter(staged.reshape(n_y * owned, slots * block), "y")
     input_grad = lax.dot_general(
         cotangent_all, weight, (((1,), (1,)), ((), ())), preferred_element_type=jnp.float32
     ).astype(jnp.bfloat16)

time: 176 us -> 165 us (0.938)
  waiting for transfers between devices: 49.5 us -> 40.5 us
  local copies, waits for them, and re-layouts: 53.9 us -> 48.2 us
  other arithmetic: 6.65 us -> 9.7 us
    ppermute x3, waiting for transfers between devices: 36.2 us -> 0.01 us  [direct_scatter(): total = total + lax.ppermute(take(idx + shift), axis, perm)]
    ppermute x4, waiting for transfers between devices: 11.1 us -> 32.2 us  [meeting_scatter(): a = lax.ppermute(a, axis, fwd) + take(idx + ahead - s)]
    ppermute x3, waiting for transfers between devices: 0.01 us -> 6.11 us  [meeting_scatter(): b = lax.ppermute(b, axis, bwd)]
    squeeze x0 -> x2, local copies, waits for them, and re-layouts: none -> 4.14 us  [the longest x1 4.08 us: ring_scatter(): other = lax.dynamic_index_in_dim(value, 1 - idx, dim, keepdims=False)]
    reshape x1 -> x0, local copies, waits for them, and re-layouts: 3.51 us -> none  [per_device(): picked.reshape(n_y, n_z, n_core, owned, slots * block)]
    add x3, other arithmetic: 0.06 us -> 3.45 us  [meeting_scatter(): a = lax.ppermute(a, axis, fwd) + take(idx + ahead - s)]
    unnamed x18 -> x16, local copies, waits for them, and re-layouts: 10.1 us -> 6.88 us
    squeeze x3 -> x1, local copies, waits for them, and re-layouts: 3.2 us -> 0.03 us  [take(): return lax.dynamic_index_in_dim(chunks, j % n, 0, keepdims=False)]
  transfers between devices with their start and end apart: 13 -> 13, of which waited for: 6 -> 6; matrix products, arithmetic and copies ran while one was open for 30% -> 33% of each run, Pallas kernels for 0% -> 0%
where the time goes in v8:
time: 165 us; the launch traced here: 164 us
  local copies, waits for them, and re-layouts  48.2 us (29%)
  waiting for transfers between devices  40.5 us (25%)
  matrix products  33.5 us (20%)
  starting transfers between devices  17.4 us (11%)
  between operations  14.3 us (9%)
  other arithmetic  9.7 us (6%)
    ppermute x4, waiting for transfers between devices, meeting_scatter(): a = lax.ppermute(a, axis, fwd) + take(idx + ahead - s)  32.2 us
    dot_general x1, matrix products, slot_grad(): lax.dot_general(tok_rows, picked, (((2,), (2,)), ((0,), (0,))), preferred...  14.9 us
    gather x1, local copies, waits for them, and re-layouts, slot_grad(): picked = jnp.take(cot_rows, column_blocks, axis=0, mode='clip')  14.1 us
    reshape x1, local copies, waits for them, and re-layouts, per_device(): weight = jnp.einsum('bkc,bikj->bicj', onehot, blocks_view, preferred_elem...  12.1 us
    reshape x1, local copies, waits for them, and re-layouts, per_device(): blocks_view = block_values.reshape(row_blocks, block, slots, block)  10.6 us
    ppermute x3, starting transfers between devices, meeting_scatter(): b = lax.ppermute(b, axis, bwd)  10.5 us
    dot_general x1, matrix products, per_device(): jnp.einsum('bkc,bikj->bicj', onehot, blocks_view, preferred_element_type=...  8.94 us
    unnamed x16, local copies, waits for them, and re-layouts  6.88 us
  transfers between devices with their start and end apart: 13, of which 6 were waited for; matrix products, arithmetic and copies ran while one was open for 33% of the time, Pallas kernels for 0%

profile of v8, /device:TPU:2, one launch (start us, length us, event | category | flops | bytes accessed | tf_op | source)
XLA Modules:
  0.0 163.6 jit_solution(13165316085796653166)
XLA Ops:
  7.2 1.8 %copy.15 = bf16[128,1024]{0,1:T(8,128)(2,1)} copy(bf16[128,1024]{1,0:T(8,128)(2,1)} %param.9) | data formatting | bytes 524288 | tf_op args[4]
  9.1 10.6 %reshape.74 = bf16[32,64,12,64]{3,2,1,0:T(8,128)(2,1)} reshape(bf16[2048,768]{1,0:T(8,128)(2,1)} %param.6) | data formatting | bytes 6291456 | tf_op jit(solution)/shard_map/reshape | solution.py:90
  20.0 8.9 %convert_bitcast_fusion = bf16[32,64,16,64]{3,2,1,0:T(8,128)(2,1)} fusion(bf16[32,64,12,64]{3,2,1,0:T(8,128)(2,1)} %reshape.74, s32[32,12]{1,0:T(8,128)S(1)} %copy.12, pred[32,12]{1,0:T(8,128)(4,1)S(1)} %iota_compare_fusion.1), kind=kOutput, calls=%fused_computation.1 | convolution fusion | flops 52441088 | bytes 7341952 | tf_op jit(solution)/shard_map/bkc,bikj->bicj/dot_general | solution.py:92
  29.0 12.1 %reshape.56 = bf16[2048,1024]{1,0:T(8,128)(2,1)} reshape(bf16[32,64,16,64]{3,2,1,0:T(8,128)(2,1)} %convert_bitcast_fusion) | data formatting | bytes 8388608 | tf_op jit(solution)/shard_map/reshape | solution.py:94
  41.3 2.5 %copy.17 = bf16[512,2048]{0,1:T(8,128)(2,1)} copy(bf16[512,2048]{1,0:T(8,128)(2,1)S(1)} %copy-done.3) | data formatting | bytes 4194304 | tf_op args[0]
  43.8 14.1 %gather_fusion = bf16[384,64,512]{2,1,0:T(8,128)(2,1)} fusion(bf16[16,64,512]{2,1,0:T(8,128)(2,1)} %bitcast.63, s32[1024]{0:T(1024)S(1)} %pad_clamp_fusion), kind=kCustom, calls=%fused_computation | custom fusion | bytes 50333184 | tf_op jit(solution)/shard_map/jit(_take)/gather | solution.py:23
  57.9 14.9 %multiply_select_fusion = f32[32,768,64]{1,2,0:T(8,128)} fusion(pred[32,768]{1,0:T(8,128)(4,1)S(1)} %broadcast_in_dim.28, bf16[32,768,512]{2,1,0:T(8,128)(2,1)} %bitcast.64, bf16[32,64,512]{2,1,0:T(8,128)(2,1)} %bitcast.72), kind=kOutput, calls=%fused_computation.2 | convolution fusion | flops 1613758464 | bytes 33579008 | tf_op jit(solution)/shard_map/dot_general | solution.py:26
  72.8 4.1 %dynamic-slice_bitcast_fusion = f32[32,32,768]{2,1,0:T(8,128)} fusion(f32[32,2,32,768]{3,2,1,0:T(8,128)} %bitcast.70, s32[]{:T(128)S(6)} %select_n.106), kind=kLoop, calls=%fused_computation.4 | loop fusion | bytes 6291460 | tf_op jit(solution)/shard_map/jit(dynamic_index_in_dim)/squeeze | solution.py:37
  76.9 3.8 %convolution_bitcast_fusion = f32[512,1024]{0,1:T(8,128)} fusion(bf16[2048,1024]{1,0:T(8,128)(2,1)S(1)} %copy-done.2, bf16[512,2048]{1,0:T(8,128)(2,1)S(1)} %copy-done.3), kind=kOutput, calls=%fused_computation.6 | convolution fusion | flops 2147483648 | bytes 8388608 | tf_op jit(solution)/shard_map/dot_general | solution.py:98
  80.7 2.2 %collective-permute-done = f32[32,32,768]{2,1,0:T(8,128)} collective-permute-done((f32[32,32,768]{2,1,0:T(8,128)}, f32[32,32,768]{2,1,0:T(8,128)}, u32[]{:S(2)}, u32[]{:S(2)}) %collective-permute-start) | collective-permute-done | bytes 3145760 | tf_op jit(solution)/shard_map/ppermute | solution.py:38
  82.9 3.4 %bitcast_add_fusion = f32[32,32,768]{2,1,0:T(8,128)S(1)} fusion(f32[32,32,768]{2,1,0:T(8,128)} %collective-permute-done, f32[32,2,32,768]{3,2,1,0:T(8,128)} %bitcast.71, s32[]{:T(128)S(6)} %select_n.105), kind=kLoop, calls=%fused_computation.3 | loop fusion | flops 786432 | bytes 9437188 | tf_op jit(solution)/shard_map/add | solution.py:38
  86.3 1.6 copy-done.1
  88.0 2.0 %collective-permute-start.1 = (f32[4,32,768]{2,1,0:T(8,128)S(1)}, f32[4,32,768]{2,1,0:T(8,128)S(1)}, u32[]{:S(2)}, u32[]{:S(2)}) collective-permute-start(f32[4,32,768]{2,1,0:T(8,128)S(1)} %get-tuple-element.17), channel_id=1, source_target_pairs={{0,2},{2,4},{4,6},{6,8},{8,10},{10,12},{12,14},{14,0},{1,3},{3,5},... | collective-permute-start | bytes 1179656 | tf_op jit(solution)/shard_map/ppermute | solution.py:70
  90.0 4.2 %collective-permute-start.5 = (f32[4,32,768]{2,1,0:T(8,128)S(1)}, f32[4,32,768]{2,1,0:T(8,128)S(1)}, u32[]{:S(2)}, u32[]{:S(2)}) collective-permute-start(f32[4,32,768]{2,1,0:T(8,128)S(1)} %get-tuple-element.18), channel_id=1, source_target_pairs={{0,14},{2,0},{4,2},{6,4},{8,6},{10,8},{12,10},{14,12},{1,15},{3,1}... | collective-permute-start | bytes 1179656 | tf_op jit(solution)/shard_map/ppermute | solution.py:75
  94.2 9.3 %collective-permute-done.1 = f32[4,32,768]{2,1,0:T(8,128)S(1)} collective-permute-done((f32[4,32,768]{2,1,0:T(8,128)S(1)}, f32[4,32,768]{2,1,0:T(8,128)S(1)}, u32[]{:S(2)}, u32[]{:S(2)}) %collective-permute-start.1) | collective-permute-done | bytes 393248 | tf_op jit(solution)/shard_map/ppermute | solution.py:70
  104.7 11.7 %collective-permute-done.2 = f32[4,32,768]{2,1,0:T(8,128)S(1)} collective-permute-done((f32[4,32,768]{2,1,0:T(8,128)S(1)}, f32[4,32,768]{2,1,0:T(8,128)S(1)}, u32[]{:S(2)}, u32[]{:S(2)}) %collective-permute-start.2) | collective-permute-done | bytes 393248 | tf_op jit(solution)/shard_map/ppermute | solution.py:70
  117.7 3.2 %collective-permute-start.6 = (f32[4,32,768]{2,1,0:T(8,128)S(1)}, f32[4,32,768]{2,1,0:T(8,128)S(1)}, u32[]{:S(2)}, u32[]{:S(2)}) collective-permute-start(f32[4,32,768]{2,1,0:T(8,128)S(1)} %get-tuple-element.16), channel_id=1, source_target_pairs={{0,14},{2,0},{4,2},{6,4},{8,6},{10,8},{12,10},{14,12},{1,15},{3,1}... | collective-permute-start | bytes 1179656 | tf_op jit(solution)/shard_map/ppermute | solution.py:75
  120.9 7.7 %collective-permute-done.3 = f32[4,32,768]{2,1,0:T(8,128)S(1)} collective-permute-done((f32[4,32,768]{2,1,0:T(8,128)S(1)}, f32[4,32,768]{2,1,0:T(8,128)S(1)}, u32[]{:S(2)}, u32[]{:S(2)}) %collective-permute-start.3) | collective-permute-done | bytes 393248 | tf_op jit(solution)/shard_map/ppermute | solution.py:70
  128.6 1.2 bitcast_add_fusion.4
  129.8 3.0 %collective-permute-start.7 = (f32[4,32,768]{2,1,0:T(8,128)S(1)}, f32[4,32,768]{2,1,0:T(8,128)S(1)}, u32[]{:S(2)}, u32[]{:S(2)}) collective-permute-start(f32[4,32,768]{2,1,0:T(8,128)S(1)} %get-tuple-element.14), channel_id=1, source_target_pairs={{0,14},{2,0},{4,2},{6,4},{8,6},{10,8},{12,10},{14,12},{1,15},{3,1}... | collective-permute-start | bytes 1179656 | tf_op jit(solution)/shard_map/ppermute | solution.py:75
  132.9 6.1 %collective-permute-done.7 = f32[4,32,768]{2,1,0:T(8,128)S(1)} collective-permute-done((f32[4,32,768]{2,1,0:T(8,128)S(1)}, f32[4,32,768]{2,1,0:T(8,128)S(1)}, u32[]{:S(2)}, u32[]{:S(2)}) %collective-permute-start.7) | collective-permute-done | bytes 393248 | tf_op jit(solution)/shard_map/ppermute | solution.py:75
  139.0 3.4 %collective-permute-done.4 = f32[4,32,768]{2,1,0:T(8,128)S(1)} collective-permute-done((f32[4,32,768]{2,1,0:T(8,128)S(1)}, f32[4,32,768]{2,1,0:T(8,128)S(1)}, u32[]{:S(2)}, u32[]{:S(2)}) %collective-permute-start.4) | collective-permute-done | bytes 393248 | tf_op jit(solution)/shard_map/ppermute | solution.py:70
  143.5 3.1 %collective-permute-start.10 = (f32[32,768]{1,0:T(8,128)S(1)}, f32[32,768]{1,0:T(8,128)S(1)}, u32[]{:S(2)}, u32[]{:S(2)}) collective-permute-start(f32[32,768]{1,0:T(8,128)S(1)} %get-tuple-element.20), channel_id=1, source_target_pairs={{0,48},{16,0},{32,16},{48,32},{1,49},{17,1},{33,17},{49,33},{2,50}... | collective-permute-start | bytes 294920 | tf_op jit(solution)/shard_map/ppermute | solution.py:53
  148.2 5.9 %convolution_convert_fusion = bf16[512,2048]{1,0:T(8,128)(2,1)} fusion(bf16[512,1024]{0,1:T(8,128)(2,1)S(1)} %copy-done, bf16[2048,1024]{1,0:T(8,128)(2,1)} %reshape.56), kind=kOutput, calls=%fused_computation.5 | convolution fusion | flops 2148532224 | bytes 7340032 | tf_op jit(solution)/shard_map/dot_general | solution.py:107
  (42 shorter events, 8.4 us)
Async XLA Ops:
  7.2 36.6 %all-gather.2.cloned.1.call-start = ((), (), s32[]{:S(2)}) async-start(), calls=%async_computation.1 | async-start | bytes 1310720 | tf_op jit(solution)/shard_map/all_gather | solution.py:96
  9.0 145.1 %reduce-scatter.2.cloned.1.call-start = ((), (), s32[]{:S(2)}) async-start(), calls=%async_computation.2 | async-start | bytes 2621440 | tf_op jit(solution)/shard_map/reduce_scatter | solution.py:99
  9.1 10.7 %copy-start.4 = (s32[32,12]{0,1:T(8,128)S(1)}, s32[32,12]{0,1:T(8,128)}, u32[]{:S(2)}) copy-start(s32[32,12]{0,1:T(8,128)} %param.7) | copy-start | bytes 4612
  9.1 10.8 %copy-start.5 = (s32[32]{0:T(128)S(1)}, s32[32]{0:T(128)}, u32[]{:S(2)}) copy-start(s32[32]{0:T(128)} %param.8) | copy-start | bytes 388
  29.0 12.3 %copy-start.3 = (bf16[512,2048]{1,0:T(8,128)(2,1)S(1)}, bf16[512,2048]{1,0:T(8,128)(2,1)}, u32[]{:S(2)}) copy-start(bf16[512,2048]{1,0:T(8,128)(2,1)} %param.5) | copy-start | bytes 6291460
  72.8 4.1 %copy-start.2 = (bf16[2048,1024]{1,0:T(8,128)(2,1)S(1)}, bf16[2048,1024]{1,0:T(8,128)(2,1)}, u32[]{:S(2)}) copy-start(bf16[2048,1024]{1,0:T(8,128)(2,1)} %reshape.56) | copy-start | bytes 12582916
  76.9 6.0 %collective-permute-start = (f32[32,32,768]{2,1,0:T(8,128)}, f32[32,32,768]{2,1,0:T(8,128)}, u32[]{:S(2)}, u32[]{:S(2)}) collective-permute-start(f32[32,32,768]{2,1,0:T(8,128)} %dynamic-slice_bitcast_fusion), channel_id=1, source_target_pairs={{0,1},{1,0},{2,3},{3,2},{4,5},{5,4},{6,7},{7,6},{8,9},{9,8},{10,11... | collective-permute-start | bytes 9437192 | tf_op jit(solution)/shard_map/ppermute | solution.py:38
  86.3 1.6 %copy-start.1 = (f32[32,32,768]{2,1,0:T(8,128)}, f32[32,32,768]{2,1,0:T(8,128)S(1)}, u32[]{:S(2)}) copy-start(f32[32,32,768]{2,1,0:T(8,128)S(1)} %bitcast_add_fusion) | copy-start | bytes 9437188
  88.0 60.2 %copy-start = (bf16[512,1024]{0,1:T(8,128)(2,1)S(1)}, bf16[512,1024]{0,1:T(8,128)(2,1)}, u32[]{:S(2)}) copy-start(bf16[512,1024]{0,1:T(8,128)(2,1)} %all-gather.2.cloned.1.call-done) | copy-start | bytes 3145732
  88.0 15.5 %collective-permute-start.1 = (f32[4,32,768]{2,1,0:T(8,128)S(1)}, f32[4,32,768]{2,1,0:T(8,128)S(1)}, u32[]{:S(2)}, u32[]{:S(2)}) collective-permute-start(f32[4,32,768]{2,1,0:T(8,128)S(1)} %get-tuple-element.17), channel_id=1, source_target_pairs={{0,2},{2,4},{4,6},{6,8},{8,10},{10,12},{12,14},{14,0},{1,3},{3,5},... | collective-permute-start | bytes 1179656 | tf_op jit(solution)/shard_map/ppermute | solution.py:70
  90.0 14.7 %collective-permute-start.5 = (f32[4,32,768]{2,1,0:T(8,128)S(1)}, f32[4,32,768]{2,1,0:T(8,128)S(1)}, u32[]{:S(2)}, u32[]{:S(2)}) collective-permute-start(f32[4,32,768]{2,1,0:T(8,128)S(1)} %get-tuple-element.18), channel_id=1, source_target_pairs={{0,14},{2,0},{4,2},{6,4},{8,6},{10,8},{12,10},{14,12},{1,15},{3,1}... | collective-permute-start | bytes 1179656 | tf_op jit(solution)/shard_map/ppermute | solution.py:75
  104.5 11.9 %collective-permute-start.2 = (f32[4,32,768]{2,1,0:T(8,128)S(1)}, f32[4,32,768]{2,1,0:T(8,128)S(1)}, u32[]{:S(2)}, u32[]{:S(2)}) collective-permute-start(f32[4,32,768]{2,1,0:T(8,128)S(1)} %bitcast_add_fusion.6), channel_id=1, source_target_pairs={{0,2},{2,4},{4,6},{6,8},{8,10},{10,12},{12,14},{14,0},{1,3},{3,5},... | collective-permute-start | bytes 1179656 | tf_op jit(solution)/shard_map/ppermute | solution.py:70
  117.6 11.0 %collective-permute-start.3 = (f32[4,32,768]{2,1,0:T(8,128)S(1)}, f32[4,32,768]{2,1,0:T(8,128)S(1)}, u32[]{:S(2)}, u32[]{:S(2)}) collective-permute-start(f32[4,32,768]{2,1,0:T(8,128)S(1)} %get-tuple-element.15), channel_id=1, source_target_pairs={{0,2},{2,4},{4,6},{6,8},{8,10},{10,12},{12,14},{14,0},{1,3},{3,5},... | collective-permute-start | bytes 1179656 | tf_op jit(solution)/shard_map/ppermute | solution.py:70
  117.7 10.9 %collective-permute-start.6 = (f32[4,32,768]{2,1,0:T(8,128)S(1)}, f32[4,32,768]{2,1,0:T(8,128)S(1)}, u32[]{:S(2)}, u32[]{:S(2)}) collective-permute-start(f32[4,32,768]{2,1,0:T(8,128)S(1)} %get-tuple-element.16), channel_id=1, source_target_pairs={{0,14},{2,0},{4,2},{6,4},{8,6},{10,8},{12,10},{14,12},{1,15},{3,1}... | collective-permute-start | bytes 1179656 | tf_op jit(solution)/shard_map/ppermute | solution.py:75
  129.8 9.1 %collective-permute-start.7 = (f32[4,32,768]{2,1,0:T(8,128)S(1)}, f32[4,32,768]{2,1,0:T(8,128)S(1)}, u32[]{:S(2)}, u32[]{:S(2)}) collective-permute-start(f32[4,32,768]{2,1,0:T(8,128)S(1)} %get-tuple-element.14), channel_id=1, source_target_pairs={{0,14},{2,0},{4,2},{6,4},{8,6},{10,8},{12,10},{14,12},{1,15},{3,1}... | collective-permute-start | bytes 1179656 | tf_op jit(solution)/shard_map/ppermute | solution.py:75
  132.9 9.5 %collective-permute-start.4 = (f32[4,32,768]{2,1,0:T(8,128)S(1)}, f32[4,32,768]{2,1,0:T(8,128)S(1)}, u32[]{:S(2)}, u32[]{:S(2)}) collective-permute-start(f32[4,32,768]{2,1,0:T(8,128)S(1)} %get-tuple-element.13), channel_id=1, source_target_pairs={{0,2},{2,4},{4,6},{6,8},{8,10},{10,12},{12,14},{14,0},{1,3},{3,5},... | collective-permute-start | bytes 1179656 | tf_op jit(solution)/shard_map/ppermute | solution.py:70
  143.5 12.5 %collective-permute-start.10 = (f32[32,768]{1,0:T(8,128)S(1)}, f32[32,768]{1,0:T(8,128)S(1)}, u32[]{:S(2)}, u32[]{:S(2)}) collective-permute-start(f32[32,768]{1,0:T(8,128)S(1)} %get-tuple-element.20), channel_id=1, source_target_pairs={{0,48},{16,0},{32,16},{48,32},{1,49},{17,1},{33,17},{49,33},{2,50}... | collective-permute-start | bytes 294920 | tf_op jit(solution)/shard_map/ppermute | solution.py:53
  146.6 9.4 %collective-permute-start.9 = (f32[32,768]{1,0:T(8,128)S(1)}, f32[32,768]{1,0:T(8,128)S(1)}, u32[]{:S(2)}, u32[]{:S(2)}) collective-permute-start(f32[32,768]{1,0:T(8,128)S(1)} %get-tuple-element.21), channel_id=1, source_target_pairs={{0,32},{16,48},{32,0},{48,16},{1,33},{17,49},{33,1},{49,17},{2,34}... | collective-permute-start | bytes 294920 | tf_op jit(solution)/shard_map/ppermute | solution.py:53
  147.2 8.8 %collective-permute-start.8 = (f32[32,768]{1,0:T(8,128)S(1)}, f32[32,768]{1,0:T(8,128)S(1)}, u32[]{:S(2)}, u32[]{:S(2)}) collective-permute-start(f32[32,768]{1,0:T(8,128)S(1)} %get-tuple-element.19), channel_id=1, source_target_pairs={{0,16},{16,32},{32,48},{48,0},{1,17},{17,33},{33,49},{49,1},{2,18}... | collective-permute-start | bytes 294920 | tf_op jit(solution)/shard_map/ppermute | solution.py:53
Sparse Core Ops, SparseCore 0:
  10.3 30.2 all-gather.1
  80.8 34.1 reduce-scatter.1
